TPU v7x, 256 devices: a whole 4x4x8 slice. The times are simulated.
256 devices in a mesh: seq: 32 (over z, y_lo, core), mp: 8 (over y_hi, x).
Axes of the slice: x: 4, y: 4 (y_hi: 2, y_lo: 2; y = y_hi * 2 + y_lo), z: 8, core: 2. Of those that a mesh axis runs over, the one named last changes fastest.
Arguments:
- tokens: bfloat16 [12288, 3072], P('seq', 'mp'), may hold values from -6 to 6
- w_qkv: bfloat16 [3072, 3, 3072], P(None, None, 'mp'), may hold values from -1 to 1
- q_gain: float32 [128], replicated, may hold values from 0 to 5
- k_gain: float32 [128], replicated, may hold values from 0 to 5
- w_out: bfloat16 [3072, 3072], P('mp'), may hold values from -0.15625 to 0.15625
- neighbours: int32 [32, 6], replicated, may hold values from 0 to 31, as said below
- counts: int32 [32], replicated, may hold values from 1 to 6
Outputs:
- mixed: bfloat16 [12288, 3072], P('seq', 'mp')
Inputs may be any that keep to these rules, and one draw needn't show every extreme that they name: `neighbours`: each row lists distinct tiles, each within 4 tiles of the row's own tile counted cyclically modulo 32.
All inputs are finite; a program needn't handle non-finite values.
Results may differ from a plain program's by a relative error of at most 0.014.
Values may be sent and summed in bfloat16 or wider, within the bound.
No kernel may reach another device: no remote copies, remote signals or barrier semaphores. Data moves between devices by JAX's collectives and lax.ppermute only.
A program may use at most 128 MiB of HBM per device.

v0:
```python
import jax
import jax.numpy as jnp
from jax import lax
from jax.experimental import pallas as pl
from jax.experimental.pallas import tpu as pltpu
from jax.sharding import PartitionSpec as P

HD = 128
TILE = 384
REACH = 4
NB = 6


def passed_along(value, axis, steps):
    count = lax.axis_size(axis)
    pairs = [(source, (source + steps) % count) for source in range(count)]
    return lax.ppermute(value, axis, pairs)


def head_norm(projected, gain_vec):
    per_head = projected.reshape(projected.shape[0], -1, HD)
    factor = lax.rsqrt(jnp.mean(per_head * per_head, axis=-1, keepdims=True) + 1e-06)
    return (per_head * factor * gain_vec).astype(jnp.bfloat16)


def attend_kernel(mask_ref, q_ref, gain_ref, *rest):
    slots = len(rest) - 4
    kv_refs = rest[:slots]
    out_ref = rest[slots]
    m_ref, l_ref, acc_ref = rest[slots + 1 :]
    factor = HD ** (-0.5)
    q_raw = q_ref[...]
    norm = lax.rsqrt(jnp.mean(q_raw * q_raw, axis=-1, keepdims=True) + 1e-06)
    q = (q_raw * norm * gain_ref[...]).astype(jnp.bfloat16)
    m_ref[...] = jnp.full(m_ref.shape, -jnp.inf, jnp.float32)
    l_ref[...] = jnp.zeros(l_ref.shape, jnp.float32)
    acc_ref[...] = jnp.zeros(acc_ref.shape, jnp.float32)

    def scores_of(i):
        return lax.dot_general(
            q, kv_refs[i][0], (((1,), (1,)), ((), ())), preferred_element_type=jnp.float32
        )

    for i in range(slots):
        @pl.when(mask_ref[i] > 0)
        def _():
            m_ref[...] = jnp.maximum(m_ref[...], scores_of(i))
    highest = jnp.max(m_ref[...], axis=-1, keepdims=True)
    for i in range(slots):
        @pl.when(mask_ref[i] > 0)
        def _():
            p = jnp.exp((scores_of(i) - highest) * factor)
            l_ref[...] = l_ref[...] + p
            acc_ref[...] = acc_ref[...] + jnp.dot(
                p.astype(jnp.bfloat16), kv_refs[i][1], preferred_element_type=jnp.float32
            )
    total = jnp.sum(l_ref[...], axis=-1, keepdims=True)
    out_ref[...] = (acc_ref[...] / total).astype(jnp.bfloat16)


def attend(slot_mask, q_raw, q_gain, kv_tiles):
    rows, columns = q_raw.shape
    heads = columns // HD
    keys = kv_tiles[0].shape[2]
    slots = len(kv_tiles)
    kv_spec = pl.BlockSpec((2, None, keys, HD), lambda h, mask: (0, h, 0, 0))
    return pl.pallas_call(
        attend_kernel,
        grid_spec=pltpu.PrefetchScalarGridSpec(
            num_scalar_prefetch=1,
            grid=(heads,),
            in_specs=[
                pl.BlockSpec((rows, HD), lambda h, mask: (0, h)),
                pl.BlockSpec((1, HD), lambda h, mask: (0, 0)),
            ]
            + [kv_spec] * slots,
            out_specs=pl.BlockSpec((rows, HD), lambda h, mask: (0, h)),
            scratch_shapes=[
                pltpu.VMEM((rows, keys), jnp.float32),
                pltpu.VMEM((rows, keys), jnp.float32),
                pltpu.VMEM((rows, HD), jnp.float32),
            ],
        ),
        out_shape=jax.ShapeDtypeStruct((rows, columns), jnp.bfloat16),
    )(slot_mask, q_raw, q_gain.reshape(1, HD), *kv_tiles)


def on_device(tokens, w_qkv, q_gain, k_gain, w_out, neighbours, counts):
    tok_rows = tokens.shape[0]
    columns = w_qkv.shape[2]
    heads_here = columns // HD
    tiles_here = tok_rows // TILE
    total_tiles = neighbours.shape[0]
    feats = tokens.shape[1]
    mp_count = lax.axis_size("mp")
    mp_here = lax.axis_index("mp")

    def rows_of(block):
        return lax.dynamic_slice_in_dim(w_qkv, block * feats, feats, 0)

    projected = jnp.einsum(
        "tf,fjc->jtc", tokens, rows_of(mp_here), preferred_element_type=jnp.float32
    )
    for step in range(1, mp_count):
        source = (mp_here - step) % mp_count
        projected = projected + jnp.einsum(
            "tf,fjc->jtc",
            passed_along(tokens, "mp", step),
            rows_of(source),
            preferred_element_type=jnp.float32,
        )
    key_part = head_norm(projected[1], k_gain).transpose(1, 0, 2)
    value_part = projected[2].astype(jnp.bfloat16).reshape(tok_rows, heads_here, HD).transpose(1, 0, 2)
    paired = jnp.stack([key_part, value_part])
    position = lax.axis_index("seq")
    seq_count = lax.axis_size("seq")
    core = position % 2
    partner = [(source, source ^ 1) for source in range(seq_count)]
    from_m4 = passed_along(paired, "seq", 4)
    from_m2 = passed_along(paired, "seq", 2)
    from_p2 = passed_along(paired, "seq", -2)
    from_p4 = passed_along(paired, "seq", -4)
    fwd_own = lax.ppermute(paired, "seq", partner)
    fwd_a = lax.ppermute(from_m2, "seq", partner)
    fwd_b = lax.ppermute(from_p2, "seq", partner)
    fwd_c = lax.ppermute(jnp.where(core == 0, from_p4, from_m4), "seq", partner)
    kv_tiles = [paired, from_m4, from_m2, from_p2, from_p4, fwd_own, fwd_a, fwd_b, fwd_c]
    odd = core == 1
    slot_offsets = jnp.stack(
        [
            jnp.int32(0),
            jnp.int32(-4),
            jnp.int32(-2),
            jnp.int32(2),
            jnp.int32(4),
            jnp.where(odd, -1, 1).astype(jnp.int32),
            jnp.where(odd, -3, -1).astype(jnp.int32),
            jnp.where(odd, 1, 3).astype(jnp.int32),
            jnp.where(odd, 3, -3).astype(jnp.int32),
        ]
    )
    slot_tile = jnp.mod(position + slot_offsets, total_tiles)
    listed = lax.dynamic_slice_in_dim(neighbours, position, 1, 0)
    used_counts = lax.dynamic_slice_in_dim(counts, position, 1, 0)
    slot_used = jnp.arange(NB, dtype=jnp.int32)[None, :] < used_counts[:, None]
    hits = (listed[:, :, None] == slot_tile[None, None, :]) & slot_used[:, :, None]
    tile_mask = jnp.any(hits, axis=1)[0].astype(jnp.int32)
    q_raw = projected[0]
    attended = attend(tile_mask, q_raw, q_gain, kv_tiles)
    out_cols = w_out.shape[1] // mp_count
    total = jnp.dot(
        attended,
        lax.dynamic_slice_in_dim(w_out, mp_here * out_cols, out_cols, 1),
        preferred_element_type=jnp.float32,
    ).astype(jnp.bfloat16).astype(jnp.float32)
    for step in range(1, mp_count):
        target = (mp_here + step) % mp_count
        term = jnp.dot(
            attended,
            lax.dynamic_slice_in_dim(w_out, target * out_cols, out_cols, 1),
            preferred_element_type=jnp.float32,
        ).astype(jnp.bfloat16)
        total = total + passed_along(term, "mp", step).astype(jnp.float32)
    return total.astype(jnp.bfloat16)


def solution(mesh):
    return jax.shard_map(
        on_device,
        mesh=mesh,
        in_specs=(P("seq", "mp"), P(None, None, "mp"), P(), P(), P("mp", None), P(), P()),
        out_specs=P("seq", "mp"),
        check_vma=False,
    )
```

profile of v0, /device:TPU:8, one launch (start us, length us, event | category | flops | bytes accessed | tf_op | source)
XLA Modules:
  0.0 135.6 jit_solution(13448043719217567680)
XLA Ops:
  0.0 4.8 %collective-permute-start.5 = (bf16[384,384]{1,0:T(8,128)(2,1)}, bf16[384,384]{1,0:T(8,128)(2,1)}, u32[]{:S(2)}, u32[]{:S(2)}) collective-permute-start(bf16[384,384]{1,0:T(8,128)(2,1)} %param.7), channel_id=1, source_target_pairs={{0,6},{1,7},{2,0},{3,1},{4,2},{5,3},{6,4},{7,5},{8,14},{9,15},{10,... | collective-permute-start | bytes 884744 | tf_op jit(solution)/shard_map/ppermute | solution.py:17
  6.0 2.3 %collective-permute-start.3 = (bf16[384,384]{1,0:T(8,128)(2,1)}, bf16[384,384]{1,0:T(8,128)(2,1)S(1)}, u32[]{:S(2)}, u32[]{:S(2)}) collective-permute-start(bf16[384,384]{1,0:T(8,128)(2,1)} %param.7), channel_id=1, source_target_pairs={{0,4},{1,5},{2,6},{3,7},{4,0},{5,1},{6,2},{7,3},{8,12},{9,13},{10,... | collective-permute-start | bytes 884744 | tf_op jit(solution)/shard_map/ppermute | solution.py:17
  9.2 1.8 %collective-permute-start = (bf16[384,384]{1,0:T(8,128)(2,1)}, bf16[384,384]{1,0:T(8,128)(2,1)}, u32[]{:S(2)}, u32[]{:S(2)}) collective-permute-start(bf16[384,384]{1,0:T(8,128)(2,1)} %param.7), channel_id=1, source_target_pairs={{0,1},{1,2},{2,3},{3,4},{4,5},{5,6},{6,7},{7,0},{8,9},{9,10},{10,1... | collective-permute-start | bytes 884744 | tf_op jit(solution)/shard_map/ppermute | solution.py:17
  11.0 3.1 %fusion.25 = f32[3,384,384]{1,2,0:T(8,128)} fusion(bf16[3072,3,384]{2,0,1:T(8,128)(2,1)} %param.8, s32[]{:T(128)S(6)} %select_n.151, bf16[384,384]{1,0:T(8,128)(2,1)} %param.7), kind=kOutput, calls=%fused_computation.32 | convolution fusion | flops 339738624 | bytes 2949124 | tf_op jit(solution)/shard_map/tf,fjc->jtc/dot_general | solution.py:101
  14.2 5.5 %collective-permute-start.1 = (bf16[384,384]{1,0:T(8,128)(2,1)S(1)}, bf16[384,384]{1,0:T(8,128)(2,1)S(1)}, u32[]{:S(2)}, u32[]{:S(2)}) collective-permute-start(bf16[384,384]{1,0:T(8,128)(2,1)S(1)} %copy-done.6), channel_id=1, source_target_pairs={{0,2},{1,3},{2,4},{3,5},{4,6},{5,7},{6,0},{7,1},{8,10},{9,11},{10,... | collective-permute-start | bytes 884744 | tf_op jit(solution)/shard_map/ppermute | solution.py:17
  19.6 2.0 %fusion.13 = f32[3,384,384]{1,2,0:T(8,128)S(1)} fusion(bf16[3072,3,384]{2,0,1:T(8,128)(2,1)} %param.8, s32[]{:T(128)S(6)} %select_n.163, bf16[384,384]{1,0:T(8,128)(2,1)} %collective-permute-done.5), kind=kOutput, calls=%fused_computation.20 | convolution fusion | flops 339738624 | bytes 2949124 | tf_op jit(solution)/shard_map/tf,fjc->jtc/dot_general | solution.py:106
  21.7 7.5 %collective-permute-done = bf16[384,384]{1,0:T(8,128)(2,1)} collective-permute-done((bf16[384,384]{1,0:T(8,128)(2,1)}, bf16[384,384]{1,0:T(8,128)(2,1)}, u32[]{:S(2)}, u32[]{:S(2)}) %collective-permute-start) | collective-permute-done | bytes 294944 | tf_op jit(solution)/shard_map/ppermute | solution.py:17
  29.5 1.9 %fusion.23 = f32[3,384,384]{1,2,0:T(8,128)S(1)} fusion(bf16[3072,3,384]{2,0,1:T(8,128)(2,1)} %param.8, s32[]{:T(128)S(6)} %select_n.153, bf16[384,384]{1,0:T(8,128)(2,1)} %collective-permute-done), kind=kOutput, calls=%fused_computation.30 | convolution fusion | flops 339738624 | bytes 2949124 | tf_op jit(solution)/shard_map/tf,fjc->jtc/dot_general | solution.py:106
  31.5 2.9 %collective-permute-done.1 = bf16[384,384]{1,0:T(8,128)(2,1)S(1)} collective-permute-done((bf16[384,384]{1,0:T(8,128)(2,1)S(1)}, bf16[384,384]{1,0:T(8,128)(2,1)S(1)}, u32[]{:S(2)}, u32[]{:S(2)}) %collective-permute-start.1) | collective-permute-done | bytes 294944 | tf_op jit(solution)/shard_map/ppermute | solution.py:17
  34.3 1.8 %fusion.21 = f32[3,384,384]{1,2,0:T(8,128)S(1)} fusion(bf16[3072,3,384]{2,0,1:T(8,128)(2,1)} %param.8, s32[]{:T(128)S(6)} %select_n.155, bf16[384,384]{1,0:T(8,128)(2,1)S(1)} %collective-permute-done.1), kind=kOutput, calls=%fused_computation.28 | convolution fusion | flops 339738624 | bytes 2949124 | tf_op jit(solution)/shard_map/tf,fjc->jtc/dot_general | solution.py:106
  44.0 2.0 %collective-permute-start.8 = (bf16[2,3,384,128]{3,2,1,0:T(8,128)(2,1)S(1)}, bf16[2,3,384,128]{3,2,1,0:T(8,128)(2,1)}, u32[]{:S(2)}, u32[]{:S(2)}) collective-permute-start(bf16[2,3,384,128]{3,2,1,0:T(8,128)(2,1)S(1)} %pad_maximum_fusion.rest_0_), channel_id=1, source_target_pairs={{0,16},{8,24},{16,32},{24,40},{32,48},{40,56},{48,64},{56,72},{64,... | collective-permute-start | bytes 1769480 | tf_op jit(solution)/shard_map/ppermute | solution.py:17
  46.0 7.1 %collective-permute-start.10 = (bf16[2,3,384,128]{3,2,1,0:T(8,128)(2,1)S(1)}, bf16[2,3,384,128]{3,2,1,0:T(8,128)(2,1)S(1)}, u32[]{:S(2)}, u32[]{:S(2)}) collective-permute-start(bf16[2,3,384,128]{3,2,1,0:T(8,128)(2,1)S(1)} %pad_maximum_fusion.rest_0_), channel_id=1, source_target_pairs={{0,224},{8,232},{16,240},{24,248},{32,0},{40,8},{48,16},{56,24},{6... | collective-permute-start | bytes 1769480 | tf_op jit(solution)/shard_map/ppermute | solution.py:17
  53.1 15.4 %collective-permute-done.9.rest_3_ = bf16[2,3,384,128]{3,2,1,0:T(8,128)(2,1)} collective-permute-done((bf16[2,3,384,128]{3,2,1,0:T(8,128)(2,1)S(1)}, bf16[2,3,384,128]{3,2,1,0:T(8,128)(2,1)}, u32[]{:S(2)}, u32[]{:S(2)}) %collective-permute-start.9) | collective-permute-done | bytes 589856 | tf_op jit(solution)/shard_map/ppermute | solution.py:17
  68.4 2.5 %collective-permute-done.8.rest_2_ = bf16[2,3,384,128]{3,2,1,0:T(8,128)(2,1)} collective-permute-done((bf16[2,3,384,128]{3,2,1,0:T(8,128)(2,1)S(1)}, bf16[2,3,384,128]{3,2,1,0:T(8,128)(2,1)}, u32[]{:S(2)}, u32[]{:S(2)}) %collective-permute-start.8) | collective-permute-done | bytes 589856 | tf_op jit(solution)/shard_map/ppermute | solution.py:17
  71.0 6.8 %collective-permute-done.7.rest_1_ = bf16[2,3,384,128]{3,2,1,0:T(8,128)(2,1)} collective-permute-done((bf16[2,3,384,128]{3,2,1,0:T(8,128)(2,1)S(1)}, bf16[2,3,384,128]{3,2,1,0:T(8,128)(2,1)}, u32[]{:S(2)}, u32[]{:S(2)}) %collective-permute-start.7) | collective-permute-done | bytes 589856 | tf_op jit(solution)/shard_map/ppermute | solution.py:17
  81.5 10.6 %shard_map.73 = bf16[384,384]{1,0:T(8,128)(2,1)} custom-call(s32[9]{0:T(128)} %convert_element_type.62.mask_ref, f32[384,384]{1,0:T(8,128)} %get-tuple-element.6.q_ref, f32[1,128]{1,0:T(1,128)} %bitcast.55, bf16[2,3,384,128]{3,2,1,0:T(8,128)(2,1)} %copy-done.4, bf16[2,3,384,128]{3,2,1,0:T(8,128)(2,1)} %collective-permute-done.7.rest_1_, ...), custom_call_target="tpu_custom_call" | custom-call | tf_op jit(solution)/shard_map/pallas_call | solution.py:67
  96.9 4.1 %collective-permute-start.16 = (bf16[384,384]{1,0:T(8,128)(2,1)S(1)}, bf16[384,384]{1,0:T(8,128)(2,1)S(1)}, u32[]{:S(2)}, u32[]{:S(2)}) collective-permute-start(bf16[384,384]{1,0:T(8,128)(2,1)S(1)} %convolution_convert_fusion.5), channel_id=1, source_target_pairs={{0,2},{1,3},{2,4},{3,5},{4,6},{5,7},{6,0},{7,1},{8,10},{9,11},{10,... | collective-permute-start | bytes 884744 | tf_op jit(solution)/shard_map/ppermute | solution.py:17
  101.3 3.2 %collective-permute-start.17 = (bf16[384,384]{1,0:T(8,128)(2,1)S(1)}, bf16[384,384]{1,0:T(8,128)(2,1)S(1)}, u32[]{:S(2)}, u32[]{:S(2)}) collective-permute-start(bf16[384,384]{1,0:T(8,128)(2,1)S(1)} %convolution_convert_fusion.4), channel_id=1, source_target_pairs={{0,3},{1,4},{2,5},{3,6},{4,7},{5,0},{6,1},{7,2},{8,11},{9,12},{10,... | collective-permute-start | bytes 884744 | tf_op jit(solution)/shard_map/ppermute | solution.py:17
  104.5 2.7 %collective-permute-start.18 = (bf16[384,384]{1,0:T(8,128)(2,1)S(1)}, bf16[384,384]{1,0:T(8,128)(2,1)S(1)}, u32[]{:S(2)}, u32[]{:S(2)}) collective-permute-start(bf16[384,384]{1,0:T(8,128)(2,1)S(1)} %convolution_convert_fusion.3), channel_id=1, source_target_pairs={{0,4},{1,5},{2,6},{3,7},{4,0},{5,1},{6,2},{7,3},{8,12},{9,13},{10,... | collective-permute-start | bytes 884744 | tf_op jit(solution)/shard_map/ppermute | solution.py:17
  107.6 12.8 %collective-permute-done.15 = bf16[384,384]{1,0:T(8,128)(2,1)S(1)} collective-permute-done((bf16[384,384]{1,0:T(8,128)(2,1)S(1)}, bf16[384,384]{1,0:T(8,128)(2,1)S(1)}, u32[]{:S(2)}, u32[]{:S(2)}) %collective-permute-start.15) | collective-permute-done | bytes 294944 | tf_op jit(solution)/shard_map/ppermute | solution.py:17
  120.4 3.0 %collective-permute-done.17 = bf16[384,384]{1,0:T(8,128)(2,1)S(1)} collective-permute-done((bf16[384,384]{1,0:T(8,128)(2,1)S(1)}, bf16[384,384]{1,0:T(8,128)(2,1)S(1)}, u32[]{:S(2)}, u32[]{:S(2)}) %collective-permute-start.17) | collective-permute-done | bytes 294944 | tf_op jit(solution)/shard_map/ppermute | solution.py:17
  123.4 5.6 %collective-permute-done.18 = bf16[384,384]{1,0:T(8,128)(2,1)S(1)} collective-permute-done((bf16[384,384]{1,0:T(8,128)(2,1)S(1)}, bf16[384,384]{1,0:T(8,128)(2,1)S(1)}, u32[]{:S(2)}, u32[]{:S(2)}) %collective-permute-start.18) | collective-permute-done | bytes 294944 | tf_op jit(solution)/shard_map/ppermute | solution.py:17
  128.9 1.4 %collective-permute-done.19 = bf16[384,384]{1,0:T(8,128)(2,1)S(1)} collective-permute-done((bf16[384,384]{1,0:T(8,128)(2,1)S(1)}, bf16[384,384]{1,0:T(8,128)(2,1)S(1)}, u32[]{:S(2)}, u32[]{:S(2)}) %collective-permute-start.19) | collective-permute-done | bytes 294944 | tf_op jit(solution)/shard_map/ppermute | solution.py:17
  130.3 4.0 %collective-permute-done.21 = bf16[384,384]{1,0:T(8,128)(2,1)S(1)} collective-permute-done((bf16[384,384]{1,0:T(8,128)(2,1)S(1)}, bf16[384,384]{1,0:T(8,128)(2,1)S(1)}, u32[]{:S(2)}, u32[]{:S(2)}) %collective-permute-start.21) | collective-permute-done | bytes 294944 | tf_op jit(solution)/shard_map/ppermute | solution.py:17
  (73 shorter events, 20.7 us)
Async XLA Ops:
  0.0 92.1 %copy-start = (bf16[384,3072]{1,0:T(8,128)(2,1)S(1)}, bf16[384,3072]{1,0:T(8,128)(2,1)}, u32[]{:S(2)}) copy-start(bf16[384,3072]{1,0:T(8,128)(2,1)} %param.11) | copy-start | bytes 7077892
  0.0 14.1 %collective-permute-start.5 = (bf16[384,384]{1,0:T(8,128)(2,1)}, bf16[384,384]{1,0:T(8,128)(2,1)}, u32[]{:S(2)}, u32[]{:S(2)}) collective-permute-start(bf16[384,384]{1,0:T(8,128)(2,1)} %param.7), channel_id=1, source_target_pairs={{0,6},{1,7},{2,0},{3,1},{4,2},{5,3},{6,4},{7,5},{8,14},{9,15},{10,... | collective-permute-start | bytes 884744 | tf_op jit(solution)/shard_map/ppermute | solution.py:17
  4.8 32.7 %collective-permute-start.4 = (bf16[384,384]{1,0:T(8,128)(2,1)}, bf16[384,384]{1,0:T(8,128)(2,1)S(1)}, u32[]{:S(2)}, u32[]{:S(2)}) collective-permute-start(bf16[384,384]{1,0:T(8,128)(2,1)} %param.7), channel_id=1, source_target_pairs={{0,5},{1,6},{2,7},{3,0},{4,1},{5,2},{6,3},{7,4},{8,13},{9,14},{10,... | collective-permute-start | bytes 884744 | tf_op jit(solution)/shard_map/ppermute | solution.py:17
  6.0 30.8 %collective-permute-start.3 = (bf16[384,384]{1,0:T(8,128)(2,1)}, bf16[384,384]{1,0:T(8,128)(2,1)S(1)}, u32[]{:S(2)}, u32[]{:S(2)}) collective-permute-start(bf16[384,384]{1,0:T(8,128)(2,1)} %param.7), channel_id=1, source_target_pairs={{0,4},{1,5},{2,6},{3,7},{4,0},{5,1},{6,2},{7,3},{8,12},{9,13},{10,... | collective-permute-start | bytes 884744 | tf_op jit(solution)/shard_map/ppermute | solution.py:17
  8.3 27.8 %collective-permute-start.2 = (bf16[384,384]{1,0:T(8,128)(2,1)}, bf16[384,384]{1,0:T(8,128)(2,1)S(1)}, u32[]{:S(2)}, u32[]{:S(2)}) collective-permute-start(bf16[384,384]{1,0:T(8,128)(2,1)} %param.7), channel_id=1, source_target_pairs={{0,3},{1,4},{2,5},{3,6},{4,7},{5,0},{6,1},{7,2},{8,11},{9,12},{10,... | collective-permute-start | bytes 884744 | tf_op jit(solution)/shard_map/ppermute | solution.py:17
  9.2 20.0 %collective-permute-start = (bf16[384,384]{1,0:T(8,128)(2,1)}, bf16[384,384]{1,0:T(8,128)(2,1)}, u32[]{:S(2)}, u32[]{:S(2)}) collective-permute-start(bf16[384,384]{1,0:T(8,128)(2,1)} %param.7), channel_id=1, source_target_pairs={{0,1},{1,2},{2,3},{3,4},{4,5},{5,6},{6,7},{7,0},{8,9},{9,10},{10,1... | collective-permute-start | bytes 884744 | tf_op jit(solution)/shard_map/ppermute | solution.py:17
  14.2 20.2 %collective-permute-start.1 = (bf16[384,384]{1,0:T(8,128)(2,1)S(1)}, bf16[384,384]{1,0:T(8,128)(2,1)S(1)}, u32[]{:S(2)}, u32[]{:S(2)}) collective-permute-start(bf16[384,384]{1,0:T(8,128)(2,1)S(1)} %copy-done.6), channel_id=1, source_target_pairs={{0,2},{1,3},{2,4},{3,5},{4,6},{5,7},{6,0},{7,1},{8,10},{9,11},{10,... | collective-permute-start | bytes 884744 | tf_op jit(solution)/shard_map/ppermute | solution.py:17
  29.2 9.0 %collective-permute-start.6 = (bf16[384,384]{1,0:T(8,128)(2,1)S(1)}, bf16[384,384]{1,0:T(8,128)(2,1)S(1)}, u32[]{:S(2)}, u32[]{:S(2)}) collective-permute-start(bf16[384,384]{1,0:T(8,128)(2,1)S(1)} %copy-done.6), channel_id=1, source_target_pairs={{0,7},{1,0},{2,1},{3,2},{4,3},{5,4},{6,5},{7,6},{8,15},{9,8},{10,9... | collective-permute-start | bytes 884744 | tf_op jit(solution)/shard_map/ppermute | solution.py:17
  43.0 38.5 %copy-start.4 = (bf16[2,3,384,128]{3,2,1,0:T(8,128)(2,1)}, bf16[2,3,384,128]{3,2,1,0:T(8,128)(2,1)S(1)}, u32[]{:S(2)}) copy-start(bf16[2,3,384,128]{3,2,1,0:T(8,128)(2,1)S(1)} %pad_maximum_fusion.rest_0_) | copy-start | bytes 1769476
  43.0 25.4 %collective-permute-start.9 = (bf16[2,3,384,128]{3,2,1,0:T(8,128)(2,1)S(1)}, bf16[2,3,384,128]{3,2,1,0:T(8,128)(2,1)}, u32[]{:S(2)}, u32[]{:S(2)}) collective-permute-start(bf16[2,3,384,128]{3,2,1,0:T(8,128)(2,1)S(1)} %pad_maximum_fusion.rest_0_), channel_id=1, source_target_pairs={{0,240},{8,248},{16,0},{24,8},{32,16},{40,24},{48,32},{56,40},{64,... | collective-permute-start | bytes 1769480 | tf_op jit(solution)/shard_map/ppermute | solution.py:17
  44.0 27.0 %collective-permute-start.8 = (bf16[2,3,384,128]{3,2,1,0:T(8,128)(2,1)S(1)}, bf16[2,3,384,128]{3,2,1,0:T(8,128)(2,1)}, u32[]{:S(2)}, u32[]{:S(2)}) collective-permute-start(bf16[2,3,384,128]{3,2,1,0:T(8,128)(2,1)S(1)} %pad_maximum_fusion.rest_0_), channel_id=1, source_target_pairs={{0,16},{8,24},{16,32},{24,40},{32,48},{40,56},{48,64},{56,72},{64,... | collective-permute-start | bytes 1769480 | tf_op jit(solution)/shard_map/ppermute | solution.py:17
  46.0 25.0 %collective-permute-start.10 = (bf16[2,3,384,128]{3,2,1,0:T(8,128)(2,1)S(1)}, bf16[2,3,384,128]{3,2,1,0:T(8,128)(2,1)S(1)}, u32[]{:S(2)}, u32[]{:S(2)}) collective-permute-start(bf16[2,3,384,128]{3,2,1,0:T(8,128)(2,1)S(1)} %pad_maximum_fusion.rest_0_), channel_id=1, source_target_pairs={{0,224},{8,232},{16,240},{24,248},{32,0},{40,8},{48,16},{56,24},{6... | collective-permute-start | bytes 1769480 | tf_op jit(solution)/shard_map/ppermute | solution.py:17
  53.1 24.7 %collective-permute-start.7 = (bf16[2,3,384,128]{3,2,1,0:T(8,128)(2,1)S(1)}, bf16[2,3,384,128]{3,2,1,0:T(8,128)(2,1)}, u32[]{:S(2)}, u32[]{:S(2)}) collective-permute-start(bf16[2,3,384,128]{3,2,1,0:T(8,128)(2,1)S(1)} %pad_maximum_fusion.rest_0_), channel_id=1, source_target_pairs={{0,32},{8,40},{16,48},{24,56},{32,64},{40,72},{48,80},{56,88},{64,... | collective-permute-start | bytes 1769480 | tf_op jit(solution)/shard_map/ppermute | solution.py:17
  53.1 28.4 %collective-permute-start.11 = (bf16[2,3,384,128]{3,2,1,0:T(8,128)(2,1)S(1)}, bf16[2,3,384,128]{3,2,1,0:T(8,128)(2,1)}, u32[]{:S(2)}, u32[]{:S(2)}) collective-permute-start(bf16[2,3,384,128]{3,2,1,0:T(8,128)(2,1)S(1)} %pad_maximum_fusion.rest_0_), channel_id=1, source_target_pairs={{0,8},{8,0},{16,24},{24,16},{32,40},{40,32},{48,56},{56,48},{64,72... | collective-permute-start | bytes 1769480 | tf_op jit(solution)/shard_map/ppermute | solution.py:123
  68.4 13.1 %collective-permute-start.13 = (bf16[2,3,384,128]{3,2,1,0:T(8,128)(2,1)}, bf16[2,3,384,128]{3,2,1,0:T(8,128)(2,1)}, u32[]{:S(2)}, u32[]{:S(2)}) collective-permute-start(bf16[2,3,384,128]{3,2,1,0:T(8,128)(2,1)} %collective-permute-done.9.rest_3_), channel_id=1, source_target_pairs={{0,8},{8,0},{16,24},{24,16},{32,40},{40,32},{48,56},{56,48},{64,72... | collective-permute-start | bytes 1769480 | tf_op jit(solution)/shard_map/ppermute | solution.py:125
  71.0 10.5 %collective-permute-start.12 = (bf16[2,3,384,128]{3,2,1,0:T(8,128)(2,1)}, bf16[2,3,384,128]{3,2,1,0:T(8,128)(2,1)}, u32[]{:S(2)}, u32[]{:S(2)}) collective-permute-start(bf16[2,3,384,128]{3,2,1,0:T(8,128)(2,1)} %collective-permute-done.8.rest_2_), channel_id=1, source_target_pairs={{0,8},{8,0},{16,24},{24,16},{32,40},{40,32},{48,56},{56,48},{64,72... | collective-permute-start | bytes 1769480 | tf_op jit(solution)/shard_map/ppermute | solution.py:124
  78.7 2.8 %collective-permute-start.14 = (bf16[2,3,384,128]{3,2,1,0:T(8,128)(2,1)}, bf16[2,3,384,128]{3,2,1,0:T(8,128)(2,1)}, u32[]{:S(2)}, u32[]{:S(2)}) collective-permute-start(bf16[2,3,384,128]{3,2,1,0:T(8,128)(2,1)} %broadcast_select_fusion), channel_id=1, source_target_pairs={{0,8},{8,0},{16,24},{24,16},{32,40},{40,32},{48,56},{56,48},{64,72... | collective-permute-start | bytes 1769480 | tf_op jit(solution)/shard_map/ppermute | solution.py:126
  96.8 23.6 %collective-permute-start.15 = (bf16[384,384]{1,0:T(8,128)(2,1)S(1)}, bf16[384,384]{1,0:T(8,128)(2,1)S(1)}, u32[]{:S(2)}, u32[]{:S(2)}) collective-permute-start(bf16[384,384]{1,0:T(8,128)(2,1)S(1)} %convolution_convert_fusion.6), channel_id=1, source_target_pairs={{0,1},{1,2},{2,3},{3,4},{4,5},{5,6},{6,7},{7,0},{8,9},{9,10},{10,1... | collective-permute-start | bytes 884744 | tf_op jit(solution)/shard_map/ppermute | solution.py:17
  96.9 23.5 %collective-permute-start.16 = (bf16[384,384]{1,0:T(8,128)(2,1)S(1)}, bf16[384,384]{1,0:T(8,128)(2,1)S(1)}, u32[]{:S(2)}, u32[]{:S(2)}) collective-permute-start(bf16[384,384]{1,0:T(8,128)(2,1)S(1)} %convolution_convert_fusion.5), channel_id=1, source_target_pairs={{0,2},{1,3},{2,4},{3,5},{4,6},{5,7},{6,0},{7,1},{8,10},{9,11},{10,... | collective-permute-start | bytes 884744 | tf_op jit(solution)/shard_map/ppermute | solution.py:17
  101.3 22.0 %collective-permute-start.17 = (bf16[384,384]{1,0:T(8,128)(2,1)S(1)}, bf16[384,384]{1,0:T(8,128)(2,1)S(1)}, u32[]{:S(2)}, u32[]{:S(2)}) collective-permute-start(bf16[384,384]{1,0:T(8,128)(2,1)S(1)} %convolution_convert_fusion.4), channel_id=1, source_target_pairs={{0,3},{1,4},{2,5},{3,6},{4,7},{5,0},{6,1},{7,2},{8,11},{9,12},{10,... | collective-permute-start | bytes 884744 | tf_op jit(solution)/shard_map/ppermute | solution.py:17
  104.5 24.4 %collective-permute-start.18 = (bf16[384,384]{1,0:T(8,128)(2,1)S(1)}, bf16[384,384]{1,0:T(8,128)(2,1)S(1)}, u32[]{:S(2)}, u32[]{:S(2)}) collective-permute-start(bf16[384,384]{1,0:T(8,128)(2,1)S(1)} %convolution_convert_fusion.3), channel_id=1, source_target_pairs={{0,4},{1,5},{2,6},{3,7},{4,0},{5,1},{6,2},{7,3},{8,12},{9,13},{10,... | collective-permute-start | bytes 884744 | tf_op jit(solution)/shard_map/ppermute | solution.py:17
  107.5 22.9 %collective-permute-start.19 = (bf16[384,384]{1,0:T(8,128)(2,1)S(1)}, bf16[384,384]{1,0:T(8,128)(2,1)S(1)}, u32[]{:S(2)}, u32[]{:S(2)}) collective-permute-start(bf16[384,384]{1,0:T(8,128)(2,1)S(1)} %convolution_convert_fusion.2), channel_id=1, source_target_pairs={{0,5},{1,6},{2,7},{3,0},{4,1},{5,2},{6,3},{7,4},{8,13},{9,14},{10,... | collective-permute-start | bytes 884744 | tf_op jit(solution)/shard_map/ppermute | solution.py:17
  120.4 10.0 %collective-permute-start.20 = (bf16[384,384]{1,0:T(8,128)(2,1)S(1)}, bf16[384,384]{1,0:T(8,128)(2,1)S(1)}, u32[]{:S(2)}, u32[]{:S(2)}) collective-permute-start(bf16[384,384]{1,0:T(8,128)(2,1)S(1)} %convolution_convert_fusion.1), channel_id=1, source_target_pairs={{0,6},{1,7},{2,0},{3,1},{4,2},{5,3},{6,4},{7,5},{8,14},{9,15},{10,... | collective-permute-start | bytes 884744 | tf_op jit(solution)/shard_map/ppermute | solution.py:17
  120.4 14.0 %collective-permute-start.21 = (bf16[384,384]{1,0:T(8,128)(2,1)S(1)}, bf16[384,384]{1,0:T(8,128)(2,1)S(1)}, u32[]{:S(2)}, u32[]{:S(2)}) collective-permute-start(bf16[384,384]{1,0:T(8,128)(2,1)S(1)} %convolution_convert_fusion), channel_id=1, source_target_pairs={{0,7},{1,0},{2,1},{3,2},{4,3},{5,4},{6,5},{7,6},{8,15},{9,8},{10,9... | collective-permute-start | bytes 884744 | tf_op jit(solution)/shard_map/ppermute | solution.py:17
  (7 other events, 86.1 us)
where the time goes:
time: 136 us
  waiting for transfers between devices  61.9 us (46%)
  starting transfers between devices  37 us (27%)
  matrix products  18.1 us (13%)
  Pallas kernels  10.6 us (8%)
  local copies, waits for them, and re-layouts  5.19 us (4%)
  other arithmetic  2.48 us (2%)
    ppermute x18, waiting for transfers between devices, passed_along(): return lax.ppermute(value, axis, pairs)  61.9 us
    ppermute x18, starting transfers between devices, passed_along(): return lax.ppermute(value, axis, pairs)  36.9 us
    pallas_call x1, Pallas kernels, attend(): pl.pallas_call(attend_kernel, grid_spec=pltpu.PrefetchScalarGridSpec(num_...  10.6 us
    dot_general x7, matrix products, on_device(): jnp.einsum('tf,fjc->jtc', passed_along(tokens, 'mp', step), rows_of(sourc...  8.48 us
    dot_general x7, matrix products, on_device(): jnp.dot(attended, lax.dynamic_slice_in_dim(w_out, target * out_cols, out_...  5.28 us
    dot_general x1, matrix products, on_device(): jnp.einsum('tf,fjc->jtc', tokens, rows_of(mp_here), preferred_element_typ...  3.13 us
  transfers between devices with their start and end apart: 22, of which 10 were waited for; matrix products, arithmetic and copies ran while one was open for 11% of the time, Pallas kernels for 0%

commit v1 on v0

--- a/solution.py
+++ b/solution.py
@@ -98,9 +98,36 @@
     def rows_of(block):
         return lax.dynamic_slice_in_dim(w_qkv, block * feats, feats, 0)
 
+    position = lax.axis_index("seq")
+    seq_count = lax.axis_size("seq")
+    core = position % 2
+    odd = core == 1
+    slot_offsets = jnp.stack(
+        [
+            jnp.int32(0),
+            jnp.int32(-4),
+            jnp.int32(-2),
+            jnp.int32(2),
+            jnp.int32(4),
+            jnp.where(odd, -1, 1).astype(jnp.int32),
+            jnp.where(odd, -3, -1).astype(jnp.int32),
+            jnp.where(odd, 1, 3).astype(jnp.int32),
+            jnp.int32(-3),
+            jnp.int32(3),
+        ]
+    )
+    slot_tile = jnp.mod(position + slot_offsets, total_tiles)
+    slot_tile = slot_tile.at[8].set(jnp.where(odd, -1, slot_tile[8]))
+    slot_tile = slot_tile.at[9].set(jnp.where(odd, slot_tile[9], -1))
+    listed = lax.dynamic_slice_in_dim(neighbours, position, 1, 0)
+    used_counts = lax.dynamic_slice_in_dim(counts, position, 1, 0)
+    slot_used = jnp.arange(NB, dtype=jnp.int32)[None, :] < used_counts[:, None]
+    hits = (listed[:, :, None] == slot_tile[None, None, :]) & slot_used[:, :, None]
+    tile_mask = jnp.any(hits, axis=1)[0].astype(jnp.int32)
     projected = jnp.einsum(
         "tf,fjc->jtc", tokens, rows_of(mp_here), preferred_element_type=jnp.float32
     )
+    projected, tile_mask = lax.optimization_barrier((projected, tile_mask))
     for step in range(1, mp_count):
         source = (mp_here - step) % mp_count
         projected = projected + jnp.einsum(
@@ -112,9 +139,6 @@
     key_part = head_norm(projected[1], k_gain).transpose(1, 0, 2)
     value_part = projected[2].astype(jnp.bfloat16).reshape(tok_rows, heads_here, HD).transpose(1, 0, 2)
     paired = jnp.stack([key_part, value_part])
-    position = lax.axis_index("seq")
-    seq_count = lax.axis_size("seq")
-    core = position % 2
     partner = [(source, source ^ 1) for source in range(seq_count)]
     from_m4 = passed_along(paired, "seq", 4)
     from_m2 = passed_along(paired, "seq", 2)
@@ -123,28 +147,11 @@
     fwd_own = lax.ppermute(paired, "seq", partner)
     fwd_a = lax.ppermute(from_m2, "seq", partner)
     fwd_b = lax.ppermute(from_p2, "seq", partner)
-    fwd_c = lax.ppermute(jnp.where(core == 0, from_p4, from_m4), "seq", partner)
-    kv_tiles = [paired, from_m4, from_m2, from_p2, from_p4, fwd_own, fwd_a, fwd_b, fwd_c]
-    odd = core == 1
-    slot_offsets = jnp.stack(
-        [
-            jnp.int32(0),
-            jnp.int32(-4),
-            jnp.int32(-2),
-            jnp.int32(2),
-            jnp.int32(4),
-            jnp.where(odd, -1, 1).astype(jnp.int32),
-            jnp.where(odd, -3, -1).astype(jnp.int32),
-            jnp.where(odd, 1, 3).astype(jnp.int32),
-            jnp.where(odd, 3, -3).astype(jnp.int32),
-        ]
-    )
-    slot_tile = jnp.mod(position + slot_offsets, total_tiles)
-    listed = lax.dynamic_slice_in_dim(neighbours, position, 1, 0)
-    used_counts = lax.dynamic_slice_in_dim(counts, position, 1, 0)
-    slot_used = jnp.arange(NB, dtype=jnp.int32)[None, :] < used_counts[:, None]
-    hits = (listed[:, :, None] == slot_tile[None, None, :]) & slot_used[:, :, None]
-    tile_mask = jnp.any(hits, axis=1)[0].astype(jnp.int32)
+    even_to_odd = [(source, source ^ 1) for source in range(0, seq_count, 2)]
+    odd_to_even = [(source, source ^ 1) for source in range(1, seq_count, 2)]
+    fwd_even = lax.ppermute(from_m4, "seq", odd_to_even)
+    fwd_odd = lax.ppermute(from_p4, "seq", even_to_odd)
+    kv_tiles = [paired, from_m4, from_m2, from_p2, from_p4, fwd_own, fwd_a, fwd_b, fwd_even, fwd_odd]
     q_raw = projected[0]
     attended = attend(tile_mask, q_raw, q_gain, kv_tiles)
     out_cols = w_out.shape[1] // mp_count

time: 136 us -> 141 us (1.037)
  the two profiles are of different devices: /device:TPU:8 before, /device:TPU:47 now
where the time goes in v1:
time: 141 us
  waiting for transfers between devices  57.4 us (41%)
  starting transfers between devices  41.6 us (30%)
  matrix products  18.1 us (13%)
  Pallas kernels  14.6 us (10%)
  local copies, waits for them, and re-layouts  5.61 us (4%)
  between operations  1.76 us (1%)
  other arithmetic  1.68 us (1%)
    ppermute x18, waiting for transfers between devices, passed_along(): return lax.ppermute(value, axis, pairs)  56.3 us
    ppermute x18, starting transfers between devices, passed_along(): return lax.ppermute(value, axis, pairs)  30.6 us
    pallas_call x1, Pallas kernels, attend(): pl.pallas_call(attend_kernel, grid_spec=pltpu.PrefetchScalarGridSpec(num_...  14.6 us
    dot_general x7, matrix products, on_device(): jnp.einsum('tf,fjc->jtc', passed_along(tokens, 'mp', step), rows_of(sourc...  8.48 us
    dot_general x7, matrix products, on_device(): jnp.dot(attended, lax.dynamic_slice_in_dim(w_out, target * out_cols, out_...  5.27 us
    ppermute x1, starting transfers between devices, on_device(): fwd_even = lax.ppermute(from_m4, 'seq', odd_to_even)  4.09 us
    dot_general x1, matrix products, on_device(): jnp.einsum('tf,fjc->jtc', tokens, rows_of(mp_here), preferred_element_typ...  3.14 us
  transfers between devices with their start and end apart: 23, of which 12 were waited for; matrix products, arithmetic and copies ran while one was open for 11% of the time, Pallas kernels for 0%

profile of v1, /device:TPU:47, one launch (start us, length us, event | category | flops | bytes accessed | tf_op | source)
XLA Modules:
  0.0 140.7 jit_solution(11806943562391984310)
XLA Ops:
  0.3 2.0 %collective-permute-start.3 = (bf16[384,384]{1,0:T(8,128)(2,1)}, bf16[384,384]{1,0:T(8,128)(2,1)S(1)}, u32[]{:S(2)}, u32[]{:S(2)}) collective-permute-start(bf16[384,384]{1,0:T(8,128)(2,1)} %param.11), channel_id=1, source_target_pairs={{0,4},{1,5},{2,6},{3,7},{4,0},{5,1},{6,2},{7,3},{8,12},{9,13},{10,... | collective-permute-start | bytes 884744 | tf_op jit(solution)/shard_map/ppermute | solution.py:17
  2.3 3.7 %collective-permute-start.2 = (bf16[384,384]{1,0:T(8,128)(2,1)}, bf16[384,384]{1,0:T(8,128)(2,1)S(1)}, u32[]{:S(2)}, u32[]{:S(2)}) collective-permute-start(bf16[384,384]{1,0:T(8,128)(2,1)} %param.11), channel_id=1, source_target_pairs={{0,3},{1,4},{2,5},{3,6},{4,7},{5,0},{6,1},{7,2},{8,11},{9,12},{10,... | collective-permute-start | bytes 884744 | tf_op jit(solution)/shard_map/ppermute | solution.py:17
  6.0 2.3 %collective-permute-start.5 = (bf16[384,384]{1,0:T(8,128)(2,1)}, bf16[384,384]{1,0:T(8,128)(2,1)}, u32[]{:S(2)}, u32[]{:S(2)}) collective-permute-start(bf16[384,384]{1,0:T(8,128)(2,1)} %param.11), channel_id=1, source_target_pairs={{0,6},{1,7},{2,0},{3,1},{4,2},{5,3},{6,4},{7,5},{8,14},{9,15},{10,... | collective-permute-start | bytes 884744 | tf_op jit(solution)/shard_map/ppermute | solution.py:17
  8.3 3.1 %convolution_bitcast_fusion = f32[3,384,384]{2,1,0:T(8,128)} fusion(bf16[3072,3,384]{2,0,1:T(8,128)(2,1)} %param.12, s32[]{:T(128)S(6)} %select_n.137, bf16[384,384]{1,0:T(8,128)(2,1)} %param.11), kind=kOutput, calls=%fused_computation.7 | convolution fusion | flops 339738624 | bytes 2949124 | tf_op jit(solution)/shard_map/tf,fjc->jtc/dot_general | solution.py:127
  16.3 6.2 %collective-permute-done.5 = bf16[384,384]{1,0:T(8,128)(2,1)} collective-permute-done((bf16[384,384]{1,0:T(8,128)(2,1)}, bf16[384,384]{1,0:T(8,128)(2,1)}, u32[]{:S(2)}, u32[]{:S(2)}) %collective-permute-start.5) | collective-permute-done | bytes 294944 | tf_op jit(solution)/shard_map/ppermute | solution.py:17
  22.5 2.7 %collective-permute-start.1 = (bf16[384,384]{1,0:T(8,128)(2,1)S(1)}, bf16[384,384]{1,0:T(8,128)(2,1)S(1)}, u32[]{:S(2)}, u32[]{:S(2)}) collective-permute-start(bf16[384,384]{1,0:T(8,128)(2,1)S(1)} %copy-done.6), channel_id=1, source_target_pairs={{0,2},{1,3},{2,4},{3,5},{4,6},{5,7},{6,0},{7,1},{8,10},{9,11},{10,... | collective-permute-start | bytes 884744 | tf_op jit(solution)/shard_map/ppermute | solution.py:17
  25.3 2.0 %fusion.10 = f32[3,384,384]{1,2,0:T(8,128)S(1)} fusion(bf16[3072,3,384]{2,0,1:T(8,128)(2,1)} %param.12, s32[]{:T(128)S(6)} %select_n.157, bf16[384,384]{1,0:T(8,128)(2,1)} %collective-permute-done.5), kind=kOutput, calls=%fused_computation.26 | convolution fusion | flops 339738624 | bytes 2949124 | tf_op jit(solution)/shard_map/tf,fjc->jtc/dot_general | solution.py:133
  28.6 1.9 %fusion.20 = f32[3,384,384]{1,2,0:T(8,128)S(1)} fusion(bf16[3072,3,384]{2,0,1:T(8,128)(2,1)} %param.12, s32[]{:T(128)S(6)} %select_n.147, bf16[384,384]{1,0:T(8,128)(2,1)} %collective-permute-done), kind=kOutput, calls=%fused_computation.36 | convolution fusion | flops 339738624 | bytes 2949124 | tf_op jit(solution)/shard_map/tf,fjc->jtc/dot_general | solution.py:133
  30.5 1.8 %fusion.18 = f32[3,384,384]{1,2,0:T(8,128)S(1)} fusion(bf16[3072,3,384]{2,0,1:T(8,128)(2,1)} %param.12, s32[]{:T(128)S(6)} %select_n.149, bf16[384,384]{1,0:T(8,128)(2,1)S(1)} %collective-permute-done.1), kind=kOutput, calls=%fused_computation.34 | convolution fusion | flops 339738624 | bytes 2949124 | tf_op jit(solution)/shard_map/tf,fjc->jtc/dot_general | solution.py:133
  34.4 6.9 %collective-permute-done.6 = bf16[384,384]{1,0:T(8,128)(2,1)S(1)} collective-permute-done((bf16[384,384]{1,0:T(8,128)(2,1)S(1)}, bf16[384,384]{1,0:T(8,128)(2,1)S(1)}, u32[]{:S(2)}, u32[]{:S(2)}) %collective-permute-start.6) | collective-permute-done | bytes 294944 | tf_op jit(solution)/shard_map/ppermute | solution.py:17
  46.3 2.6 %collective-permute-start.9 = (bf16[2,3,384,128]{3,2,1,0:T(8,128)(2,1)S(1)}, bf16[2,3,384,128]{3,2,1,0:T(8,128)(2,1)}, u32[]{:S(2)}, u32[]{:S(2)}) collective-permute-start(bf16[2,3,384,128]{3,2,1,0:T(8,128)(2,1)S(1)} %pad_maximum_fusion.rest_0_), channel_id=1, source_target_pairs={{0,240},{8,248},{16,0},{24,8},{32,16},{40,24},{48,32},{56,40},{64,... | collective-permute-start | bytes 1769480 | tf_op jit(solution)/shard_map/ppermute | solution.py:17
  50.3 1.6 %collective-permute-start.7 = (bf16[2,3,384,128]{3,2,1,0:T(8,128)(2,1)S(1)}, bf16[2,3,384,128]{3,2,1,0:T(8,128)(2,1)}, u32[]{:S(2)}, u32[]{:S(2)}) collective-permute-start(bf16[2,3,384,128]{3,2,1,0:T(8,128)(2,1)S(1)} %pad_maximum_fusion.rest_0_), channel_id=1, source_target_pairs={{0,32},{8,40},{16,48},{24,56},{32,64},{40,72},{48,80},{56,88},{64,... | collective-permute-start | bytes 1769480 | tf_op jit(solution)/shard_map/ppermute | solution.py:17
  53.4 6.6 %collective-permute-done.10.rest_4_ = bf16[2,3,384,128]{3,2,1,0:T(8,128)(2,1)S(1)} collective-permute-done((bf16[2,3,384,128]{3,2,1,0:T(8,128)(2,1)S(1)}, bf16[2,3,384,128]{3,2,1,0:T(8,128)(2,1)S(1)}, u32[]{:S(2)}, u32[]{:S(2)}) %collective-permute-start.10) | collective-permute-done | bytes 589856 | tf_op jit(solution)/shard_map/ppermute | solution.py:17
  61.3 14.4 %collective-permute-done.9.rest_3_ = bf16[2,3,384,128]{3,2,1,0:T(8,128)(2,1)} collective-permute-done((bf16[2,3,384,128]{3,2,1,0:T(8,128)(2,1)S(1)}, bf16[2,3,384,128]{3,2,1,0:T(8,128)(2,1)}, u32[]{:S(2)}, u32[]{:S(2)}) %collective-permute-start.9) | collective-permute-done | bytes 589856 | tf_op jit(solution)/shard_map/ppermute | solution.py:17
  77.3 2.6 %collective-permute-start.12 = (bf16[2,3,384,128]{3,2,1,0:T(8,128)(2,1)}, bf16[2,3,384,128]{3,2,1,0:T(8,128)(2,1)}, u32[]{:S(2)}, u32[]{:S(2)}) collective-permute-start(bf16[2,3,384,128]{3,2,1,0:T(8,128)(2,1)} %collective-permute-done.8.rest_2_), channel_id=1, source_target_pairs={{0,8},{8,0},{16,24},{24,16},{32,40},{40,32},{48,56},{56,48},{64,72... | collective-permute-start | bytes 1769480 | tf_op jit(solution)/shard_map/ppermute | solution.py:148
  79.9 4.1 %collective-permute-start.14 = (bf16[2,3,384,128]{3,2,1,0:T(8,128)(2,1)}, bf16[2,3,384,128]{3,2,1,0:T(8,128)(2,1)}, u32[]{:S(2)}, u32[]{:S(2)}) collective-permute-start(bf16[2,3,384,128]{3,2,1,0:T(8,128)(2,1)} %collective-permute-done.7.rest_1_), channel_id=1, source_target_pairs={{8,0},{24,16},{40,32},{56,48},{72,64},{88,80},{104,96},{120,112},{... | collective-permute-start | bytes 1769480 | tf_op jit(solution)/shard_map/ppermute | solution.py:152
  85.1 14.6 %shard_map.73 = bf16[384,384]{1,0:T(8,128)(2,1)} custom-call(s32[10]{0:T(128)} %convert_element_type.62.mask_ref, f32[384,384]{1,0:T(8,128)} %get-tuple-element.34.q_ref, f32[1,128]{1,0:T(1,128)} %bitcast.84, bf16[2,3,384,128]{3,2,1,0:T(8,128)(2,1)} %copy-done.4, bf16[2,3,384,128]{3,2,1,0:T(8,128)(2,1)} %collective-permute-done.7.rest_1_, ...), custom_call_target="tpu_custom_call" | custom-call | tf_op jit(solution)/shard_map/pallas_call | solution.py:67
  104.5 2.2 %collective-permute-start.17 = (bf16[384,384]{1,0:T(8,128)(2,1)S(1)}, bf16[384,384]{1,0:T(8,128)(2,1)S(1)}, u32[]{:S(2)}, u32[]{:S(2)}) collective-permute-start(bf16[384,384]{1,0:T(8,128)(2,1)S(1)} %convolution_convert_fusion.5), channel_id=1, source_target_pairs={{0,2},{1,3},{2,4},{3,5},{4,6},{5,7},{6,0},{7,1},{8,10},{9,11},{10,... | collective-permute-start | bytes 884744 | tf_op jit(solution)/shard_map/ppermute | solution.py:17
  107.0 1.7 %collective-permute-start.18 = (bf16[384,384]{1,0:T(8,128)(2,1)S(1)}, bf16[384,384]{1,0:T(8,128)(2,1)S(1)}, u32[]{:S(2)}, u32[]{:S(2)}) collective-permute-start(bf16[384,384]{1,0:T(8,128)(2,1)S(1)} %convolution_convert_fusion.4), channel_id=1, source_target_pairs={{0,3},{1,4},{2,5},{3,6},{4,7},{5,0},{6,1},{7,2},{8,11},{9,12},{10,... | collective-permute-start | bytes 884744 | tf_op jit(solution)/shard_map/ppermute | solution.py:17
  114.5 5.0 %collective-permute-start.22 = (bf16[384,384]{1,0:T(8,128)(2,1)S(1)}, bf16[384,384]{1,0:T(8,128)(2,1)S(1)}, u32[]{:S(2)}, u32[]{:S(2)}) collective-permute-start(bf16[384,384]{1,0:T(8,128)(2,1)S(1)} %convolution_convert_fusion), channel_id=1, source_target_pairs={{0,7},{1,0},{2,1},{3,2},{4,3},{5,4},{6,5},{7,6},{8,15},{9,8},{10,9... | collective-permute-start | bytes 884744 | tf_op jit(solution)/shard_map/ppermute | solution.py:17
  119.5 2.0 %collective-permute-done.18 = bf16[384,384]{1,0:T(8,128)(2,1)S(1)} collective-permute-done((bf16[384,384]{1,0:T(8,128)(2,1)S(1)}, bf16[384,384]{1,0:T(8,128)(2,1)S(1)}, u32[]{:S(2)}, u32[]{:S(2)}) %collective-permute-start.18) | collective-permute-done | bytes 294944 | tf_op jit(solution)/shard_map/ppermute | solution.py:17
  121.5 5.1 %collective-permute-done.20 = bf16[384,384]{1,0:T(8,128)(2,1)S(1)} collective-permute-done((bf16[384,384]{1,0:T(8,128)(2,1)S(1)}, bf16[384,384]{1,0:T(8,128)(2,1)S(1)}, u32[]{:S(2)}, u32[]{:S(2)}) %collective-permute-start.20) | collective-permute-done | bytes 294944 | tf_op jit(solution)/shard_map/ppermute | solution.py:17
  126.6 6.9 %collective-permute-done.21 = bf16[384,384]{1,0:T(8,128)(2,1)S(1)} collective-permute-done((bf16[384,384]{1,0:T(8,128)(2,1)S(1)}, bf16[384,384]{1,0:T(8,128)(2,1)S(1)}, u32[]{:S(2)}, u32[]{:S(2)}) %collective-permute-start.21) | collective-permute-done | bytes 294944 | tf_op jit(solution)/shard_map/ppermute | solution.py:17
  133.5 6.0 %collective-permute-done.22 = bf16[384,384]{1,0:T(8,128)(2,1)S(1)} collective-permute-done((bf16[384,384]{1,0:T(8,128)(2,1)S(1)}, bf16[384,384]{1,0:T(8,128)(2,1)S(1)}, u32[]{:S(2)}, u32[]{:S(2)}) %collective-permute-start.22) | collective-permute-done | bytes 294944 | tf_op jit(solution)/shard_map/ppermute | solution.py:17
  (80 shorter events, 30.8 us)
Async XLA Ops:
  0.0 99.7 %copy-start = (bf16[384,3072]{1,0:T(8,128)(2,1)S(1)}, bf16[384,3072]{1,0:T(8,128)(2,1)}, u32[]{:S(2)}) copy-start(bf16[384,3072]{1,0:T(8,128)(2,1)} %param.15) | copy-start | bytes 7077892
  0.0 33.7 %collective-permute-start.4 = (bf16[384,384]{1,0:T(8,128)(2,1)}, bf16[384,384]{1,0:T(8,128)(2,1)S(1)}, u32[]{:S(2)}, u32[]{:S(2)}) collective-permute-start(bf16[384,384]{1,0:T(8,128)(2,1)} %param.11), channel_id=1, source_target_pairs={{0,5},{1,6},{2,7},{3,0},{4,1},{5,2},{6,3},{7,4},{8,13},{9,14},{10,... | collective-permute-start | bytes 884744 | tf_op jit(solution)/shard_map/ppermute | solution.py:17
  0.3 32.7 %collective-permute-start.3 = (bf16[384,384]{1,0:T(8,128)(2,1)}, bf16[384,384]{1,0:T(8,128)(2,1)S(1)}, u32[]{:S(2)}, u32[]{:S(2)}) collective-permute-start(bf16[384,384]{1,0:T(8,128)(2,1)} %param.11), channel_id=1, source_target_pairs={{0,4},{1,5},{2,6},{3,7},{4,0},{5,1},{6,2},{7,3},{8,12},{9,13},{10,... | collective-permute-start | bytes 884744 | tf_op jit(solution)/shard_map/ppermute | solution.py:17
  2.3 30.0 %collective-permute-start.2 = (bf16[384,384]{1,0:T(8,128)(2,1)}, bf16[384,384]{1,0:T(8,128)(2,1)S(1)}, u32[]{:S(2)}, u32[]{:S(2)}) collective-permute-start(bf16[384,384]{1,0:T(8,128)(2,1)} %param.11), channel_id=1, source_target_pairs={{0,3},{1,4},{2,5},{3,6},{4,7},{5,0},{6,1},{7,2},{8,11},{9,12},{10,... | collective-permute-start | bytes 884744 | tf_op jit(solution)/shard_map/ppermute | solution.py:17
  6.0 21.3 %collective-permute-start = (bf16[384,384]{1,0:T(8,128)(2,1)}, bf16[384,384]{1,0:T(8,128)(2,1)}, u32[]{:S(2)}, u32[]{:S(2)}) collective-permute-start(bf16[384,384]{1,0:T(8,128)(2,1)} %param.11), channel_id=1, source_target_pairs={{0,1},{1,2},{2,3},{3,4},{4,5},{5,6},{6,7},{7,0},{8,9},{9,10},{10,1... | collective-permute-start | bytes 884744 | tf_op jit(solution)/shard_map/ppermute | solution.py:17
  6.0 16.5 %collective-permute-start.5 = (bf16[384,384]{1,0:T(8,128)(2,1)}, bf16[384,384]{1,0:T(8,128)(2,1)}, u32[]{:S(2)}, u32[]{:S(2)}) collective-permute-start(bf16[384,384]{1,0:T(8,128)(2,1)} %param.11), channel_id=1, source_target_pairs={{0,6},{1,7},{2,0},{3,1},{4,2},{5,3},{6,4},{7,5},{8,14},{9,15},{10,... | collective-permute-start | bytes 884744 | tf_op jit(solution)/shard_map/ppermute | solution.py:17
  22.5 8.0 %collective-permute-start.1 = (bf16[384,384]{1,0:T(8,128)(2,1)S(1)}, bf16[384,384]{1,0:T(8,128)(2,1)S(1)}, u32[]{:S(2)}, u32[]{:S(2)}) collective-permute-start(bf16[384,384]{1,0:T(8,128)(2,1)S(1)} %copy-done.6), channel_id=1, source_target_pairs={{0,2},{1,3},{2,4},{3,5},{4,6},{5,7},{6,0},{7,1},{8,10},{9,11},{10,... | collective-permute-start | bytes 884744 | tf_op jit(solution)/shard_map/ppermute | solution.py:17
  27.3 14.0 %collective-permute-start.6 = (bf16[384,384]{1,0:T(8,128)(2,1)S(1)}, bf16[384,384]{1,0:T(8,128)(2,1)S(1)}, u32[]{:S(2)}, u32[]{:S(2)}) collective-permute-start(bf16[384,384]{1,0:T(8,128)(2,1)S(1)} %copy-done.6), channel_id=1, source_target_pairs={{0,7},{1,0},{2,1},{3,2},{4,3},{5,4},{6,5},{7,6},{8,15},{9,8},{10,9... | collective-permute-start | bytes 884744 | tf_op jit(solution)/shard_map/ppermute | solution.py:17
  46.0 14.0 %collective-permute-start.10 = (bf16[2,3,384,128]{3,2,1,0:T(8,128)(2,1)S(1)}, bf16[2,3,384,128]{3,2,1,0:T(8,128)(2,1)S(1)}, u32[]{:S(2)}, u32[]{:S(2)}) collective-permute-start(bf16[2,3,384,128]{3,2,1,0:T(8,128)(2,1)S(1)} %pad_maximum_fusion.rest_0_), channel_id=1, source_target_pairs={{0,224},{8,232},{16,240},{24,248},{32,0},{40,8},{48,16},{56,24},{6... | collective-permute-start | bytes 1769480 | tf_op jit(solution)/shard_map/ppermute | solution.py:17
  46.3 29.4 %collective-permute-start.9 = (bf16[2,3,384,128]{3,2,1,0:T(8,128)(2,1)S(1)}, bf16[2,3,384,128]{3,2,1,0:T(8,128)(2,1)}, u32[]{:S(2)}, u32[]{:S(2)}) collective-permute-start(bf16[2,3,384,128]{3,2,1,0:T(8,128)(2,1)S(1)} %pad_maximum_fusion.rest_0_), channel_id=1, source_target_pairs={{0,240},{8,248},{16,0},{24,8},{32,16},{40,24},{48,32},{56,40},{64,... | collective-permute-start | bytes 1769480 | tf_op jit(solution)/shard_map/ppermute | solution.py:17
  48.9 28.4 %collective-permute-start.8 = (bf16[2,3,384,128]{3,2,1,0:T(8,128)(2,1)S(1)}, bf16[2,3,384,128]{3,2,1,0:T(8,128)(2,1)}, u32[]{:S(2)}, u32[]{:S(2)}) collective-permute-start(bf16[2,3,384,128]{3,2,1,0:T(8,128)(2,1)S(1)} %pad_maximum_fusion.rest_0_), channel_id=1, source_target_pairs={{0,16},{8,24},{16,32},{24,40},{32,48},{40,56},{48,64},{56,72},{64,... | collective-permute-start | bytes 1769480 | tf_op jit(solution)/shard_map/ppermute | solution.py:17
  50.3 29.6 %collective-permute-start.7 = (bf16[2,3,384,128]{3,2,1,0:T(8,128)(2,1)S(1)}, bf16[2,3,384,128]{3,2,1,0:T(8,128)(2,1)}, u32[]{:S(2)}, u32[]{:S(2)}) collective-permute-start(bf16[2,3,384,128]{3,2,1,0:T(8,128)(2,1)S(1)} %pad_maximum_fusion.rest_0_), channel_id=1, source_target_pairs={{0,32},{8,40},{16,48},{24,56},{32,64},{40,72},{48,80},{56,88},{64,... | collective-permute-start | bytes 1769480 | tf_op jit(solution)/shard_map/ppermute | solution.py:17
  51.9 32.0 %collective-permute-start.11 = (bf16[2,3,384,128]{3,2,1,0:T(8,128)(2,1)S(1)}, bf16[2,3,384,128]{3,2,1,0:T(8,128)(2,1)}, u32[]{:S(2)}, u32[]{:S(2)}) collective-permute-start(bf16[2,3,384,128]{3,2,1,0:T(8,128)(2,1)S(1)} %pad_maximum_fusion.rest_0_), channel_id=1, source_target_pairs={{0,8},{8,0},{16,24},{24,16},{32,40},{40,32},{48,56},{56,48},{64,72... | collective-permute-start | bytes 1769480 | tf_op jit(solution)/shard_map/ppermute | solution.py:147
  60.0 24.0 %collective-permute-start.15 = (bf16[2,3,384,128]{3,2,1,0:T(8,128)(2,1)S(1)}, bf16[2,3,384,128]{3,2,1,0:T(8,128)(2,1)}, u32[]{:S(2)}, u32[]{:S(2)}) collective-permute-start(bf16[2,3,384,128]{3,2,1,0:T(8,128)(2,1)S(1)} %collective-permute-done.10.rest_4_), channel_id=1, source_target_pairs={{0,8},{16,24},{32,40},{48,56},{64,72},{80,88},{96,104},{112,120},{... | collective-permute-start | bytes 1769480 | tf_op jit(solution)/shard_map/ppermute | solution.py:153
  75.7 8.3 %collective-permute-start.13 = (bf16[2,3,384,128]{3,2,1,0:T(8,128)(2,1)}, bf16[2,3,384,128]{3,2,1,0:T(8,128)(2,1)}, u32[]{:S(2)}, u32[]{:S(2)}) collective-permute-start(bf16[2,3,384,128]{3,2,1,0:T(8,128)(2,1)} %collective-permute-done.9.rest_3_), channel_id=1, source_target_pairs={{0,8},{8,0},{16,24},{24,16},{32,40},{40,32},{48,56},{56,48},{64,72... | collective-permute-start | bytes 1769480 | tf_op jit(solution)/shard_map/ppermute | solution.py:149
  77.3 6.7 %collective-permute-start.12 = (bf16[2,3,384,128]{3,2,1,0:T(8,128)(2,1)}, bf16[2,3,384,128]{3,2,1,0:T(8,128)(2,1)}, u32[]{:S(2)}, u32[]{:S(2)}) collective-permute-start(bf16[2,3,384,128]{3,2,1,0:T(8,128)(2,1)} %collective-permute-done.8.rest_2_), channel_id=1, source_target_pairs={{0,8},{8,0},{16,24},{24,16},{32,40},{40,32},{48,56},{56,48},{64,72... | collective-permute-start | bytes 1769480 | tf_op jit(solution)/shard_map/ppermute | solution.py:148
  79.9 5.2 %collective-permute-start.14 = (bf16[2,3,384,128]{3,2,1,0:T(8,128)(2,1)}, bf16[2,3,384,128]{3,2,1,0:T(8,128)(2,1)}, u32[]{:S(2)}, u32[]{:S(2)}) collective-permute-start(bf16[2,3,384,128]{3,2,1,0:T(8,128)(2,1)} %collective-permute-done.7.rest_1_), channel_id=1, source_target_pairs={{8,0},{24,16},{40,32},{56,48},{72,64},{88,80},{104,96},{120,112},{... | collective-permute-start | bytes 1769480 | tf_op jit(solution)/shard_map/ppermute | solution.py:152
  104.4 8.3 %collective-permute-start.16 = (bf16[384,384]{1,0:T(8,128)(2,1)S(1)}, bf16[384,384]{1,0:T(8,128)(2,1)S(1)}, u32[]{:S(2)}, u32[]{:S(2)}) collective-permute-start(bf16[384,384]{1,0:T(8,128)(2,1)S(1)} %convolution_convert_fusion.6), channel_id=1, source_target_pairs={{0,1},{1,2},{2,3},{3,4},{4,5},{5,6},{6,7},{7,0},{8,9},{9,10},{10,1... | collective-permute-start | bytes 884744 | tf_op jit(solution)/shard_map/ppermute | solution.py:17
  104.5 10.1 %collective-permute-start.17 = (bf16[384,384]{1,0:T(8,128)(2,1)S(1)}, bf16[384,384]{1,0:T(8,128)(2,1)S(1)}, u32[]{:S(2)}, u32[]{:S(2)}) collective-permute-start(bf16[384,384]{1,0:T(8,128)(2,1)S(1)} %convolution_convert_fusion.5), channel_id=1, source_target_pairs={{0,2},{1,3},{2,4},{3,5},{4,6},{5,7},{6,0},{7,1},{8,10},{9,11},{10,... | collective-permute-start | bytes 884744 | tf_op jit(solution)/shard_map/ppermute | solution.py:17
  107.0 14.5 %collective-permute-start.18 = (bf16[384,384]{1,0:T(8,128)(2,1)S(1)}, bf16[384,384]{1,0:T(8,128)(2,1)S(1)}, u32[]{:S(2)}, u32[]{:S(2)}) collective-permute-start(bf16[384,384]{1,0:T(8,128)(2,1)S(1)} %convolution_convert_fusion.4), channel_id=1, source_target_pairs={{0,3},{1,4},{2,5},{3,6},{4,7},{5,0},{6,1},{7,2},{8,11},{9,12},{10,... | collective-permute-start | bytes 884744 | tf_op jit(solution)/shard_map/ppermute | solution.py:17
  108.7 12.8 %collective-permute-start.19 = (bf16[384,384]{1,0:T(8,128)(2,1)S(1)}, bf16[384,384]{1,0:T(8,128)(2,1)S(1)}, u32[]{:S(2)}, u32[]{:S(2)}) collective-permute-start(bf16[384,384]{1,0:T(8,128)(2,1)S(1)} %convolution_convert_fusion.3), channel_id=1, source_target_pairs={{0,4},{1,5},{2,6},{3,7},{4,0},{5,1},{6,2},{7,3},{8,12},{9,13},{10,... | collective-permute-start | bytes 884744 | tf_op jit(solution)/shard_map/ppermute | solution.py:17
  110.7 15.9 %collective-permute-start.20 = (bf16[384,384]{1,0:T(8,128)(2,1)S(1)}, bf16[384,384]{1,0:T(8,128)(2,1)S(1)}, u32[]{:S(2)}, u32[]{:S(2)}) collective-permute-start(bf16[384,384]{1,0:T(8,128)(2,1)S(1)} %convolution_convert_fusion.2), channel_id=1, source_target_pairs={{0,5},{1,6},{2,7},{3,0},{4,1},{5,2},{6,3},{7,4},{8,13},{9,14},{10,... | collective-permute-start | bytes 884744 | tf_op jit(solution)/shard_map/ppermute | solution.py:17
  112.7 20.9 %collective-permute-start.21 = (bf16[384,384]{1,0:T(8,128)(2,1)S(1)}, bf16[384,384]{1,0:T(8,128)(2,1)S(1)}, u32[]{:S(2)}, u32[]{:S(2)}) collective-permute-start(bf16[384,384]{1,0:T(8,128)(2,1)S(1)} %convolution_convert_fusion.1), channel_id=1, source_target_pairs={{0,6},{1,7},{2,0},{3,1},{4,2},{5,3},{6,4},{7,5},{8,14},{9,15},{10,... | collective-permute-start | bytes 884744 | tf_op jit(solution)/shard_map/ppermute | solution.py:17
  114.5 25.0 %collective-permute-start.22 = (bf16[384,384]{1,0:T(8,128)(2,1)S(1)}, bf16[384,384]{1,0:T(8,128)(2,1)S(1)}, u32[]{:S(2)}, u32[]{:S(2)}) collective-permute-start(bf16[384,384]{1,0:T(8,128)(2,1)S(1)} %convolution_convert_fusion), channel_id=1, source_target_pairs={{0,7},{1,0},{2,1},{3,2},{4,3},{5,4},{6,5},{7,6},{8,15},{9,8},{10,9... | collective-permute-start | bytes 884744 | tf_op jit(solution)/shard_map/ppermute | solution.py:17
  (9 other events, 136.8 us)

commit v2 on v0

--- a/solution.py
+++ b/solution.py
@@ -148,18 +148,12 @@
     q_raw = projected[0]
     attended = attend(tile_mask, q_raw, q_gain, kv_tiles)
     out_cols = w_out.shape[1] // mp_count
-    total = jnp.dot(
-        attended,
-        lax.dynamic_slice_in_dim(w_out, mp_here * out_cols, out_cols, 1),
-        preferred_element_type=jnp.float32,
-    ).astype(jnp.bfloat16).astype(jnp.float32)
+    terms = jnp.dot(attended, w_out, preferred_element_type=jnp.float32).astype(jnp.bfloat16)
+    terms = terms.reshape(tok_rows, mp_count, out_cols).transpose(1, 0, 2)
+    total = lax.dynamic_index_in_dim(terms, mp_here, 0, keepdims=False).astype(jnp.float32)
     for step in range(1, mp_count):
         target = (mp_here + step) % mp_count
-        term = jnp.dot(
-            attended,
-            lax.dynamic_slice_in_dim(w_out, target * out_cols, out_cols, 1),
-            preferred_element_type=jnp.float32,
-        ).astype(jnp.bfloat16)
+        term = lax.dynamic_index_in_dim(terms, target, 0, keepdims=False)
         total = total + passed_along(term, "mp", step).astype(jnp.float32)
     return total.astype(jnp.bfloat16)
 

time: 136 us -> 137 us (level)
  the two profiles are of different devices: /device:TPU:8 before, /device:TPU:29 now
where the time goes in v2:
time: 137 us; the launch traced here: 138 us
  waiting for transfers between devices  62.1 us (45%)
  starting transfers between devices  33.6 us (25%)
  matrix products  14 us (10%)
  Pallas kernels  12.5 us (9%)
  local copies, waits for them, and re-layouts  10.9 us (8%)
  other arithmetic  4.56 us (3%)
    ppermute x18, waiting for transfers between devices, passed_along(): return lax.ppermute(value, axis, pairs)  62.1 us
    ppermute x18, starting transfers between devices, passed_along(): return lax.ppermute(value, axis, pairs)  26.5 us
    pallas_call x1, Pallas kernels, attend(): pl.pallas_call(attend_kernel, grid_spec=pltpu.PrefetchScalarGridSpec(num_...  12.5 us
    dot_general x7, matrix products, on_device(): jnp.einsum('tf,fjc->jtc', passed_along(tokens, 'mp', step), rows_of(sourc...  8.48 us
    another operation x1, local copies, waits for them, and re-layouts  4.93 us
    dot_general x1, matrix products, on_device(): jnp.einsum('tf,fjc->jtc', tokens, rows_of(mp_here), preferred_element_typ...  3.13 us
  transfers between devices with their start and end apart: 22, of which 10 were waited for; matrix products, arithmetic and copies ran while one was open for 11% of the time, Pallas kernels for 0%

profile of v2, /device:TPU:29, one launch (start us, length us, event | category | flops | bytes accessed | tf_op | source)
XLA Modules:
  0.0 137.9 jit_solution(13069460128989064802)
XLA Ops:
  0.2 2.5 %collective-permute-start.4 = (bf16[384,384]{1,0:T(8,128)(2,1)}, bf16[384,384]{1,0:T(8,128)(2,1)S(1)}, u32[]{:S(2)}, u32[]{:S(2)}) collective-permute-start(bf16[384,384]{1,0:T(8,128)(2,1)} %param.7), channel_id=1, source_target_pairs={{0,5},{1,6},{2,7},{3,0},{4,1},{5,2},{6,3},{7,4},{8,13},{9,14},{10,... | collective-permute-start | bytes 884744 | tf_op jit(solution)/shard_map/ppermute | solution.py:17
  2.7 2.0 %collective-permute-start.3 = (bf16[384,384]{1,0:T(8,128)(2,1)}, bf16[384,384]{1,0:T(8,128)(2,1)S(1)}, u32[]{:S(2)}, u32[]{:S(2)}) collective-permute-start(bf16[384,384]{1,0:T(8,128)(2,1)} %param.7), channel_id=1, source_target_pairs={{0,4},{1,5},{2,6},{3,7},{4,0},{5,1},{6,2},{7,3},{8,12},{9,13},{10,... | collective-permute-start | bytes 884744 | tf_op jit(solution)/shard_map/ppermute | solution.py:17
  6.9 3.1 %fusion.16 = f32[3,384,384]{1,2,0:T(8,128)} fusion(bf16[3072,3,384]{2,0,1:T(8,128)(2,1)} %param.8, s32[]{:T(128)S(6)} %select_n.154, bf16[384,384]{1,0:T(8,128)(2,1)} %param.7), kind=kOutput, calls=%fused_computation.16 | convolution fusion | flops 339738624 | bytes 2949124 | tf_op jit(solution)/shard_map/tf,fjc->jtc/dot_general | solution.py:101
  10.0 4.5 %collective-permute-done.5 = bf16[384,384]{1,0:T(8,128)(2,1)} collective-permute-done((bf16[384,384]{1,0:T(8,128)(2,1)}, bf16[384,384]{1,0:T(8,128)(2,1)}, u32[]{:S(2)}, u32[]{:S(2)}) %collective-permute-start.5) | collective-permute-done | bytes 294944 | tf_op jit(solution)/shard_map/ppermute | solution.py:17
  14.5 2.0 %fusion.4 = f32[3,384,384]{1,2,0:T(8,128)S(1)} fusion(bf16[3072,3,384]{2,0,1:T(8,128)(2,1)} %param.8, s32[]{:T(128)S(6)} %select_n.166, bf16[384,384]{1,0:T(8,128)(2,1)} %collective-permute-done.5), kind=kOutput, calls=%fused_computation.4 | convolution fusion | flops 339738624 | bytes 2949124 | tf_op jit(solution)/shard_map/tf,fjc->jtc/dot_general | solution.py:106
  16.6 10.2 %collective-permute-done = bf16[384,384]{1,0:T(8,128)(2,1)} collective-permute-done((bf16[384,384]{1,0:T(8,128)(2,1)}, bf16[384,384]{1,0:T(8,128)(2,1)}, u32[]{:S(2)}, u32[]{:S(2)}) %collective-permute-start) | collective-permute-done | bytes 294944 | tf_op jit(solution)/shard_map/ppermute | solution.py:17
  29.0 4.0 %collective-permute-done.1 = bf16[384,384]{1,0:T(8,128)(2,1)S(1)} collective-permute-done((bf16[384,384]{1,0:T(8,128)(2,1)S(1)}, bf16[384,384]{1,0:T(8,128)(2,1)S(1)}, u32[]{:S(2)}, u32[]{:S(2)}) %collective-permute-start.1) | collective-permute-done | bytes 294944 | tf_op jit(solution)/shard_map/ppermute | solution.py:17
  42.5 2.4 %collective-permute-start.8 = (bf16[2,3,384,128]{3,2,1,0:T(8,128)(2,1)S(1)}, bf16[2,3,384,128]{3,2,1,0:T(8,128)(2,1)}, u32[]{:S(2)}, u32[]{:S(2)}) collective-permute-start(bf16[2,3,384,128]{3,2,1,0:T(8,128)(2,1)S(1)} %pad_maximum_fusion.rest_0_), channel_id=1, source_target_pairs={{0,16},{8,24},{16,32},{24,40},{32,48},{40,56},{48,64},{56,72},{64,... | collective-permute-start | bytes 1769480 | tf_op jit(solution)/shard_map/ppermute | solution.py:17
  44.9 6.8 %collective-permute-start.10 = (bf16[2,3,384,128]{3,2,1,0:T(8,128)(2,1)S(1)}, bf16[2,3,384,128]{3,2,1,0:T(8,128)(2,1)S(1)}, u32[]{:S(2)}, u32[]{:S(2)}) collective-permute-start(bf16[2,3,384,128]{3,2,1,0:T(8,128)(2,1)S(1)} %pad_maximum_fusion.rest_0_), channel_id=1, source_target_pairs={{0,224},{8,232},{16,240},{24,248},{32,0},{40,8},{48,16},{56,24},{6... | collective-permute-start | bytes 1769480 | tf_op jit(solution)/shard_map/ppermute | solution.py:17
  51.6 2.3 %collective-permute-start.11 = (bf16[2,3,384,128]{3,2,1,0:T(8,128)(2,1)S(1)}, bf16[2,3,384,128]{3,2,1,0:T(8,128)(2,1)}, u32[]{:S(2)}, u32[]{:S(2)}) collective-permute-start(bf16[2,3,384,128]{3,2,1,0:T(8,128)(2,1)S(1)} %pad_maximum_fusion.rest_0_), channel_id=1, source_target_pairs={{0,8},{8,0},{16,24},{24,16},{32,40},{40,32},{48,56},{56,48},{64,72... | collective-permute-start | bytes 1769480 | tf_op jit(solution)/shard_map/ppermute | solution.py:123
  54.0 12.0 %collective-permute-done.9.rest_3_ = bf16[2,3,384,128]{3,2,1,0:T(8,128)(2,1)} collective-permute-done((bf16[2,3,384,128]{3,2,1,0:T(8,128)(2,1)S(1)}, bf16[2,3,384,128]{3,2,1,0:T(8,128)(2,1)}, u32[]{:S(2)}, u32[]{:S(2)}) %collective-permute-start.9) | collective-permute-done | bytes 589856 | tf_op jit(solution)/shard_map/ppermute | solution.py:17
  66.0 2.7 %collective-permute-start.13 = (bf16[2,3,384,128]{3,2,1,0:T(8,128)(2,1)}, bf16[2,3,384,128]{3,2,1,0:T(8,128)(2,1)}, u32[]{:S(2)}, u32[]{:S(2)}) collective-permute-start(bf16[2,3,384,128]{3,2,1,0:T(8,128)(2,1)} %collective-permute-done.9.rest_3_), channel_id=1, source_target_pairs={{0,8},{8,0},{16,24},{24,16},{32,40},{40,32},{48,56},{56,48},{64,72... | collective-permute-start | bytes 1769480 | tf_op jit(solution)/shard_map/ppermute | solution.py:125
  68.7 2.7 %collective-permute-done.8.rest_2_ = bf16[2,3,384,128]{3,2,1,0:T(8,128)(2,1)} collective-permute-done((bf16[2,3,384,128]{3,2,1,0:T(8,128)(2,1)S(1)}, bf16[2,3,384,128]{3,2,1,0:T(8,128)(2,1)}, u32[]{:S(2)}, u32[]{:S(2)}) %collective-permute-start.8) | collective-permute-done | bytes 589856 | tf_op jit(solution)/shard_map/ppermute | solution.py:17
  71.9 4.2 %collective-permute-done.7.rest_1_ = bf16[2,3,384,128]{3,2,1,0:T(8,128)(2,1)} collective-permute-done((bf16[2,3,384,128]{3,2,1,0:T(8,128)(2,1)S(1)}, bf16[2,3,384,128]{3,2,1,0:T(8,128)(2,1)}, u32[]{:S(2)}, u32[]{:S(2)}) %collective-permute-start.7) | collective-permute-done | bytes 589856 | tf_op jit(solution)/shard_map/ppermute | solution.py:17
  76.1 2.0 %broadcast_select_fusion = bf16[2,3,384,128]{3,2,1,0:T(8,128)(2,1)} fusion(bf16[2,3,384,128]{3,2,1,0:T(8,128)(2,1)S(1)} %collective-permute-done.10.rest_4_, bf16[2,3,384,128]{3,2,1,0:T(8,128)(2,1)} %collective-permute-done.7.rest_1_, pred[]{:T(512)S(6)} %eq.49), kind=kLoop, calls=%fused_computation.31 | loop fusion | flops 294912 | bytes 1769473 | tf_op jit(solution)/shard_map/jit(_where)/select_n | solution.py:126
  81.8 12.5 %shard_map.73 = bf16[384,384]{1,0:T(8,128)(2,1)} custom-call(s32[9]{0:T(128)} %convert_element_type.44.mask_ref, f32[384,384]{1,0:T(8,128)} %get-tuple-element.14.q_ref, f32[1,128]{1,0:T(1,128)} %bitcast.86, bf16[2,3,384,128]{3,2,1,0:T(8,128)(2,1)} %copy-done.3, bf16[2,3,384,128]{3,2,1,0:T(8,128)(2,1)} %collective-permute-done.7.rest_1_, ...), custom_call_target="tpu_custom_call" | custom-call | tf_op jit(solution)/shard_map/pallas_call | solution.py:67
  94.3 2.3 %convolution_convert_fusion = bf16[384,3072]{1,0:T(8,128)(2,1)S(1)} fusion(bf16[384,384]{1,0:T(8,128)(2,1)} %shard_map.73, bf16[384,3072]{1,0:T(8,128)(2,1)S(1)} %copy-done), kind=kOutput, calls=%fused_computation | convolution fusion | flops 907149312 | bytes 5013504 | tf_op jit(solution)/shard_map/dot_general | solution.py:151
  97.2 4.9 %constant_dynamic-slice_fusion.7 = (bf16[384,1,384]{2,1,0:T(2,128)(2,1)S(1)}, bf16[384,1,384]{2,1,0:T(2,128)(2,1)S(1)}, bf16[384,1,384]{2,1,0:T(2,128)(2,1)S(1)}...) fusion(bf16[384,8,384]{2,1,0:T(8,128)(2,1)S(1)} %bitcast.73, ...), kind=kLoop, calls=%fused_computation.57 | loop fusion | bytes 4718624 | tf_op jit(solution)/shard_map/dynamic-slice
  105.5 2.3 %collective-permute-start.17 = (bf16[384,384]{1,0:T(8,128)(2,1)S(1)}, bf16[384,384]{1,0:T(8,128)(2,1)S(1)}, u32[]{:S(2)}, u32[]{:S(2)}) collective-permute-start(bf16[384,384]{1,0:T(8,128)(2,1)S(1)} %bitcast.83), channel_id=1, source_target_pairs={{0,3},{1,4},{2,5},{3,6},{4,7},{5,0},{6,1},{7,2},{8,11},{9,12},{10,... | collective-permute-start | bytes 884744 | tf_op jit(solution)/shard_map/ppermute | solution.py:17
  108.8 2.5 %collective-permute-done.21 = bf16[384,384]{1,0:T(8,128)(2,1)S(1)} collective-permute-done((bf16[384,384]{1,0:T(8,128)(2,1)S(1)}, bf16[384,384]{1,0:T(8,128)(2,1)S(1)}, u32[]{:S(2)}, u32[]{:S(2)}) %collective-permute-start.21) | collective-permute-done | bytes 294944 | tf_op jit(solution)/shard_map/ppermute | solution.py:17
  112.6 2.4 %collective-permute-start.20 = (bf16[384,384]{1,0:T(8,128)(2,1)S(1)}, bf16[384,384]{1,0:T(8,128)(2,1)S(1)}, u32[]{:S(2)}, u32[]{:S(2)}) collective-permute-start(bf16[384,384]{1,0:T(8,128)(2,1)S(1)} %bitcast.79), channel_id=1, source_target_pairs={{0,6},{1,7},{2,0},{3,1},{4,2},{5,3},{6,4},{7,5},{8,14},{9,15},{10,... | collective-permute-start | bytes 884744 | tf_op jit(solution)/shard_map/ppermute | solution.py:17
  115.0 3.1 %collective-permute-done.16 = bf16[384,384]{1,0:T(8,128)(2,1)S(1)} collective-permute-done((bf16[384,384]{1,0:T(8,128)(2,1)S(1)}, bf16[384,384]{1,0:T(8,128)(2,1)S(1)}, u32[]{:S(2)}, u32[]{:S(2)}) %collective-permute-start.16) | collective-permute-done | bytes 294944 | tf_op jit(solution)/shard_map/ppermute | solution.py:17
  118.1 12.0 %collective-permute-done.17 = bf16[384,384]{1,0:T(8,128)(2,1)S(1)} collective-permute-done((bf16[384,384]{1,0:T(8,128)(2,1)S(1)}, bf16[384,384]{1,0:T(8,128)(2,1)S(1)}, u32[]{:S(2)}, u32[]{:S(2)}) %collective-permute-start.17) | collective-permute-done | bytes 294944 | tf_op jit(solution)/shard_map/ppermute | solution.py:17
  130.1 6.8 %collective-permute-done.18 = bf16[384,384]{1,0:T(8,128)(2,1)S(1)} collective-permute-done((bf16[384,384]{1,0:T(8,128)(2,1)S(1)}, bf16[384,384]{1,0:T(8,128)(2,1)S(1)}, u32[]{:S(2)}, u32[]{:S(2)}) %collective-permute-start.18) | collective-permute-done | bytes 294944 | tf_op jit(solution)/shard_map/ppermute | solution.py:17
  (76 shorter events, 25.3 us)
Async XLA Ops:
  0.0 94.3 %copy-start = (bf16[384,3072]{1,0:T(8,128)(2,1)S(1)}, bf16[384,3072]{1,0:T(8,128)(2,1)}, u32[]{:S(2)}) copy-start(bf16[384,3072]{1,0:T(8,128)(2,1)} %param.11) | copy-start | bytes 7077892
  0.0 14.5 %collective-permute-start.5 = (bf16[384,384]{1,0:T(8,128)(2,1)}, bf16[384,384]{1,0:T(8,128)(2,1)}, u32[]{:S(2)}, u32[]{:S(2)}) collective-permute-start(bf16[384,384]{1,0:T(8,128)(2,1)} %param.7), channel_id=1, source_target_pairs={{0,6},{1,7},{2,0},{3,1},{4,2},{5,3},{6,4},{7,5},{8,14},{9,15},{10,... | collective-permute-start | bytes 884744 | tf_op jit(solution)/shard_map/ppermute | solution.py:17
  0.2 36.0 %collective-permute-start.4 = (bf16[384,384]{1,0:T(8,128)(2,1)}, bf16[384,384]{1,0:T(8,128)(2,1)S(1)}, u32[]{:S(2)}, u32[]{:S(2)}) collective-permute-start(bf16[384,384]{1,0:T(8,128)(2,1)} %param.7), channel_id=1, source_target_pairs={{0,5},{1,6},{2,7},{3,0},{4,1},{5,2},{6,3},{7,4},{8,13},{9,14},{10,... | collective-permute-start | bytes 884744 | tf_op jit(solution)/shard_map/ppermute | solution.py:17
  2.7 32.8 %collective-permute-start.3 = (bf16[384,384]{1,0:T(8,128)(2,1)}, bf16[384,384]{1,0:T(8,128)(2,1)S(1)}, u32[]{:S(2)}, u32[]{:S(2)}) collective-permute-start(bf16[384,384]{1,0:T(8,128)(2,1)} %param.7), channel_id=1, source_target_pairs={{0,4},{1,5},{2,6},{3,7},{4,0},{5,1},{6,2},{7,3},{8,12},{9,13},{10,... | collective-permute-start | bytes 884744 | tf_op jit(solution)/shard_map/ppermute | solution.py:17
  4.7 30.1 %collective-permute-start.2 = (bf16[384,384]{1,0:T(8,128)(2,1)}, bf16[384,384]{1,0:T(8,128)(2,1)S(1)}, u32[]{:S(2)}, u32[]{:S(2)}) collective-permute-start(bf16[384,384]{1,0:T(8,128)(2,1)} %param.7), channel_id=1, source_target_pairs={{0,3},{1,4},{2,5},{3,6},{4,7},{5,0},{6,1},{7,2},{8,11},{9,12},{10,... | collective-permute-start | bytes 884744 | tf_op jit(solution)/shard_map/ppermute | solution.py:17
  5.5 21.3 %collective-permute-start = (bf16[384,384]{1,0:T(8,128)(2,1)}, bf16[384,384]{1,0:T(8,128)(2,1)}, u32[]{:S(2)}, u32[]{:S(2)}) collective-permute-start(bf16[384,384]{1,0:T(8,128)(2,1)} %param.7), channel_id=1, source_target_pairs={{0,1},{1,2},{2,3},{3,4},{4,5},{5,6},{6,7},{7,0},{8,9},{9,10},{10,1... | collective-permute-start | bytes 884744 | tf_op jit(solution)/shard_map/ppermute | solution.py:17
  14.5 18.6 %collective-permute-start.1 = (bf16[384,384]{1,0:T(8,128)(2,1)S(1)}, bf16[384,384]{1,0:T(8,128)(2,1)S(1)}, u32[]{:S(2)}, u32[]{:S(2)}) collective-permute-start(bf16[384,384]{1,0:T(8,128)(2,1)S(1)} %copy-done.5), channel_id=1, source_target_pairs={{0,2},{1,3},{2,4},{3,5},{4,6},{5,7},{6,0},{7,1},{8,10},{9,11},{10,... | collective-permute-start | bytes 884744 | tf_op jit(solution)/shard_map/ppermute | solution.py:17
  26.7 10.1 %collective-permute-start.6 = (bf16[384,384]{1,0:T(8,128)(2,1)S(1)}, bf16[384,384]{1,0:T(8,128)(2,1)S(1)}, u32[]{:S(2)}, u32[]{:S(2)}) collective-permute-start(bf16[384,384]{1,0:T(8,128)(2,1)S(1)} %copy-done.5), channel_id=1, source_target_pairs={{0,7},{1,0},{2,1},{3,2},{4,3},{5,4},{6,5},{7,6},{8,15},{9,8},{10,9... | collective-permute-start | bytes 884744 | tf_op jit(solution)/shard_map/ppermute | solution.py:17
  42.4 39.4 %copy-start.3 = (bf16[2,3,384,128]{3,2,1,0:T(8,128)(2,1)}, bf16[2,3,384,128]{3,2,1,0:T(8,128)(2,1)S(1)}, u32[]{:S(2)}) copy-start(bf16[2,3,384,128]{3,2,1,0:T(8,128)(2,1)S(1)} %pad_maximum_fusion.rest_0_) | copy-start | bytes 1769476
  42.4 23.6 %collective-permute-start.9 = (bf16[2,3,384,128]{3,2,1,0:T(8,128)(2,1)S(1)}, bf16[2,3,384,128]{3,2,1,0:T(8,128)(2,1)}, u32[]{:S(2)}, u32[]{:S(2)}) collective-permute-start(bf16[2,3,384,128]{3,2,1,0:T(8,128)(2,1)S(1)} %pad_maximum_fusion.rest_0_), channel_id=1, source_target_pairs={{0,240},{8,248},{16,0},{24,8},{32,16},{40,24},{48,32},{56,40},{64,... | collective-permute-start | bytes 1769480 | tf_op jit(solution)/shard_map/ppermute | solution.py:17
  42.5 28.9 %collective-permute-start.8 = (bf16[2,3,384,128]{3,2,1,0:T(8,128)(2,1)S(1)}, bf16[2,3,384,128]{3,2,1,0:T(8,128)(2,1)}, u32[]{:S(2)}, u32[]{:S(2)}) collective-permute-start(bf16[2,3,384,128]{3,2,1,0:T(8,128)(2,1)S(1)} %pad_maximum_fusion.rest_0_), channel_id=1, source_target_pairs={{0,16},{8,24},{16,32},{24,40},{32,48},{40,56},{48,64},{56,72},{64,... | collective-permute-start | bytes 1769480 | tf_op jit(solution)/shard_map/ppermute | solution.py:17
  44.9 27.0 %collective-permute-start.10 = (bf16[2,3,384,128]{3,2,1,0:T(8,128)(2,1)S(1)}, bf16[2,3,384,128]{3,2,1,0:T(8,128)(2,1)S(1)}, u32[]{:S(2)}, u32[]{:S(2)}) collective-permute-start(bf16[2,3,384,128]{3,2,1,0:T(8,128)(2,1)S(1)} %pad_maximum_fusion.rest_0_), channel_id=1, source_target_pairs={{0,224},{8,232},{16,240},{24,248},{32,0},{40,8},{48,16},{56,24},{6... | collective-permute-start | bytes 1769480 | tf_op jit(solution)/shard_map/ppermute | solution.py:17
  51.6 24.5 %collective-permute-start.7 = (bf16[2,3,384,128]{3,2,1,0:T(8,128)(2,1)S(1)}, bf16[2,3,384,128]{3,2,1,0:T(8,128)(2,1)}, u32[]{:S(2)}, u32[]{:S(2)}) collective-permute-start(bf16[2,3,384,128]{3,2,1,0:T(8,128)(2,1)S(1)} %pad_maximum_fusion.rest_0_), channel_id=1, source_target_pairs={{0,32},{8,40},{16,48},{24,56},{32,64},{40,72},{48,80},{56,88},{64,... | collective-permute-start | bytes 1769480 | tf_op jit(solution)/shard_map/ppermute | solution.py:17
  51.6 30.1 %collective-permute-start.11 = (bf16[2,3,384,128]{3,2,1,0:T(8,128)(2,1)S(1)}, bf16[2,3,384,128]{3,2,1,0:T(8,128)(2,1)}, u32[]{:S(2)}, u32[]{:S(2)}) collective-permute-start(bf16[2,3,384,128]{3,2,1,0:T(8,128)(2,1)S(1)} %pad_maximum_fusion.rest_0_), channel_id=1, source_target_pairs={{0,8},{8,0},{16,24},{24,16},{32,40},{40,32},{48,56},{56,48},{64,72... | collective-permute-start | bytes 1769480 | tf_op jit(solution)/shard_map/ppermute | solution.py:123
  66.0 15.8 %collective-permute-start.13 = (bf16[2,3,384,128]{3,2,1,0:T(8,128)(2,1)}, bf16[2,3,384,128]{3,2,1,0:T(8,128)(2,1)}, u32[]{:S(2)}, u32[]{:S(2)}) collective-permute-start(bf16[2,3,384,128]{3,2,1,0:T(8,128)(2,1)} %collective-permute-done.9.rest_3_), channel_id=1, source_target_pairs={{0,8},{8,0},{16,24},{24,16},{32,40},{40,32},{48,56},{56,48},{64,72... | collective-permute-start | bytes 1769480 | tf_op jit(solution)/shard_map/ppermute | solution.py:125
  71.4 10.4 %collective-permute-start.12 = (bf16[2,3,384,128]{3,2,1,0:T(8,128)(2,1)}, bf16[2,3,384,128]{3,2,1,0:T(8,128)(2,1)}, u32[]{:S(2)}, u32[]{:S(2)}) collective-permute-start(bf16[2,3,384,128]{3,2,1,0:T(8,128)(2,1)} %collective-permute-done.8.rest_2_), channel_id=1, source_target_pairs={{0,8},{8,0},{16,24},{24,16},{32,40},{40,32},{48,56},{56,48},{64,72... | collective-permute-start | bytes 1769480 | tf_op jit(solution)/shard_map/ppermute | solution.py:124
  78.1 3.7 %collective-permute-start.14 = (bf16[2,3,384,128]{3,2,1,0:T(8,128)(2,1)}, bf16[2,3,384,128]{3,2,1,0:T(8,128)(2,1)}, u32[]{:S(2)}, u32[]{:S(2)}) collective-permute-start(bf16[2,3,384,128]{3,2,1,0:T(8,128)(2,1)} %broadcast_select_fusion), channel_id=1, source_target_pairs={{0,8},{8,0},{16,24},{24,16},{32,40},{40,32},{48,56},{56,48},{64,72... | collective-permute-start | bytes 1769480 | tf_op jit(solution)/shard_map/ppermute | solution.py:126
  102.2 9.1 %collective-permute-start.21 = (bf16[384,384]{1,0:T(8,128)(2,1)S(1)}, bf16[384,384]{1,0:T(8,128)(2,1)S(1)}, u32[]{:S(2)}, u32[]{:S(2)}) collective-permute-start(bf16[384,384]{1,0:T(8,128)(2,1)S(1)} %bitcast.84), channel_id=1, source_target_pairs={{0,7},{1,0},{2,1},{3,2},{4,3},{5,4},{6,5},{7,6},{8,15},{9,8},{10,9... | collective-permute-start | bytes 884744 | tf_op jit(solution)/shard_map/ppermute | solution.py:17
  102.3 10.3 %collective-permute-start.15 = (bf16[384,384]{1,0:T(8,128)(2,1)S(1)}, bf16[384,384]{1,0:T(8,128)(2,1)S(1)}, u32[]{:S(2)}, u32[]{:S(2)}) collective-permute-start(bf16[384,384]{1,0:T(8,128)(2,1)S(1)} %bitcast.82), channel_id=1, source_target_pairs={{0,1},{1,2},{2,3},{3,4},{4,5},{5,6},{6,7},{7,0},{8,9},{9,10},{10,1... | collective-permute-start | bytes 884744 | tf_op jit(solution)/shard_map/ppermute | solution.py:17
  104.1 14.0 %collective-permute-start.16 = (bf16[384,384]{1,0:T(8,128)(2,1)S(1)}, bf16[384,384]{1,0:T(8,128)(2,1)S(1)}, u32[]{:S(2)}, u32[]{:S(2)}) collective-permute-start(bf16[384,384]{1,0:T(8,128)(2,1)S(1)} %bitcast.85), channel_id=1, source_target_pairs={{0,2},{1,3},{2,4},{3,5},{4,6},{5,7},{6,0},{7,1},{8,10},{9,11},{10,... | collective-permute-start | bytes 884744 | tf_op jit(solution)/shard_map/ppermute | solution.py:17
  105.5 24.6 %collective-permute-start.17 = (bf16[384,384]{1,0:T(8,128)(2,1)S(1)}, bf16[384,384]{1,0:T(8,128)(2,1)S(1)}, u32[]{:S(2)}, u32[]{:S(2)}) collective-permute-start(bf16[384,384]{1,0:T(8,128)(2,1)S(1)} %bitcast.83), channel_id=1, source_target_pairs={{0,3},{1,4},{2,5},{3,6},{4,7},{5,0},{6,1},{7,2},{8,11},{9,12},{10,... | collective-permute-start | bytes 884744 | tf_op jit(solution)/shard_map/ppermute | solution.py:17
  107.8 29.1 %collective-permute-start.18 = (bf16[384,384]{1,0:T(8,128)(2,1)S(1)}, bf16[384,384]{1,0:T(8,128)(2,1)S(1)}, u32[]{:S(2)}, u32[]{:S(2)}) collective-permute-start(bf16[384,384]{1,0:T(8,128)(2,1)S(1)} %bitcast.81), channel_id=1, source_target_pairs={{0,4},{1,5},{2,6},{3,7},{4,0},{5,1},{6,2},{7,3},{8,12},{9,13},{10,... | collective-permute-start | bytes 884744 | tf_op jit(solution)/shard_map/ppermute | solution.py:17
  111.3 25.6 %collective-permute-start.19 = (bf16[384,384]{1,0:T(8,128)(2,1)S(1)}, bf16[384,384]{1,0:T(8,128)(2,1)S(1)}, u32[]{:S(2)}, u32[]{:S(2)}) collective-permute-start(bf16[384,384]{1,0:T(8,128)(2,1)S(1)} %bitcast.80), channel_id=1, source_target_pairs={{0,5},{1,6},{2,7},{3,0},{4,1},{5,2},{6,3},{7,4},{8,13},{9,14},{10,... | collective-permute-start | bytes 884744 | tf_op jit(solution)/shard_map/ppermute | solution.py:17
  112.6 24.3 %collective-permute-start.20 = (bf16[384,384]{1,0:T(8,128)(2,1)S(1)}, bf16[384,384]{1,0:T(8,128)(2,1)S(1)}, u32[]{:S(2)}, u32[]{:S(2)}) collective-permute-start(bf16[384,384]{1,0:T(8,128)(2,1)S(1)} %bitcast.79), channel_id=1, source_target_pairs={{0,6},{1,7},{2,0},{3,1},{4,2},{5,3},{6,4},{7,5},{8,14},{9,15},{10,... | collective-permute-start | bytes 884744 | tf_op jit(solution)/shard_map/ppermute | solution.py:17
  (7 other events, 123.1 us)

commit v3 on v2

--- a/solution.py
+++ b/solution.py
@@ -148,8 +148,12 @@
     q_raw = projected[0]
     attended = attend(tile_mask, q_raw, q_gain, kv_tiles)
     out_cols = w_out.shape[1] // mp_count
-    terms = jnp.dot(attended, w_out, preferred_element_type=jnp.float32).astype(jnp.bfloat16)
-    terms = terms.reshape(tok_rows, mp_count, out_cols).transpose(1, 0, 2)
+    terms = jnp.einsum(
+        "tk,kjc->jtc",
+        attended,
+        w_out.reshape(w_out.shape[0], mp_count, out_cols),
+        preferred_element_type=jnp.float32,
+    ).astype(jnp.bfloat16)
     total = lax.dynamic_index_in_dim(terms, mp_here, 0, keepdims=False).astype(jnp.float32)
     for step in range(1, mp_count):
         target = (mp_here + step) % mp_count

time: 137 us -> 134 us (0.978)
  the two profiles are of different devices: /device:TPU:29 before, /device:TPU:8 now
where the time goes in v3:
time: 134 us
  waiting for transfers between devices  61.6 us (46%)
  starting transfers between devices  37.6 us (28%)
  matrix products  13.4 us (10%)
  Pallas kernels  10.6 us (8%)
  local copies, waits for them, and re-layouts  5.6 us (4%)
  other arithmetic  5.14 us (4%)
    ppermute x18, waiting for transfers between devices, passed_along(): return lax.ppermute(value, axis, pairs)  61.5 us
    ppermute x18, starting transfers between devices, passed_along(): return lax.ppermute(value, axis, pairs)  37.6 us
    pallas_call x1, Pallas kernels, attend(): pl.pallas_call(attend_kernel, grid_spec=pltpu.PrefetchScalarGridSpec(num_...  10.6 us
    dot_general x7, matrix products, on_device(): jnp.einsum('tf,fjc->jtc', passed_along(tokens, 'mp', step), rows_of(sourc...  8.34 us
    dot_general x1, matrix products, on_device(): jnp.einsum('tk,kjc->jtc', attended, w_out.reshape(w_out.shape[0], mp_coun...  3.16 us
  transfers between devices with their start and end apart: 22, of which 11 were waited for; matrix products, arithmetic and copies ran while one was open for 9% of the time, Pallas kernels for 0%

profile of v3, /device:TPU:8, one launch (start us, length us, event | category | flops | bytes accessed | tf_op | source)
XLA Modules:
  0.0 134.3 jit_solution(4889287980329600259)
XLA Ops:
  0.0 4.8 %collective-permute-start.5 = (bf16[384,384]{1,0:T(8,128)(2,1)}, bf16[384,384]{1,0:T(8,128)(2,1)S(1)}, u32[]{:S(2)}, u32[]{:S(2)}) collective-permute-start(bf16[384,384]{1,0:T(8,128)(2,1)} %param.7), channel_id=1, source_target_pairs={{0,6},{1,7},{2,0},{3,1},{4,2},{5,3},{6,4},{7,5},{8,14},{9,15},{10,... | collective-permute-start | bytes 884744 | tf_op jit(solution)/shard_map/ppermute | solution.py:17
  6.0 2.3 %collective-permute-start.3 = (bf16[384,384]{1,0:T(8,128)(2,1)}, bf16[384,384]{1,0:T(8,128)(2,1)S(1)}, u32[]{:S(2)}, u32[]{:S(2)}) collective-permute-start(bf16[384,384]{1,0:T(8,128)(2,1)} %param.7), channel_id=1, source_target_pairs={{0,4},{1,5},{2,6},{3,7},{4,0},{5,1},{6,2},{7,3},{8,12},{9,13},{10,... | collective-permute-start | bytes 884744 | tf_op jit(solution)/shard_map/ppermute | solution.py:17
  9.2 1.8 %collective-permute-start = (bf16[384,384]{1,0:T(8,128)(2,1)}, bf16[384,384]{1,0:T(8,128)(2,1)S(1)}, u32[]{:S(2)}, u32[]{:S(2)}) collective-permute-start(bf16[384,384]{1,0:T(8,128)(2,1)} %param.7), channel_id=1, source_target_pairs={{0,1},{1,2},{2,3},{3,4},{4,5},{5,6},{6,7},{7,0},{8,9},{9,10},{10,1... | collective-permute-start | bytes 884744 | tf_op jit(solution)/shard_map/ppermute | solution.py:17
  11.0 1.9 %fusion.22 = f32[3,384,384]{1,2,0:T(8,128)S(1)} fusion(bf16[3072,3,384]{2,0,1:T(8,128)(2,1)} %param.8, s32[]{:T(128)S(6)} %select_n.154, bf16[384,384]{1,0:T(8,128)(2,1)} %param.7), kind=kOutput, calls=%fused_computation.19 | convolution fusion | flops 339738624 | bytes 2949124 | tf_op jit(solution)/shard_map/tf,fjc->jtc/dot_general | solution.py:101
  13.1 6.4 %collective-permute-start.1 = (bf16[384,384]{1,0:T(8,128)(2,1)S(1)}, bf16[384,384]{1,0:T(8,128)(2,1)S(1)}, u32[]{:S(2)}, u32[]{:S(2)}) collective-permute-start(bf16[384,384]{1,0:T(8,128)(2,1)S(1)} %copy-done.8), channel_id=1, source_target_pairs={{0,2},{1,3},{2,4},{3,5},{4,6},{5,7},{6,0},{7,1},{8,10},{9,11},{10,... | collective-permute-start | bytes 884744 | tf_op jit(solution)/shard_map/ppermute | solution.py:17
  19.5 2.0 %fusion.10 = f32[3,384,384]{1,2,0:T(8,128)S(1)} fusion(bf16[3072,3,384]{2,0,1:T(8,128)(2,1)} %param.8, s32[]{:T(128)S(6)} %select_n.166, bf16[384,384]{1,0:T(8,128)(2,1)S(1)} %collective-permute-done.5), kind=kOutput, calls=%fused_computation.7 | convolution fusion | flops 339738624 | bytes 2949124 | tf_op jit(solution)/shard_map/tf,fjc->jtc/dot_general | solution.py:106
  21.5 7.7 %collective-permute-done = bf16[384,384]{1,0:T(8,128)(2,1)S(1)} collective-permute-done((bf16[384,384]{1,0:T(8,128)(2,1)}, bf16[384,384]{1,0:T(8,128)(2,1)S(1)}, u32[]{:S(2)}, u32[]{:S(2)}) %collective-permute-start) | collective-permute-done | bytes 294944 | tf_op jit(solution)/shard_map/ppermute | solution.py:17
  29.4 1.8 %fusion.20 = f32[3,384,384]{1,2,0:T(8,128)S(1)} fusion(bf16[3072,3,384]{2,0,1:T(8,128)(2,1)} %param.8, s32[]{:T(128)S(6)} %select_n.156, bf16[384,384]{1,0:T(8,128)(2,1)S(1)} %collective-permute-done), kind=kOutput, calls=%fused_computation.17 | convolution fusion | flops 339738624 | bytes 2949124 | tf_op jit(solution)/shard_map/tf,fjc->jtc/dot_general | solution.py:106
  31.3 3.1 %collective-permute-done.1 = bf16[384,384]{1,0:T(8,128)(2,1)S(1)} collective-permute-done((bf16[384,384]{1,0:T(8,128)(2,1)S(1)}, bf16[384,384]{1,0:T(8,128)(2,1)S(1)}, u32[]{:S(2)}, u32[]{:S(2)}) %collective-permute-start.1) | collective-permute-done | bytes 294944 | tf_op jit(solution)/shard_map/ppermute | solution.py:17
  34.3 1.8 %fusion.18 = f32[3,384,384]{1,2,0:T(8,128)S(1)} fusion(bf16[3072,3,384]{2,0,1:T(8,128)(2,1)} %param.8, s32[]{:T(128)S(6)} %select_n.158, bf16[384,384]{1,0:T(8,128)(2,1)S(1)} %collective-permute-done.1), kind=kOutput, calls=%fused_computation.15 | convolution fusion | flops 339738624 | bytes 2949124 | tf_op jit(solution)/shard_map/tf,fjc->jtc/dot_general | solution.py:106
  42.3 2.0 %collective-permute-start.8 = (bf16[2,3,384,128]{3,2,1,0:T(8,128)(2,1)S(1)}, bf16[2,3,384,128]{3,2,1,0:T(8,128)(2,1)S(1)}, u32[]{:S(2)}, u32[]{:S(2)}) collective-permute-start(bf16[2,3,384,128]{3,2,1,0:T(8,128)(2,1)S(1)} %pad_maximum_fusion.rest_0_), channel_id=1, source_target_pairs={{0,16},{8,24},{16,32},{24,40},{32,48},{40,56},{48,64},{56,72},{64,... | collective-permute-start | bytes 1769480 | tf_op jit(solution)/shard_map/ppermute | solution.py:17
  44.3 7.1 %collective-permute-start.10 = (bf16[2,3,384,128]{3,2,1,0:T(8,128)(2,1)S(1)}, bf16[2,3,384,128]{3,2,1,0:T(8,128)(2,1)S(1)}, u32[]{:S(2)}, u32[]{:S(2)}) collective-permute-start(bf16[2,3,384,128]{3,2,1,0:T(8,128)(2,1)S(1)} %pad_maximum_fusion.rest_0_), channel_id=1, source_target_pairs={{0,224},{8,232},{16,240},{24,248},{32,0},{40,8},{48,16},{56,24},{6... | collective-permute-start | bytes 1769480 | tf_op jit(solution)/shard_map/ppermute | solution.py:17
  51.3 15.4 %collective-permute-done.9.rest_3_ = bf16[2,3,384,128]{3,2,1,0:T(8,128)(2,1)S(1)} collective-permute-done((bf16[2,3,384,128]{3,2,1,0:T(8,128)(2,1)S(1)}, bf16[2,3,384,128]{3,2,1,0:T(8,128)(2,1)S(1)}, u32[]{:S(2)}, u32[]{:S(2)}) %collective-permute-start.9) | collective-permute-done | bytes 589856 | tf_op jit(solution)/shard_map/ppermute | solution.py:17
  66.7 2.4 %collective-permute-done.8.rest_2_ = bf16[2,3,384,128]{3,2,1,0:T(8,128)(2,1)S(1)} collective-permute-done((bf16[2,3,384,128]{3,2,1,0:T(8,128)(2,1)S(1)}, bf16[2,3,384,128]{3,2,1,0:T(8,128)(2,1)S(1)}, u32[]{:S(2)}, u32[]{:S(2)}) %collective-permute-start.8) | collective-permute-done | bytes 589856 | tf_op jit(solution)/shard_map/ppermute | solution.py:17
  69.2 6.8 %collective-permute-done.7.rest_1_ = bf16[2,3,384,128]{3,2,1,0:T(8,128)(2,1)S(1)} collective-permute-done((bf16[2,3,384,128]{3,2,1,0:T(8,128)(2,1)S(1)}, bf16[2,3,384,128]{3,2,1,0:T(8,128)(2,1)S(1)}, u32[]{:S(2)}, u32[]{:S(2)}) %collective-permute-start.7) | collective-permute-done | bytes 589856 | tf_op jit(solution)/shard_map/ppermute | solution.py:17
  80.0 10.6 %shard_map.73 = bf16[384,384]{1,0:T(8,128)(2,1)} custom-call(s32[9]{0:T(128)} %convert_element_type.46.mask_ref, f32[384,384]{1,0:T(8,128)} %get-tuple-element.13.q_ref, f32[1,128]{1,0:T(1,128)} %bitcast.73, bf16[2,3,384,128]{3,2,1,0:T(8,128)(2,1)} %copy-done.2, bf16[2,3,384,128]{3,2,1,0:T(8,128)(2,1)} %copy-done.4, bf16[2,3,384,128]{3,2,1,0:T(8,128)(2,1)} %copy-done.6, ...), custom_call_target="tpu_custom_call" | custom-call | tf_op jit(solution)/shard_map/pallas_call | solution.py:67
  90.6 3.2 %fusion.3 = bf16[384,8,384]{2,0,1:T(8,128)(2,1)S(1)} fusion(bf16[48,8,8,384]{3,2,1,0:T(8,128)(2,1)} %bitcast.74, bf16[384,384]{1,0:T(8,128)(2,1)} %shard_map.73), kind=kOutput, calls=%fused_computation.3 | convolution fusion | flops 907149312 | bytes 5013504 | tf_op jit(solution)/shard_map/tk,kjc->jtc/dot_general | solution.py:151
  94.7 5.6 %collective-permute-start.21 = (bf16[384,384]{1,0:T(8,128)(2,1)S(1)}, bf16[384,384]{1,0:T(8,128)(2,1)S(1)}, u32[]{:S(2)}, u32[]{:S(2)}) collective-permute-start(bf16[384,384]{1,0:T(8,128)(2,1)S(1)} %get-tuple-element.6), channel_id=1, source_target_pairs={{0,7},{1,0},{2,1},{3,2},{4,3},{5,4},{6,5},{7,6},{8,15},{9,8},{10,9... | collective-permute-start | bytes 884744 | tf_op jit(solution)/shard_map/ppermute | solution.py:17
  101.0 1.6 %collective-permute-start.19 = (bf16[384,384]{1,0:T(8,128)(2,1)S(1)}, bf16[384,384]{1,0:T(8,128)(2,1)}, u32[]{:S(2)}, u32[]{:S(2)}) collective-permute-start(bf16[384,384]{1,0:T(8,128)(2,1)S(1)} %get-tuple-element.8), channel_id=1, source_target_pairs={{0,5},{1,6},{2,7},{3,0},{4,1},{5,2},{6,3},{7,4},{8,13},{9,14},{10,... | collective-permute-start | bytes 884744 | tf_op jit(solution)/shard_map/ppermute | solution.py:17
  104.2 10.3 %collective-permute-done.15 = bf16[384,384]{1,0:T(8,128)(2,1)S(1)} collective-permute-done((bf16[384,384]{1,0:T(8,128)(2,1)S(1)}, bf16[384,384]{1,0:T(8,128)(2,1)S(1)}, u32[]{:S(2)}, u32[]{:S(2)}) %collective-permute-start.15) | collective-permute-done | bytes 294944 | tf_op jit(solution)/shard_map/ppermute | solution.py:17
  116.3 3.2 %collective-permute-done.19 = bf16[384,384]{1,0:T(8,128)(2,1)} collective-permute-done((bf16[384,384]{1,0:T(8,128)(2,1)S(1)}, bf16[384,384]{1,0:T(8,128)(2,1)}, u32[]{:S(2)}, u32[]{:S(2)}) %collective-permute-start.19) | collective-permute-done | bytes 294944 | tf_op jit(solution)/shard_map/ppermute | solution.py:17
  119.6 8.4 %collective-permute-done.17 = bf16[384,384]{1,0:T(8,128)(2,1)} collective-permute-done((bf16[384,384]{1,0:T(8,128)(2,1)S(1)}, bf16[384,384]{1,0:T(8,128)(2,1)}, u32[]{:S(2)}, u32[]{:S(2)}) %collective-permute-start.17) | collective-permute-done | bytes 294944 | tf_op jit(solution)/shard_map/ppermute | solution.py:17
  128.0 3.8 %collective-permute-done.16 = bf16[384,384]{1,0:T(8,128)(2,1)} collective-permute-done((bf16[384,384]{1,0:T(8,128)(2,1)S(1)}, bf16[384,384]{1,0:T(8,128)(2,1)}, u32[]{:S(2)}, u32[]{:S(2)}) %collective-permute-start.16) | collective-permute-done | bytes 294944 | tf_op jit(solution)/shard_map/ppermute | solution.py:17
  131.8 2.5 %fusion.30 = bf16[384,384]{1,0:T(8,128)(2,1)} fusion(bf16[384,384]{1,0:T(8,128)(2,1)} %copy-done.10, bf16[384,384]{1,0:T(8,128)(2,1)} %collective-permute-done.20, bf16[384,384]{1,0:T(8,128)(2,1)} %collective-permute-done.19, bf16[384,384]{1,0:T(8,128)(2,1)} %collective-permute-done.18, bf16[384,384]{1,0:T(8,128)(2,1)} %collective-permute-done.17, ...), kind=kLoop, calls=%fused_computation.31 | loop fusion | flops 2359296 | bytes 2654212 | tf_op jit(solution)/shard_map/convert_element_type | solution.py:162
  (76 shorter events, 17.5 us)
Async XLA Ops:
  0.0 77.6 %copy-start = (s32[32,6]{0,1:T(8,128)S(1)}, s32[32,6]{0,1:T(8,128)}, u32[]{:S(2)}) copy-start(s32[32,6]{0,1:T(8,128)} %param.12) | copy-start | bytes 2308
  0.0 13.1 %collective-permute-start.5 = (bf16[384,384]{1,0:T(8,128)(2,1)}, bf16[384,384]{1,0:T(8,128)(2,1)S(1)}, u32[]{:S(2)}, u32[]{:S(2)}) collective-permute-start(bf16[384,384]{1,0:T(8,128)(2,1)} %param.7), channel_id=1, source_target_pairs={{0,6},{1,7},{2,0},{3,1},{4,2},{5,3},{6,4},{7,5},{8,14},{9,15},{10,... | collective-permute-start | bytes 884744 | tf_op jit(solution)/shard_map/ppermute | solution.py:17
  4.8 32.7 %collective-permute-start.4 = (bf16[384,384]{1,0:T(8,128)(2,1)}, bf16[384,384]{1,0:T(8,128)(2,1)S(1)}, u32[]{:S(2)}, u32[]{:S(2)}) collective-permute-start(bf16[384,384]{1,0:T(8,128)(2,1)} %param.7), channel_id=1, source_target_pairs={{0,5},{1,6},{2,7},{3,0},{4,1},{5,2},{6,3},{7,4},{8,13},{9,14},{10,... | collective-permute-start | bytes 884744 | tf_op jit(solution)/shard_map/ppermute | solution.py:17
  6.0 30.8 %collective-permute-start.3 = (bf16[384,384]{1,0:T(8,128)(2,1)}, bf16[384,384]{1,0:T(8,128)(2,1)S(1)}, u32[]{:S(2)}, u32[]{:S(2)}) collective-permute-start(bf16[384,384]{1,0:T(8,128)(2,1)} %param.7), channel_id=1, source_target_pairs={{0,4},{1,5},{2,6},{3,7},{4,0},{5,1},{6,2},{7,3},{8,12},{9,13},{10,... | collective-permute-start | bytes 884744 | tf_op jit(solution)/shard_map/ppermute | solution.py:17
  8.3 27.8 %collective-permute-start.2 = (bf16[384,384]{1,0:T(8,128)(2,1)}, bf16[384,384]{1,0:T(8,128)(2,1)S(1)}, u32[]{:S(2)}, u32[]{:S(2)}) collective-permute-start(bf16[384,384]{1,0:T(8,128)(2,1)} %param.7), channel_id=1, source_target_pairs={{0,3},{1,4},{2,5},{3,6},{4,7},{5,0},{6,1},{7,2},{8,11},{9,12},{10,... | collective-permute-start | bytes 884744 | tf_op jit(solution)/shard_map/ppermute | solution.py:17
  9.2 20.0 %collective-permute-start = (bf16[384,384]{1,0:T(8,128)(2,1)}, bf16[384,384]{1,0:T(8,128)(2,1)S(1)}, u32[]{:S(2)}, u32[]{:S(2)}) collective-permute-start(bf16[384,384]{1,0:T(8,128)(2,1)} %param.7), channel_id=1, source_target_pairs={{0,1},{1,2},{2,3},{3,4},{4,5},{5,6},{6,7},{7,0},{8,9},{9,10},{10,1... | collective-permute-start | bytes 884744 | tf_op jit(solution)/shard_map/ppermute | solution.py:17
  13.1 21.2 %collective-permute-start.1 = (bf16[384,384]{1,0:T(8,128)(2,1)S(1)}, bf16[384,384]{1,0:T(8,128)(2,1)S(1)}, u32[]{:S(2)}, u32[]{:S(2)}) collective-permute-start(bf16[384,384]{1,0:T(8,128)(2,1)S(1)} %copy-done.8), channel_id=1, source_target_pairs={{0,2},{1,3},{2,4},{3,5},{4,6},{5,7},{6,0},{7,1},{8,10},{9,11},{10,... | collective-permute-start | bytes 884744 | tf_op jit(solution)/shard_map/ppermute | solution.py:17
  29.2 8.9 %collective-permute-start.6 = (bf16[384,384]{1,0:T(8,128)(2,1)S(1)}, bf16[384,384]{1,0:T(8,128)(2,1)S(1)}, u32[]{:S(2)}, u32[]{:S(2)}) collective-permute-start(bf16[384,384]{1,0:T(8,128)(2,1)S(1)} %copy-done.8), channel_id=1, source_target_pairs={{0,7},{1,0},{2,1},{3,2},{4,3},{5,4},{6,5},{7,6},{8,15},{9,8},{10,9... | collective-permute-start | bytes 884744 | tf_op jit(solution)/shard_map/ppermute | solution.py:17
  41.3 38.1 %copy-start.2 = (bf16[2,3,384,128]{3,2,1,0:T(8,128)(2,1)}, bf16[2,3,384,128]{3,2,1,0:T(8,128)(2,1)S(1)}, u32[]{:S(2)}) copy-start(bf16[2,3,384,128]{3,2,1,0:T(8,128)(2,1)S(1)} %pad_maximum_fusion.rest_0_) | copy-start | bytes 1769476
  41.3 25.4 %collective-permute-start.9 = (bf16[2,3,384,128]{3,2,1,0:T(8,128)(2,1)S(1)}, bf16[2,3,384,128]{3,2,1,0:T(8,128)(2,1)S(1)}, u32[]{:S(2)}, u32[]{:S(2)}) collective-permute-start(bf16[2,3,384,128]{3,2,1,0:T(8,128)(2,1)S(1)} %pad_maximum_fusion.rest_0_), channel_id=1, source_target_pairs={{0,240},{8,248},{16,0},{24,8},{32,16},{40,24},{48,32},{56,40},{64,... | collective-permute-start | bytes 1769480 | tf_op jit(solution)/shard_map/ppermute | solution.py:17
  42.3 26.9 %collective-permute-start.8 = (bf16[2,3,384,128]{3,2,1,0:T(8,128)(2,1)S(1)}, bf16[2,3,384,128]{3,2,1,0:T(8,128)(2,1)S(1)}, u32[]{:S(2)}, u32[]{:S(2)}) collective-permute-start(bf16[2,3,384,128]{3,2,1,0:T(8,128)(2,1)S(1)} %pad_maximum_fusion.rest_0_), channel_id=1, source_target_pairs={{0,16},{8,24},{16,32},{24,40},{32,48},{40,56},{48,64},{56,72},{64,... | collective-permute-start | bytes 1769480 | tf_op jit(solution)/shard_map/ppermute | solution.py:17
  44.3 24.9 %collective-permute-start.10 = (bf16[2,3,384,128]{3,2,1,0:T(8,128)(2,1)S(1)}, bf16[2,3,384,128]{3,2,1,0:T(8,128)(2,1)S(1)}, u32[]{:S(2)}, u32[]{:S(2)}) collective-permute-start(bf16[2,3,384,128]{3,2,1,0:T(8,128)(2,1)S(1)} %pad_maximum_fusion.rest_0_), channel_id=1, source_target_pairs={{0,224},{8,232},{16,240},{24,248},{32,0},{40,8},{48,16},{56,24},{6... | collective-permute-start | bytes 1769480 | tf_op jit(solution)/shard_map/ppermute | solution.py:17
  51.3 24.6 %collective-permute-start.7 = (bf16[2,3,384,128]{3,2,1,0:T(8,128)(2,1)S(1)}, bf16[2,3,384,128]{3,2,1,0:T(8,128)(2,1)S(1)}, u32[]{:S(2)}, u32[]{:S(2)}) collective-permute-start(bf16[2,3,384,128]{3,2,1,0:T(8,128)(2,1)S(1)} %pad_maximum_fusion.rest_0_), channel_id=1, source_target_pairs={{0,32},{8,40},{16,48},{24,56},{32,64},{40,72},{48,80},{56,88},{64,... | collective-permute-start | bytes 1769480 | tf_op jit(solution)/shard_map/ppermute | solution.py:17
  51.3 27.9 %collective-permute-start.11 = (bf16[2,3,384,128]{3,2,1,0:T(8,128)(2,1)S(1)}, bf16[2,3,384,128]{3,2,1,0:T(8,128)(2,1)S(1)}, u32[]{:S(2)}, u32[]{:S(2)}) collective-permute-start(bf16[2,3,384,128]{3,2,1,0:T(8,128)(2,1)S(1)} %pad_maximum_fusion.rest_0_), channel_id=1, source_target_pairs={{0,8},{8,0},{16,24},{24,16},{32,40},{40,32},{48,56},{56,48},{64,72... | collective-permute-start | bytes 1769480 | tf_op jit(solution)/shard_map/ppermute | solution.py:123
  66.7 12.5 %collective-permute-start.13 = (bf16[2,3,384,128]{3,2,1,0:T(8,128)(2,1)S(1)}, bf16[2,3,384,128]{3,2,1,0:T(8,128)(2,1)}, u32[]{:S(2)}, u32[]{:S(2)}) collective-permute-start(bf16[2,3,384,128]{3,2,1,0:T(8,128)(2,1)S(1)} %collective-permute-done.9.rest_3_), channel_id=1, source_target_pairs={{0,8},{8,0},{16,24},{24,16},{32,40},{40,32},{48,56},{56,48},{64,72... | collective-permute-start | bytes 1769480 | tf_op jit(solution)/shard_map/ppermute | solution.py:125
  69.1 10.1 %collective-permute-start.12 = (bf16[2,3,384,128]{3,2,1,0:T(8,128)(2,1)S(1)}, bf16[2,3,384,128]{3,2,1,0:T(8,128)(2,1)}, u32[]{:S(2)}, u32[]{:S(2)}) collective-permute-start(bf16[2,3,384,128]{3,2,1,0:T(8,128)(2,1)S(1)} %collective-permute-done.8.rest_2_), channel_id=1, source_target_pairs={{0,8},{8,0},{16,24},{24,16},{32,40},{40,32},{48,56},{56,48},{64,72... | collective-permute-start | bytes 1769480 | tf_op jit(solution)/shard_map/ppermute | solution.py:124
  77.0 2.3 %collective-permute-start.14 = (bf16[2,3,384,128]{3,2,1,0:T(8,128)(2,1)}, bf16[2,3,384,128]{3,2,1,0:T(8,128)(2,1)}, u32[]{:S(2)}, u32[]{:S(2)}) collective-permute-start(bf16[2,3,384,128]{3,2,1,0:T(8,128)(2,1)} %broadcast_select_fusion), channel_id=1, source_target_pairs={{0,8},{8,0},{16,24},{24,16},{32,40},{40,32},{48,56},{56,48},{64,72... | collective-permute-start | bytes 1769480 | tf_op jit(solution)/shard_map/ppermute | solution.py:126
  94.7 19.8 %collective-permute-start.15 = (bf16[384,384]{1,0:T(8,128)(2,1)S(1)}, bf16[384,384]{1,0:T(8,128)(2,1)S(1)}, u32[]{:S(2)}, u32[]{:S(2)}) collective-permute-start(bf16[384,384]{1,0:T(8,128)(2,1)S(1)} %get-tuple-element.5), channel_id=1, source_target_pairs={{0,1},{1,2},{2,3},{3,4},{4,5},{5,6},{6,7},{7,0},{8,9},{9,10},{10,1... | collective-permute-start | bytes 884744 | tf_op jit(solution)/shard_map/ppermute | solution.py:17
  94.7 20.1 %collective-permute-start.21 = (bf16[384,384]{1,0:T(8,128)(2,1)S(1)}, bf16[384,384]{1,0:T(8,128)(2,1)S(1)}, u32[]{:S(2)}, u32[]{:S(2)}) collective-permute-start(bf16[384,384]{1,0:T(8,128)(2,1)S(1)} %get-tuple-element.6), channel_id=1, source_target_pairs={{0,7},{1,0},{2,1},{3,2},{4,3},{5,4},{6,5},{7,6},{8,15},{9,8},{10,9... | collective-permute-start | bytes 884744 | tf_op jit(solution)/shard_map/ppermute | solution.py:17
  100.4 16.0 %collective-permute-start.20 = (bf16[384,384]{1,0:T(8,128)(2,1)}, bf16[384,384]{1,0:T(8,128)(2,1)}, u32[]{:S(2)}, u32[]{:S(2)}) collective-permute-start(bf16[384,384]{1,0:T(8,128)(2,1)} %get-tuple-element.7), channel_id=1, source_target_pairs={{0,6},{1,7},{2,0},{3,1},{4,2},{5,3},{6,4},{7,5},{8,14},{9,15},{10,... | collective-permute-start | bytes 884744 | tf_op jit(solution)/shard_map/ppermute | solution.py:17
  101.0 18.5 %collective-permute-start.19 = (bf16[384,384]{1,0:T(8,128)(2,1)S(1)}, bf16[384,384]{1,0:T(8,128)(2,1)}, u32[]{:S(2)}, u32[]{:S(2)}) collective-permute-start(bf16[384,384]{1,0:T(8,128)(2,1)S(1)} %get-tuple-element.8), channel_id=1, source_target_pairs={{0,5},{1,6},{2,7},{3,0},{4,1},{5,2},{6,3},{7,4},{8,13},{9,14},{10,... | collective-permute-start | bytes 884744 | tf_op jit(solution)/shard_map/ppermute | solution.py:17
  102.7 16.9 %collective-permute-start.18 = (bf16[384,384]{1,0:T(8,128)(2,1)S(1)}, bf16[384,384]{1,0:T(8,128)(2,1)}, u32[]{:S(2)}, u32[]{:S(2)}) collective-permute-start(bf16[384,384]{1,0:T(8,128)(2,1)S(1)} %get-tuple-element.9), channel_id=1, source_target_pairs={{0,4},{1,5},{2,6},{3,7},{4,0},{5,1},{6,2},{7,3},{8,12},{9,13},{10,... | collective-permute-start | bytes 884744 | tf_op jit(solution)/shard_map/ppermute | solution.py:17
  114.5 13.5 %collective-permute-start.17 = (bf16[384,384]{1,0:T(8,128)(2,1)S(1)}, bf16[384,384]{1,0:T(8,128)(2,1)}, u32[]{:S(2)}, u32[]{:S(2)}) collective-permute-start(bf16[384,384]{1,0:T(8,128)(2,1)S(1)} %get-tuple-element.10), channel_id=1, source_target_pairs={{0,3},{1,4},{2,5},{3,6},{4,7},{5,0},{6,1},{7,2},{8,11},{9,12},{10,... | collective-permute-start | bytes 884744 | tf_op jit(solution)/shard_map/ppermute | solution.py:17
  116.0 15.8 %collective-permute-start.16 = (bf16[384,384]{1,0:T(8,128)(2,1)S(1)}, bf16[384,384]{1,0:T(8,128)(2,1)}, u32[]{:S(2)}, u32[]{:S(2)}) collective-permute-start(bf16[384,384]{1,0:T(8,128)(2,1)S(1)} %get-tuple-element.11), channel_id=1, source_target_pairs={{0,2},{1,3},{2,4},{3,5},{4,6},{5,7},{6,0},{7,1},{8,10},{9,11},{10,... | collective-permute-start | bytes 884744 | tf_op jit(solution)/shard_map/ppermute | solution.py:17
  (11 other events, 104.8 us)

commit v4 on v3

--- a/solution.py
+++ b/solution.py
@@ -154,12 +154,8 @@
         w_out.reshape(w_out.shape[0], mp_count, out_cols),
         preferred_element_type=jnp.float32,
     ).astype(jnp.bfloat16)
-    total = lax.dynamic_index_in_dim(terms, mp_here, 0, keepdims=False).astype(jnp.float32)
-    for step in range(1, mp_count):
-        target = (mp_here + step) % mp_count
-        term = lax.dynamic_index_in_dim(terms, target, 0, keepdims=False)
-        total = total + passed_along(term, "mp", step).astype(jnp.float32)
-    return total.astype(jnp.bfloat16)
+    received = lax.all_to_all(terms, "mp", 0, 0, tiled=True).astype(jnp.float32)
+    return jnp.sum(received, axis=0).astype(jnp.bfloat16)
 
 
 def solution(mesh):

time: 134 us -> 130 us (0.970); the launches traced: 134 us -> 128 us
  blocking collectives: 0 us -> 35.6 us
  waiting for transfers between devices: 61.6 us -> 35.6 us
  starting transfers between devices: 37.6 us -> 27.8 us
  local copies, waits for them, and re-layouts: 5.6 us -> 3.32 us
  Pallas kernels: 10.6 us -> 8.65 us
  other arithmetic: 5.14 us -> 3.64 us
    all_to_all x0 -> x1, blocking collectives: none -> 35.6 us  [on_device(): received = lax.all_to_all(terms, 'mp', 0, 0, tiled=True).astype(jnp.float32)]
    ppermute x18 -> x11, waiting for transfers between devices: 61.5 us -> 35.4 us  [passed_along(): return lax.ppermute(value, axis, pairs)]
    ppermute x18 -> x11, starting transfers between devices: 37.6 us -> 27.7 us  [passed_along(): return lax.ppermute(value, axis, pairs)]
    convert_element_type x1 -> x0, other arithmetic: 2.52 us -> none  [on_device(): return total.astype(jnp.bfloat16)]
    pallas_call x1, Pallas kernels: 10.6 us -> 8.65 us  [attend(): pl.pallas_call(attend_kernel, grid_spec=pltpu.PrefetchScalarGridSpec(num_...]
  transfers between devices with their start and end apart: 22 -> 15, of which waited for: 11 -> 6; matrix products, arithmetic and copies ran while one was open for 9% -> 10% of each run, Pallas kernels for 0% -> 0%
where the time goes in v4:
time: 130 us; the launch traced here: 128 us
  waiting for transfers between devices  35.6 us (27%)
  blocking collectives  35.6 us (27%)
  starting transfers between devices  27.8 us (21%)
  matrix products  13.4 us (10%)
  Pallas kernels  8.65 us (7%)
  other arithmetic  3.64 us (3%)
  local copies, waits for them, and re-layouts  3.32 us (3%)
    all_to_all x1, blocking collectives, on_device(): received = lax.all_to_all(terms, 'mp', 0, 0, tiled=True).astype(jnp.float32)  35.6 us
    ppermute x11, waiting for transfers between devices, passed_along(): return lax.ppermute(value, axis, pairs)  35.4 us
    ppermute x11, starting transfers between devices, passed_along(): return lax.ppermute(value, axis, pairs)  27.7 us
    pallas_call x1, Pallas kernels, attend(): pl.pallas_call(attend_kernel, grid_spec=pltpu.PrefetchScalarGridSpec(num_...  8.65 us
    dot_general x7, matrix products, on_device(): jnp.einsum('tf,fjc->jtc', passed_along(tokens, 'mp', step), rows_of(sourc...  8.34 us
    dot_general x1, matrix products, on_device(): jnp.einsum('tk,kjc->jtc', attended, w_out.reshape(w_out.shape[0], mp_coun...  3.16 us
  transfers between devices with their start and end apart: 15, of which 6 were waited for; matrix products, arithmetic and copies ran while one was open for 10% of the time, Pallas kernels for 0%

profile of v4, /device:TPU:8, one launch (start us, length us, event | category | flops | bytes accessed | tf_op | source)
XLA Modules:
  0.0 128.4 jit_solution(14085450666049724394)
XLA Ops:
  0.0 4.8 %collective-permute-start.5 = (bf16[384,384]{1,0:T(8,128)(2,1)}, bf16[384,384]{1,0:T(8,128)(2,1)S(1)}, u32[]{:S(2)}, u32[]{:S(2)}) collective-permute-start(bf16[384,384]{1,0:T(8,128)(2,1)} %param.7), channel_id=1, source_target_pairs={{0,6},{1,7},{2,0},{3,1},{4,2},{5,3},{6,4},{7,5},{8,14},{9,15},{10,... | collective-permute-start | bytes 884744 | tf_op jit(solution)/shard_map/ppermute | solution.py:17
  4.8 1.3 collective-permute-start.4
  6.0 2.3 %collective-permute-start.3 = (bf16[384,384]{1,0:T(8,128)(2,1)}, bf16[384,384]{1,0:T(8,128)(2,1)S(1)}, u32[]{:S(2)}, u32[]{:S(2)}) collective-permute-start(bf16[384,384]{1,0:T(8,128)(2,1)} %param.7), channel_id=1, source_target_pairs={{0,4},{1,5},{2,6},{3,7},{4,0},{5,1},{6,2},{7,3},{8,12},{9,13},{10,... | collective-permute-start | bytes 884744 | tf_op jit(solution)/shard_map/ppermute | solution.py:17
  8.3 0.9 collective-permute-start.2
  9.2 1.8 %collective-permute-start = (bf16[384,384]{1,0:T(8,128)(2,1)}, bf16[384,384]{1,0:T(8,128)(2,1)S(1)}, u32[]{:S(2)}, u32[]{:S(2)}) collective-permute-start(bf16[384,384]{1,0:T(8,128)(2,1)} %param.7), channel_id=1, source_target_pairs={{0,1},{1,2},{2,3},{3,4},{4,5},{5,6},{6,7},{7,0},{8,9},{9,10},{10,1... | collective-permute-start | bytes 884744 | tf_op jit(solution)/shard_map/ppermute | solution.py:17
  11.0 1.9 %fusion.21 = f32[3,384,384]{1,2,0:T(8,128)S(1)} fusion(bf16[3072,3,384]{2,0,1:T(8,128)(2,1)} %param.8, s32[]{:T(128)S(6)} %select_n.101, bf16[384,384]{1,0:T(8,128)(2,1)} %param.7), kind=kOutput, calls=%fused_computation.19 | convolution fusion | flops 339738624 | bytes 2949124 | tf_op jit(solution)/shard_map/tf,fjc->jtc/dot_general | solution.py:101
  13.1 6.4 %collective-permute-start.1 = (bf16[384,384]{1,0:T(8,128)(2,1)S(1)}, bf16[384,384]{1,0:T(8,128)(2,1)S(1)}, u32[]{:S(2)}, u32[]{:S(2)}) collective-permute-start(bf16[384,384]{1,0:T(8,128)(2,1)S(1)} %copy-done.8), channel_id=1, source_target_pairs={{0,2},{1,3},{2,4},{3,5},{4,6},{5,7},{6,0},{7,1},{8,10},{9,11},{10,... | collective-permute-start | bytes 884744 | tf_op jit(solution)/shard_map/ppermute | solution.py:17
  19.5 2.0 %fusion.9 = f32[3,384,384]{1,2,0:T(8,128)S(1)} fusion(bf16[3072,3,384]{2,0,1:T(8,128)(2,1)} %param.8, s32[]{:T(128)S(6)} %select_n.113, bf16[384,384]{1,0:T(8,128)(2,1)S(1)} %collective-permute-done.5), kind=kOutput, calls=%fused_computation.7 | convolution fusion | flops 339738624 | bytes 2949124 | tf_op jit(solution)/shard_map/tf,fjc->jtc/dot_general | solution.py:106
  21.5 7.7 %collective-permute-done = bf16[384,384]{1,0:T(8,128)(2,1)S(1)} collective-permute-done((bf16[384,384]{1,0:T(8,128)(2,1)}, bf16[384,384]{1,0:T(8,128)(2,1)S(1)}, u32[]{:S(2)}, u32[]{:S(2)}) %collective-permute-start) | collective-permute-done | bytes 294944 | tf_op jit(solution)/shard_map/ppermute | solution.py:17
  29.4 1.8 %fusion.19 = f32[3,384,384]{1,2,0:T(8,128)S(1)} fusion(bf16[3072,3,384]{2,0,1:T(8,128)(2,1)} %param.8, s32[]{:T(128)S(6)} %select_n.103, bf16[384,384]{1,0:T(8,128)(2,1)S(1)} %collective-permute-done), kind=kOutput, calls=%fused_computation.17 | convolution fusion | flops 339738624 | bytes 2949124 | tf_op jit(solution)/shard_map/tf,fjc->jtc/dot_general | solution.py:106
  31.3 3.1 %collective-permute-done.1 = bf16[384,384]{1,0:T(8,128)(2,1)S(1)} collective-permute-done((bf16[384,384]{1,0:T(8,128)(2,1)S(1)}, bf16[384,384]{1,0:T(8,128)(2,1)S(1)}, u32[]{:S(2)}, u32[]{:S(2)}) %collective-permute-start.1) | collective-permute-done | bytes 294944 | tf_op jit(solution)/shard_map/ppermute | solution.py:17
  34.3 1.8 %fusion.17 = f32[3,384,384]{1,2,0:T(8,128)S(1)} fusion(bf16[3072,3,384]{2,0,1:T(8,128)(2,1)} %param.8, s32[]{:T(128)S(6)} %select_n.105, bf16[384,384]{1,0:T(8,128)(2,1)S(1)} %collective-permute-done.1), kind=kOutput, calls=%fused_computation.15 | convolution fusion | flops 339738624 | bytes 2949124 | tf_op jit(solution)/shard_map/tf,fjc->jtc/dot_general | solution.py:106
  39.0 0.9 fusion.42
  41.2 1.0 collective-permute-start.9
  42.3 2.0 %collective-permute-start.8 = (bf16[2,3,384,128]{3,2,1,0:T(8,128)(2,1)S(1)}, bf16[2,3,384,128]{3,2,1,0:T(8,128)(2,1)S(1)}, u32[]{:S(2)}, u32[]{:S(2)}) collective-permute-start(bf16[2,3,384,128]{3,2,1,0:T(8,128)(2,1)S(1)} %pad_maximum_fusion.rest_0_), channel_id=1, source_target_pairs={{0,16},{8,24},{16,32},{24,40},{32,48},{40,56},{48,64},{56,72},{64,... | collective-permute-start | bytes 1769480 | tf_op jit(solution)/shard_map/ppermute | solution.py:17
  44.2 7.1 %collective-permute-start.10 = (bf16[2,3,384,128]{3,2,1,0:T(8,128)(2,1)S(1)}, bf16[2,3,384,128]{3,2,1,0:T(8,128)(2,1)S(1)}, u32[]{:S(2)}, u32[]{:S(2)}) collective-permute-start(bf16[2,3,384,128]{3,2,1,0:T(8,128)(2,1)S(1)} %pad_maximum_fusion.rest_0_), channel_id=1, source_target_pairs={{0,224},{8,232},{16,240},{24,248},{32,0},{40,8},{48,16},{56,24},{6... | collective-permute-start | bytes 1769480 | tf_op jit(solution)/shard_map/ppermute | solution.py:17
  51.3 15.4 %collective-permute-done.9.rest_3_ = bf16[2,3,384,128]{3,2,1,0:T(8,128)(2,1)S(1)} collective-permute-done((bf16[2,3,384,128]{3,2,1,0:T(8,128)(2,1)S(1)}, bf16[2,3,384,128]{3,2,1,0:T(8,128)(2,1)S(1)}, u32[]{:S(2)}, u32[]{:S(2)}) %collective-permute-start.9) | collective-permute-done | bytes 589856 | tf_op jit(solution)/shard_map/ppermute | solution.py:17
  66.7 2.4 %collective-permute-done.8.rest_2_ = bf16[2,3,384,128]{3,2,1,0:T(8,128)(2,1)S(1)} collective-permute-done((bf16[2,3,384,128]{3,2,1,0:T(8,128)(2,1)S(1)}, bf16[2,3,384,128]{3,2,1,0:T(8,128)(2,1)S(1)}, u32[]{:S(2)}, u32[]{:S(2)}) %collective-permute-start.8) | collective-permute-done | bytes 589856 | tf_op jit(solution)/shard_map/ppermute | solution.py:17
  69.1 6.8 %collective-permute-done.7.rest_1_ = bf16[2,3,384,128]{3,2,1,0:T(8,128)(2,1)S(1)} collective-permute-done((bf16[2,3,384,128]{3,2,1,0:T(8,128)(2,1)S(1)}, bf16[2,3,384,128]{3,2,1,0:T(8,128)(2,1)S(1)}, u32[]{:S(2)}, u32[]{:S(2)}) %collective-permute-start.7) | collective-permute-done | bytes 589856 | tf_op jit(solution)/shard_map/ppermute | solution.py:17
  76.0 0.9 broadcast_select_fusion
  79.9 8.7 %shard_map.73 = bf16[384,384]{1,0:T(8,128)(2,1)} custom-call(s32[9]{0:T(128)} %convert_element_type.19.mask_ref, f32[384,384]{1,0:T(8,128)} %get-tuple-element.6.q_ref, f32[1,128]{1,0:T(1,128)} %bitcast.58, bf16[2,3,384,128]{3,2,1,0:T(8,128)(2,1)} %copy-done.2, bf16[2,3,384,128]{3,2,1,0:T(8,128)(2,1)} %copy-done.4, bf16[2,3,384,128]{3,2,1,0:T(8,128)(2,1)} %copy-done.6, ...), custom_call_target="tpu_custom_call" | custom-call | tf_op jit(solution)/shard_map/pallas_call | solution.py:67
  88.5 3.2 %convert_bitcast_fusion = bf16[8,384,384]{2,1,0:T(8,128)(2,1)S(1)} fusion(bf16[48,8,8,384]{3,2,1,0:T(8,128)(2,1)} %bitcast.59, bf16[384,384]{1,0:T(8,128)(2,1)} %shard_map.73), kind=kOutput, calls=%fused_computation.3 | convolution fusion | flops 907149312 | bytes 5013504 | tf_op jit(solution)/shard_map/tk,kjc->jtc/dot_general | solution.py:151
  91.7 35.6 %all_to_all.5 = bf16[8,384,384]{2,1,0:T(8,128)(2,1)S(1)} all-to-all(bf16[8,384,384]{2,1,0:T(8,128)(2,1)S(1)} %convert_bitcast_fusion), channel_id=1, replica_groups=mesh['seq'=32,'mp'=8] {'mp'}, dimensions={0} | all-to-all | bytes 4718592 | tf_op jit(solution)/shard_map/all_to_all | solution.py:157
  127.3 1.1 reduce_sum.22
  (58 shorter events, 7.3 us)
Async XLA Ops:
  0.0 77.5 %copy-start = (s32[32,6]{0,1:T(8,128)S(1)}, s32[32,6]{0,1:T(8,128)}, u32[]{:S(2)}) copy-start(s32[32,6]{0,1:T(8,128)} %param.12) | copy-start | bytes 2308
  0.0 13.1 %copy-start.8 = (bf16[384,384]{1,0:T(8,128)(2,1)S(1)}, bf16[384,384]{1,0:T(8,128)(2,1)}, u32[]{:S(2)}) copy-start(bf16[384,384]{1,0:T(8,128)(2,1)} %param.7) | copy-start | bytes 884740
  0.0 13.1 %collective-permute-start.5 = (bf16[384,384]{1,0:T(8,128)(2,1)}, bf16[384,384]{1,0:T(8,128)(2,1)S(1)}, u32[]{:S(2)}, u32[]{:S(2)}) collective-permute-start(bf16[384,384]{1,0:T(8,128)(2,1)} %param.7), channel_id=1, source_target_pairs={{0,6},{1,7},{2,0},{3,1},{4,2},{5,3},{6,4},{7,5},{8,14},{9,15},{10,... | collective-permute-start | bytes 884744 | tf_op jit(solution)/shard_map/ppermute | solution.py:17
  4.8 32.7 %collective-permute-start.4 = (bf16[384,384]{1,0:T(8,128)(2,1)}, bf16[384,384]{1,0:T(8,128)(2,1)S(1)}, u32[]{:S(2)}, u32[]{:S(2)}) collective-permute-start(bf16[384,384]{1,0:T(8,128)(2,1)} %param.7), channel_id=1, source_target_pairs={{0,5},{1,6},{2,7},{3,0},{4,1},{5,2},{6,3},{7,4},{8,13},{9,14},{10,... | collective-permute-start | bytes 884744 | tf_op jit(solution)/shard_map/ppermute | solution.py:17
  6.0 30.8 %collective-permute-start.3 = (bf16[384,384]{1,0:T(8,128)(2,1)}, bf16[384,384]{1,0:T(8,128)(2,1)S(1)}, u32[]{:S(2)}, u32[]{:S(2)}) collective-permute-start(bf16[384,384]{1,0:T(8,128)(2,1)} %param.7), channel_id=1, source_target_pairs={{0,4},{1,5},{2,6},{3,7},{4,0},{5,1},{6,2},{7,3},{8,12},{9,13},{10,... | collective-permute-start | bytes 884744 | tf_op jit(solution)/shard_map/ppermute | solution.py:17
  8.3 27.8 %collective-permute-start.2 = (bf16[384,384]{1,0:T(8,128)(2,1)}, bf16[384,384]{1,0:T(8,128)(2,1)S(1)}, u32[]{:S(2)}, u32[]{:S(2)}) collective-permute-start(bf16[384,384]{1,0:T(8,128)(2,1)} %param.7), channel_id=1, source_target_pairs={{0,3},{1,4},{2,5},{3,6},{4,7},{5,0},{6,1},{7,2},{8,11},{9,12},{10,... | collective-permute-start | bytes 884744 | tf_op jit(solution)/shard_map/ppermute | solution.py:17
  9.2 20.0 %collective-permute-start = (bf16[384,384]{1,0:T(8,128)(2,1)}, bf16[384,384]{1,0:T(8,128)(2,1)S(1)}, u32[]{:S(2)}, u32[]{:S(2)}) collective-permute-start(bf16[384,384]{1,0:T(8,128)(2,1)} %param.7), channel_id=1, source_target_pairs={{0,1},{1,2},{2,3},{3,4},{4,5},{5,6},{6,7},{7,0},{8,9},{9,10},{10,1... | collective-permute-start | bytes 884744 | tf_op jit(solution)/shard_map/ppermute | solution.py:17
  13.1 21.2 %collective-permute-start.1 = (bf16[384,384]{1,0:T(8,128)(2,1)S(1)}, bf16[384,384]{1,0:T(8,128)(2,1)S(1)}, u32[]{:S(2)}, u32[]{:S(2)}) collective-permute-start(bf16[384,384]{1,0:T(8,128)(2,1)S(1)} %copy-done.8), channel_id=1, source_target_pairs={{0,2},{1,3},{2,4},{3,5},{4,6},{5,7},{6,0},{7,1},{8,10},{9,11},{10,... | collective-permute-start | bytes 884744 | tf_op jit(solution)/shard_map/ppermute | solution.py:17
  19.5 16.6 %copy-start.1 = (bf16[3072,3,384]{2,0,1:T(8,128)(2,1)S(1)}, bf16[3072,3,384]{2,0,1:T(8,128)(2,1)}, u32[]{:S(2)}) copy-start(bf16[3072,3,384]{2,0,1:T(8,128)(2,1)} %param.8) | copy-start | bytes 21233668
  29.2 8.9 %collective-permute-start.6 = (bf16[384,384]{1,0:T(8,128)(2,1)S(1)}, bf16[384,384]{1,0:T(8,128)(2,1)S(1)}, u32[]{:S(2)}, u32[]{:S(2)}) collective-permute-start(bf16[384,384]{1,0:T(8,128)(2,1)S(1)} %copy-done.8), channel_id=1, source_target_pairs={{0,7},{1,0},{2,1},{3,2},{4,3},{5,4},{6,5},{7,6},{8,15},{9,8},{10,9... | collective-permute-start | bytes 884744 | tf_op jit(solution)/shard_map/ppermute | solution.py:17
  40.9 36.0 %copy-start.10 = (s32[32]{0:T(128)S(1)}, s32[32]{0:T(128)}, u32[]{:S(2)}) copy-start(s32[32]{0:T(128)} %param.13) | copy-start | bytes 388
  41.2 38.0 %copy-start.2 = (bf16[2,3,384,128]{3,2,1,0:T(8,128)(2,1)}, bf16[2,3,384,128]{3,2,1,0:T(8,128)(2,1)S(1)}, u32[]{:S(2)}) copy-start(bf16[2,3,384,128]{3,2,1,0:T(8,128)(2,1)S(1)} %pad_maximum_fusion.rest_0_) | copy-start | bytes 1769476
  41.2 25.4 %collective-permute-start.9 = (bf16[2,3,384,128]{3,2,1,0:T(8,128)(2,1)S(1)}, bf16[2,3,384,128]{3,2,1,0:T(8,128)(2,1)S(1)}, u32[]{:S(2)}, u32[]{:S(2)}) collective-permute-start(bf16[2,3,384,128]{3,2,1,0:T(8,128)(2,1)S(1)} %pad_maximum_fusion.rest_0_), channel_id=1, source_target_pairs={{0,240},{8,248},{16,0},{24,8},{32,16},{40,24},{48,32},{56,40},{64,... | collective-permute-start | bytes 1769480 | tf_op jit(solution)/shard_map/ppermute | solution.py:17
  42.3 26.9 %collective-permute-start.8 = (bf16[2,3,384,128]{3,2,1,0:T(8,128)(2,1)S(1)}, bf16[2,3,384,128]{3,2,1,0:T(8,128)(2,1)S(1)}, u32[]{:S(2)}, u32[]{:S(2)}) collective-permute-start(bf16[2,3,384,128]{3,2,1,0:T(8,128)(2,1)S(1)} %pad_maximum_fusion.rest_0_), channel_id=1, source_target_pairs={{0,16},{8,24},{16,32},{24,40},{32,48},{40,56},{48,64},{56,72},{64,... | collective-permute-start | bytes 1769480 | tf_op jit(solution)/shard_map/ppermute | solution.py:17
  44.2 24.9 %collective-permute-start.10 = (bf16[2,3,384,128]{3,2,1,0:T(8,128)(2,1)S(1)}, bf16[2,3,384,128]{3,2,1,0:T(8,128)(2,1)S(1)}, u32[]{:S(2)}, u32[]{:S(2)}) collective-permute-start(bf16[2,3,384,128]{3,2,1,0:T(8,128)(2,1)S(1)} %pad_maximum_fusion.rest_0_), channel_id=1, source_target_pairs={{0,224},{8,232},{16,240},{24,248},{32,0},{40,8},{48,16},{56,24},{6... | collective-permute-start | bytes 1769480 | tf_op jit(solution)/shard_map/ppermute | solution.py:17
  51.3 24.6 %collective-permute-start.7 = (bf16[2,3,384,128]{3,2,1,0:T(8,128)(2,1)S(1)}, bf16[2,3,384,128]{3,2,1,0:T(8,128)(2,1)S(1)}, u32[]{:S(2)}, u32[]{:S(2)}) collective-permute-start(bf16[2,3,384,128]{3,2,1,0:T(8,128)(2,1)S(1)} %pad_maximum_fusion.rest_0_), channel_id=1, source_target_pairs={{0,32},{8,40},{16,48},{24,56},{32,64},{40,72},{48,80},{56,88},{64,... | collective-permute-start | bytes 1769480 | tf_op jit(solution)/shard_map/ppermute | solution.py:17
  51.3 27.7 %collective-permute-start.11 = (bf16[2,3,384,128]{3,2,1,0:T(8,128)(2,1)S(1)}, bf16[2,3,384,128]{3,2,1,0:T(8,128)(2,1)S(1)}, u32[]{:S(2)}, u32[]{:S(2)}) collective-permute-start(bf16[2,3,384,128]{3,2,1,0:T(8,128)(2,1)S(1)} %pad_maximum_fusion.rest_0_), channel_id=1, source_target_pairs={{0,8},{8,0},{16,24},{24,16},{32,40},{40,32},{48,56},{56,48},{64,72... | collective-permute-start | bytes 1769480 | tf_op jit(solution)/shard_map/ppermute | solution.py:123
  66.7 12.6 %copy-start.5 = (bf16[2,3,384,128]{3,2,1,0:T(8,128)(2,1)}, bf16[2,3,384,128]{3,2,1,0:T(8,128)(2,1)S(1)}, u32[]{:S(2)}) copy-start(bf16[2,3,384,128]{3,2,1,0:T(8,128)(2,1)S(1)} %collective-permute-done.9.rest_3_) | copy-start | bytes 1769476
  66.7 12.4 %collective-permute-start.13 = (bf16[2,3,384,128]{3,2,1,0:T(8,128)(2,1)S(1)}, bf16[2,3,384,128]{3,2,1,0:T(8,128)(2,1)}, u32[]{:S(2)}, u32[]{:S(2)}) collective-permute-start(bf16[2,3,384,128]{3,2,1,0:T(8,128)(2,1)S(1)} %collective-permute-done.9.rest_3_), channel_id=1, source_target_pairs={{0,8},{8,0},{16,24},{24,16},{32,40},{40,32},{48,56},{56,48},{64,72... | collective-permute-start | bytes 1769480 | tf_op jit(solution)/shard_map/ppermute | solution.py:125
  69.1 10.1 %copy-start.6 = (bf16[2,3,384,128]{3,2,1,0:T(8,128)(2,1)}, bf16[2,3,384,128]{3,2,1,0:T(8,128)(2,1)S(1)}, u32[]{:S(2)}) copy-start(bf16[2,3,384,128]{3,2,1,0:T(8,128)(2,1)S(1)} %collective-permute-done.8.rest_2_) | copy-start | bytes 1769476
  69.1 9.9 %collective-permute-start.12 = (bf16[2,3,384,128]{3,2,1,0:T(8,128)(2,1)S(1)}, bf16[2,3,384,128]{3,2,1,0:T(8,128)(2,1)}, u32[]{:S(2)}, u32[]{:S(2)}) collective-permute-start(bf16[2,3,384,128]{3,2,1,0:T(8,128)(2,1)S(1)} %collective-permute-done.8.rest_2_), channel_id=1, source_target_pairs={{0,8},{8,0},{16,24},{24,16},{32,40},{40,32},{48,56},{56,48},{64,72... | collective-permute-start | bytes 1769480 | tf_op jit(solution)/shard_map/ppermute | solution.py:124
  69.1 10.1 %copy-start.3 = (bf16[2,3,384,128]{3,2,1,0:T(8,128)(2,1)}, bf16[2,3,384,128]{3,2,1,0:T(8,128)(2,1)S(1)}, u32[]{:S(2)}) copy-start(bf16[2,3,384,128]{3,2,1,0:T(8,128)(2,1)S(1)} %collective-permute-done.10.rest_4_) | copy-start | bytes 1769476
  76.0 3.3 %copy-start.4 = (bf16[2,3,384,128]{3,2,1,0:T(8,128)(2,1)}, bf16[2,3,384,128]{3,2,1,0:T(8,128)(2,1)S(1)}, u32[]{:S(2)}) copy-start(bf16[2,3,384,128]{3,2,1,0:T(8,128)(2,1)S(1)} %collective-permute-done.7.rest_1_) | copy-start | bytes 1769476
  76.9 2.3 %collective-permute-start.14 = (bf16[2,3,384,128]{3,2,1,0:T(8,128)(2,1)}, bf16[2,3,384,128]{3,2,1,0:T(8,128)(2,1)}, u32[]{:S(2)}, u32[]{:S(2)}) collective-permute-start(bf16[2,3,384,128]{3,2,1,0:T(8,128)(2,1)} %broadcast_select_fusion), channel_id=1, source_target_pairs={{0,8},{8,0},{16,24},{24,16},{32,40},{40,32},{48,56},{56,48},{64,72... | collective-permute-start | bytes 1769480 | tf_op jit(solution)/shard_map/ppermute | solution.py:126
  (2 other events, 1.6 us)

commit v5 on v4

--- a/solution.py
+++ b/solution.py
@@ -95,20 +95,14 @@
     mp_count = lax.axis_size("mp")
     mp_here = lax.axis_index("mp")
 
-    def rows_of(block):
-        return lax.dynamic_slice_in_dim(w_qkv, block * feats, feats, 0)
-
+    spread = jnp.broadcast_to(tokens[None], (mp_count,) + tokens.shape)
+    gathered = lax.all_to_all(spread, "mp", 0, 0, tiled=True)
     projected = jnp.einsum(
-        "tf,fjc->jtc", tokens, rows_of(mp_here), preferred_element_type=jnp.float32
+        "itf,ifjc->jtc",
+        gathered,
+        w_qkv.reshape(mp_count, feats, 3, columns),
+        preferred_element_type=jnp.float32,
     )
-    for step in range(1, mp_count):
-        source = (mp_here - step) % mp_count
-        projected = projected + jnp.einsum(
-            "tf,fjc->jtc",
-            passed_along(tokens, "mp", step),
-            rows_of(source),
-            preferred_element_type=jnp.float32,
-        )
     key_part = head_norm(projected[1], k_gain).transpose(1, 0, 2)
     value_part = projected[2].astype(jnp.bfloat16).reshape(tok_rows, heads_here, HD).transpose(1, 0, 2)
     paired = jnp.stack([key_part, value_part])

time: 130 us -> 131 us (level)
  the two profiles are of different devices: /device:TPU:8 before, /device:TPU:64 now
where the time goes in v5:
time: 131 us; the launch traced here: 132 us
  blocking collectives  72.9 us (56%)
  waiting for transfers between devices  24.9 us (19%)
  Pallas kernels  14.5 us (11%)
  matrix products  6.35 us (5%)
  starting transfers between devices  5.04 us (4%)
  local copies, waits for them, and re-layouts  4.92 us (4%)
  other arithmetic  3.76 us (3%)
    all_to_all x1, blocking collectives, on_device(): gathered = lax.all_to_all(spread, 'mp', 0, 0, tiled=True)  38.2 us
    all_to_all x1, blocking collectives, on_device(): received = lax.all_to_all(terms, 'mp', 0, 0, tiled=True).astype(jnp.float32)  34.6 us
    ppermute x4, waiting for transfers between devices, passed_along(): return lax.ppermute(value, axis, pairs)  24.9 us
    pallas_call x1, Pallas kernels, attend(): pl.pallas_call(attend_kernel, grid_spec=pltpu.PrefetchScalarGridSpec(num_...  14.5 us
    ppermute x4, starting transfers between devices, passed_along(): return lax.ppermute(value, axis, pairs)  5.03 us
    dot_general x1, matrix products, on_device(): jnp.einsum('itf,ifjc->jtc', gathered, w_qkv.reshape(mp_count, feats, 3, c...  3.19 us
    dot_general x1, matrix products, on_device(): jnp.einsum('tk,kjc->jtc', attended, w_out.reshape(w_out.shape[0], mp_coun...  3.16 us
  transfers between devices with their start and end apart: 8, of which 4 were waited for; matrix products, arithmetic and copies ran while one was open for 3% of the time, Pallas kernels for 0%

profile of v5, /device:TPU:64, one launch (start us, length us, event | category | flops | bytes accessed | tf_op | source)
XLA Modules:
  0.0 132.5 jit_solution(16468021308955150080)
XLA Ops:
  0.0 1.3 broadcast_in_dim.2
  1.3 38.2 %all_to_all.10 = bf16[8,384,384]{2,1,0:T(8,128)(2,1)S(1)} all-to-all(bf16[8,384,384]{2,1,0:T(8,128)(2,1)S(1)} %broadcast_in_dim.2), channel_id=1, replica_groups=mesh['seq'=32,'mp'=8] {'mp'}, dimensions={0} | all-to-all | bytes 4718592 | tf_op jit(solution)/shard_map/all_to_all | solution.py:99
  39.6 3.2 %fusion.7 = f32[3,384,384]{2,1,0:T(8,128)S(1)} fusion(bf16[8,384,3,384]{3,1,0,2:T(8,128)(2,1)S(1)} %bitcast.44, bf16[8,384,384]{2,1,0:T(8,128)(2,1)S(1)} %all_to_all.10), kind=kOutput, calls=%fused_computation.6 | convolution fusion | flops 2717908992 | bytes 11206656 | tf_op jit(solution)/shard_map/itf,ifjc->jtc/dot_general | solution.py:100
  42.8 0.9 fusion.13
  43.7 0.2 copy.20
  43.9 0.2 copy.21
  44.2 0.2 copy.22
  44.7 0.2 fusion.10
  45.0 2.0 %collective-permute-start = (bf16[2,3,384,128]{3,2,1,0:T(8,128)(2,1)S(1)}, bf16[2,3,384,128]{3,2,1,0:T(8,128)(2,1)S(1)}, u32[]{:S(2)}, u32[]{:S(2)}) collective-permute-start(bf16[2,3,384,128]{3,2,1,0:T(8,128)(2,1)S(1)} %pad_maximum_fusion.rest_0_), channel_id=1, source_target_pairs={{0,32},{8,40},{16,48},{24,56},{32,64},{40,72},{48,80},{56,88},{64,... | collective-permute-start | bytes 1769480 | tf_op jit(solution)/shard_map/ppermute | solution.py:17
  47.1 0.7 collective-permute-start.1
  47.8 2.2 %collective-permute-start.2 = (bf16[2,3,384,128]{3,2,1,0:T(8,128)(2,1)S(1)}, bf16[2,3,384,128]{3,2,1,0:T(8,128)(2,1)S(1)}, u32[]{:S(2)}, u32[]{:S(2)}) collective-permute-start(bf16[2,3,384,128]{3,2,1,0:T(8,128)(2,1)S(1)} %pad_maximum_fusion.rest_0_), channel_id=1, source_target_pairs={{0,240},{8,248},{16,0},{24,8},{32,16},{40,24},{48,32},{56,40},{64,... | collective-permute-start | bytes 1769480 | tf_op jit(solution)/shard_map/ppermute | solution.py:17
  50.0 9.0 %collective-permute-done.rest_1_ = bf16[2,3,384,128]{3,2,1,0:T(8,128)(2,1)S(1)} collective-permute-done((bf16[2,3,384,128]{3,2,1,0:T(8,128)(2,1)S(1)}, bf16[2,3,384,128]{3,2,1,0:T(8,128)(2,1)S(1)}, u32[]{:S(2)}, u32[]{:S(2)}) %collective-permute-start) | collective-permute-done | bytes 589856 | tf_op jit(solution)/shard_map/ppermute | solution.py:17
  59.1 5.2 %collective-permute-done.3.rest_4_ = bf16[2,3,384,128]{3,2,1,0:T(8,128)(2,1)S(1)} collective-permute-done((bf16[2,3,384,128]{3,2,1,0:T(8,128)(2,1)S(1)}, bf16[2,3,384,128]{3,2,1,0:T(8,128)(2,1)S(1)}, u32[]{:S(2)}, u32[]{:S(2)}) %collective-permute-start.3) | collective-permute-done | bytes 589856 | tf_op jit(solution)/shard_map/ppermute | solution.py:17
  64.3 1.0 broadcast_select_fusion
  65.3 6.6 %collective-permute-done.1.rest_2_ = bf16[2,3,384,128]{3,2,1,0:T(8,128)(2,1)S(1)} collective-permute-done((bf16[2,3,384,128]{3,2,1,0:T(8,128)(2,1)S(1)}, bf16[2,3,384,128]{3,2,1,0:T(8,128)(2,1)S(1)}, u32[]{:S(2)}, u32[]{:S(2)}) %collective-permute-start.1) | collective-permute-done | bytes 589856 | tf_op jit(solution)/shard_map/ppermute | solution.py:17
  71.9 4.0 %collective-permute-done.2.rest_3_ = bf16[2,3,384,128]{3,2,1,0:T(8,128)(2,1)S(1)} collective-permute-done((bf16[2,3,384,128]{3,2,1,0:T(8,128)(2,1)S(1)}, bf16[2,3,384,128]{3,2,1,0:T(8,128)(2,1)S(1)}, u32[]{:S(2)}, u32[]{:S(2)}) %collective-permute-start.2) | collective-permute-done | bytes 589856 | tf_op jit(solution)/shard_map/ppermute | solution.py:17
  75.9 0.7 dynamic_slice.10
  77.0 0.7 iota_compare_fusion
  77.8 0.5 convert_element_type.19.mask_ref
  78.4 0.7 copy-done.6
  79.1 14.5 %shard_map.73 = bf16[384,384]{1,0:T(8,128)(2,1)} custom-call(s32[9]{0:T(128)} %convert_element_type.19.mask_ref, f32[384,384]{1,0:T(8,128)} %get-tuple-element.6.q_ref, f32[1,128]{1,0:T(1,128)} %bitcast.43, bf16[2,3,384,128]{3,2,1,0:T(8,128)(2,1)} %copy-done.1, bf16[2,3,384,128]{3,2,1,0:T(8,128)(2,1)} %copy-done.2, bf16[2,3,384,128]{3,2,1,0:T(8,128)(2,1)} %copy-done.4, ...), custom_call_target="tpu_custom_call" | custom-call | tf_op jit(solution)/shard_map/pallas_call | solution.py:67
  93.6 3.2 %convert_bitcast_fusion = bf16[8,384,384]{2,1,0:T(8,128)(2,1)S(1)} fusion(bf16[48,8,8,384]{3,2,1,0:T(8,128)(2,1)} %bitcast.45, bf16[384,384]{1,0:T(8,128)(2,1)} %shard_map.73), kind=kOutput, calls=%fused_computation.5 | convolution fusion | flops 907149312 | bytes 5013504 | tf_op jit(solution)/shard_map/tk,kjc->jtc/dot_general | solution.py:145
  96.7 34.6 %all_to_all.11 = bf16[8,384,384]{2,1,0:T(8,128)(2,1)S(1)} all-to-all(bf16[8,384,384]{2,1,0:T(8,128)(2,1)S(1)} %convert_bitcast_fusion), channel_id=1, replica_groups=mesh['seq'=32,'mp'=8] {'mp'}, dimensions={0} | all-to-all | bytes 4718592 | tf_op jit(solution)/shard_map/all_to_all | solution.py:151
  131.4 1.1 reduce_sum.22
  (37 shorter events, 0.9 us)
Async XLA Ops:
  0.0 76.7 %copy-start = (s32[32,6]{0,1:T(8,128)S(1)}, s32[32,6]{0,1:T(8,128)}, u32[]{:S(2)}) copy-start(s32[32,6]{0,1:T(8,128)} %param.12) | copy-start | bytes 2308
  0.0 39.6 %copy-start.8 = (bf16[3072,3,384]{2,0,1:T(8,128)(2,1)S(1)}, bf16[3072,3,384]{2,0,1:T(8,128)(2,1)}, u32[]{:S(2)}) copy-start(bf16[3072,3,384]{2,0,1:T(8,128)(2,1)} %param.8) | copy-start | bytes 21233668
  43.7 1.0 copy-start.7
  44.5 31.5 %copy-start.9 = (s32[32]{0:T(128)S(1)}, s32[32]{0:T(128)}, u32[]{:S(2)}) copy-start(s32[32]{0:T(128)} %param.13) | copy-start | bytes 388
  45.0 33.3 %copy-start.1 = (bf16[2,3,384,128]{3,2,1,0:T(8,128)(2,1)}, bf16[2,3,384,128]{3,2,1,0:T(8,128)(2,1)S(1)}, u32[]{:S(2)}) copy-start(bf16[2,3,384,128]{3,2,1,0:T(8,128)(2,1)S(1)} %pad_maximum_fusion.rest_0_) | copy-start | bytes 1769476
  45.0 14.1 %collective-permute-start = (bf16[2,3,384,128]{3,2,1,0:T(8,128)(2,1)S(1)}, bf16[2,3,384,128]{3,2,1,0:T(8,128)(2,1)S(1)}, u32[]{:S(2)}, u32[]{:S(2)}) collective-permute-start(bf16[2,3,384,128]{3,2,1,0:T(8,128)(2,1)S(1)} %pad_maximum_fusion.rest_0_), channel_id=1, source_target_pairs={{0,32},{8,40},{16,48},{24,56},{32,64},{40,72},{48,80},{56,88},{64,... | collective-permute-start | bytes 1769480 | tf_op jit(solution)/shard_map/ppermute | solution.py:17
  47.0 17.3 %collective-permute-start.3 = (bf16[2,3,384,128]{3,2,1,0:T(8,128)(2,1)S(1)}, bf16[2,3,384,128]{3,2,1,0:T(8,128)(2,1)S(1)}, u32[]{:S(2)}, u32[]{:S(2)}) collective-permute-start(bf16[2,3,384,128]{3,2,1,0:T(8,128)(2,1)S(1)} %pad_maximum_fusion.rest_0_), channel_id=1, source_target_pairs={{0,224},{8,232},{16,240},{24,248},{32,0},{40,8},{48,16},{56,24},{6... | collective-permute-start | bytes 1769480 | tf_op jit(solution)/shard_map/ppermute | solution.py:17
  47.1 24.8 %collective-permute-start.1 = (bf16[2,3,384,128]{3,2,1,0:T(8,128)(2,1)S(1)}, bf16[2,3,384,128]{3,2,1,0:T(8,128)(2,1)S(1)}, u32[]{:S(2)}, u32[]{:S(2)}) collective-permute-start(bf16[2,3,384,128]{3,2,1,0:T(8,128)(2,1)S(1)} %pad_maximum_fusion.rest_0_), channel_id=1, source_target_pairs={{0,16},{8,24},{16,32},{24,40},{32,48},{40,56},{48,64},{56,72},{64,... | collective-permute-start | bytes 1769480 | tf_op jit(solution)/shard_map/ppermute | solution.py:17
  47.8 28.1 %collective-permute-start.2 = (bf16[2,3,384,128]{3,2,1,0:T(8,128)(2,1)S(1)}, bf16[2,3,384,128]{3,2,1,0:T(8,128)(2,1)S(1)}, u32[]{:S(2)}, u32[]{:S(2)}) collective-permute-start(bf16[2,3,384,128]{3,2,1,0:T(8,128)(2,1)S(1)} %pad_maximum_fusion.rest_0_), channel_id=1, source_target_pairs={{0,240},{8,248},{16,0},{24,8},{32,16},{40,24},{48,32},{56,40},{64,... | collective-permute-start | bytes 1769480 | tf_op jit(solution)/shard_map/ppermute | solution.py:17
  50.0 28.3 %collective-permute-start.4 = (bf16[2,3,384,128]{3,2,1,0:T(8,128)(2,1)S(1)}, bf16[2,3,384,128]{3,2,1,0:T(8,128)(2,1)S(1)}, u32[]{:S(2)}, u32[]{:S(2)}) collective-permute-start(bf16[2,3,384,128]{3,2,1,0:T(8,128)(2,1)S(1)} %pad_maximum_fusion.rest_0_), channel_id=1, source_target_pairs={{0,8},{8,0},{16,24},{24,16},{32,40},{40,32},{48,56},{56,48},{64,72... | collective-permute-start | bytes 1769480 | tf_op jit(solution)/shard_map/ppermute | solution.py:117
  59.1 19.3 %copy-start.2 = (bf16[2,3,384,128]{3,2,1,0:T(8,128)(2,1)}, bf16[2,3,384,128]{3,2,1,0:T(8,128)(2,1)S(1)}, u32[]{:S(2)}) copy-start(bf16[2,3,384,128]{3,2,1,0:T(8,128)(2,1)S(1)} %collective-permute-done.rest_1_) | copy-start | bytes 1769476
  64.3 14.0 %copy-start.3 = (bf16[2,3,384,128]{3,2,1,0:T(8,128)(2,1)}, bf16[2,3,384,128]{3,2,1,0:T(8,128)(2,1)S(1)}, u32[]{:S(2)}) copy-start(bf16[2,3,384,128]{3,2,1,0:T(8,128)(2,1)S(1)} %collective-permute-done.3.rest_4_) | copy-start | bytes 1769476
  65.3 13.0 %collective-permute-start.7 = (bf16[2,3,384,128]{3,2,1,0:T(8,128)(2,1)}, bf16[2,3,384,128]{3,2,1,0:T(8,128)(2,1)}, u32[]{:S(2)}, u32[]{:S(2)}) collective-permute-start(bf16[2,3,384,128]{3,2,1,0:T(8,128)(2,1)} %broadcast_select_fusion), channel_id=1, source_target_pairs={{0,8},{8,0},{16,24},{24,16},{32,40},{40,32},{48,56},{56,48},{64,72... | collective-permute-start | bytes 1769480 | tf_op jit(solution)/shard_map/ppermute | solution.py:120
  71.9 6.4 %copy-start.4 = (bf16[2,3,384,128]{3,2,1,0:T(8,128)(2,1)}, bf16[2,3,384,128]{3,2,1,0:T(8,128)(2,1)S(1)}, u32[]{:S(2)}) copy-start(bf16[2,3,384,128]{3,2,1,0:T(8,128)(2,1)S(1)} %collective-permute-done.1.rest_2_) | copy-start | bytes 1769476
  71.9 6.4 %collective-permute-start.5 = (bf16[2,3,384,128]{3,2,1,0:T(8,128)(2,1)S(1)}, bf16[2,3,384,128]{3,2,1,0:T(8,128)(2,1)}, u32[]{:S(2)}, u32[]{:S(2)}) collective-permute-start(bf16[2,3,384,128]{3,2,1,0:T(8,128)(2,1)S(1)} %collective-permute-done.1.rest_2_), channel_id=1, source_target_pairs={{0,8},{8,0},{16,24},{24,16},{32,40},{40,32},{48,56},{56,48},{64,72... | collective-permute-start | bytes 1769480 | tf_op jit(solution)/shard_map/ppermute | solution.py:118
  75.9 2.4 %copy-start.5 = (bf16[2,3,384,128]{3,2,1,0:T(8,128)(2,1)}, bf16[2,3,384,128]{3,2,1,0:T(8,128)(2,1)S(1)}, u32[]{:S(2)}) copy-start(bf16[2,3,384,128]{3,2,1,0:T(8,128)(2,1)S(1)} %collective-permute-done.2.rest_3_) | copy-start | bytes 1769476
  75.9 2.4 %collective-permute-start.6 = (bf16[2,3,384,128]{3,2,1,0:T(8,128)(2,1)S(1)}, bf16[2,3,384,128]{3,2,1,0:T(8,128)(2,1)}, u32[]{:S(2)}, u32[]{:S(2)}) collective-permute-start(bf16[2,3,384,128]{3,2,1,0:T(8,128)(2,1)S(1)} %collective-permute-done.2.rest_3_), channel_id=1, source_target_pairs={{0,8},{8,0},{16,24},{24,16},{32,40},{40,32},{48,56},{56,48},{64,72... | collective-permute-start | bytes 1769480 | tf_op jit(solution)/shard_map/ppermute | solution.py:119
  78.3 0.8 copy-start.6

commit v6 on v4

--- a/solution.py
+++ b/solution.py
@@ -24,36 +24,32 @@
 
 
 def attend_kernel(mask_ref, q_ref, gain_ref, *rest):
-    slots = len(rest) - 4
+    slots = len(rest) - 5
     kv_refs = rest[:slots]
     out_ref = rest[slots]
-    m_ref, l_ref, acc_ref = rest[slots + 1 :]
+    s_ref, m_ref, l_ref, acc_ref = rest[slots + 1 :]
     factor = HD ** (-0.5)
     q_raw = q_ref[...]
     norm = lax.rsqrt(jnp.mean(q_raw * q_raw, axis=-1, keepdims=True) + 1e-06)
     q = (q_raw * norm * gain_ref[...]).astype(jnp.bfloat16)
+    keys = s_ref.shape[2]
     m_ref[...] = jnp.full(m_ref.shape, -jnp.inf, jnp.float32)
     l_ref[...] = jnp.zeros(l_ref.shape, jnp.float32)
     acc_ref[...] = jnp.zeros(acc_ref.shape, jnp.float32)
-
-    def scores_of(i):
-        return lax.dot_general(
+    for i in range(slots):
+        bias = jnp.where(mask_ref[i] > 0, 0.0, -jnp.inf).astype(jnp.float32)
+        s = lax.dot_general(
             q, kv_refs[i][0], (((1,), (1,)), ((), ())), preferred_element_type=jnp.float32
-        )
-
-    for i in range(slots):
-        @pl.when(mask_ref[i] > 0)
-        def _():
-            m_ref[...] = jnp.maximum(m_ref[...], scores_of(i))
+        ) + bias
+        s_ref[i] = s
+        m_ref[...] = jnp.maximum(m_ref[...], s)
     highest = jnp.max(m_ref[...], axis=-1, keepdims=True)
     for i in range(slots):
-        @pl.when(mask_ref[i] > 0)
-        def _():
-            p = jnp.exp((scores_of(i) - highest) * factor)
-            l_ref[...] = l_ref[...] + p
-            acc_ref[...] = acc_ref[...] + jnp.dot(
-                p.astype(jnp.bfloat16), kv_refs[i][1], preferred_element_type=jnp.float32
-            )
+        p = jnp.exp((s_ref[i] - highest) * factor)
+        l_ref[...] = l_ref[...] + p
+        acc_ref[...] = acc_ref[...] + jnp.dot(
+            p.astype(jnp.bfloat16), kv_refs[i][1], preferred_element_type=jnp.float32
+        )
     total = jnp.sum(l_ref[...], axis=-1, keepdims=True)
     out_ref[...] = (acc_ref[...] / total).astype(jnp.bfloat16)
 
@@ -76,6 +72,7 @@
             + [kv_spec] * slots,
             out_specs=pl.BlockSpec((rows, HD), lambda h, mask: (0, h)),
             scratch_shapes=[
+                pltpu.VMEM((slots, rows, keys), jnp.float32),
                 pltpu.VMEM((rows, keys), jnp.float32),
                 pltpu.VMEM((rows, keys), jnp.float32),
                 pltpu.VMEM((rows, HD), jnp.float32),

time: 130 us -> 133 us (1.023)
  Pallas kernels: 8.65 us -> 11.3 us
  blocking collectives: 35.6 us -> 37.3 us
    pallas_call x1, Pallas kernels: 8.65 us -> 11.3 us  [attend(): pl.pallas_call(attend_kernel, grid_spec=pltpu.PrefetchScalarGridSpec(num_...]
    all_to_all x1, blocking collectives: 35.6 us -> 37.3 us  [on_device(): received = lax.all_to_all(terms, 'mp', 0, 0, tiled=True).astype(jnp.float32)]
  transfers between devices with their start and end apart: 15 -> 15, of which waited for: 6 -> 6; matrix products, arithmetic and copies ran while one was open for 10% -> 9% of each run, Pallas kernels for 0% -> 0%
where the time goes in v6:
time: 133 us
  blocking collectives  37.3 us (28%)
  waiting for transfers between devices  35.6 us (27%)
  starting transfers between devices  27.8 us (21%)
  matrix products  13.4 us (10%)
  Pallas kernels  11.3 us (8%)
  other arithmetic  3.64 us (3%)
  local copies, waits for them, and re-layouts  3.32 us (2%)
    all_to_all x1, blocking collectives, on_device(): received = lax.all_to_all(terms, 'mp', 0, 0, tiled=True).astype(jnp.float32)  37.3 us
    ppermute x11, waiting for transfers between devices, passed_along(): return lax.ppermute(value, axis, pairs)  35.4 us
    ppermute x11, starting transfers between devices, passed_along(): return lax.ppermute(value, axis, pairs)  27.7 us
    pallas_call x1, Pallas kernels, attend(): pl.pallas_call(attend_kernel, grid_spec=pltpu.PrefetchScalarGridSpec(num_...  11.3 us
    dot_general x7, matrix products, on_device(): jnp.einsum('tf,fjc->jtc', passed_along(tokens, 'mp', step), rows_of(sourc...  8.34 us
    dot_general x1, matrix products, on_device(): jnp.einsum('tk,kjc->jtc', attended, w_out.reshape(w_out.shape[0], mp_coun...  3.16 us
  transfers between devices with their start and end apart: 15, of which 6 were waited for; matrix products, arithmetic and copies ran while one was open for 9% of the time, Pallas kernels for 0%

profile of v6, /device:TPU:8, one launch (start us, length us, event | category | flops | bytes accessed | tf_op | source)
XLA Modules:
  0.0 132.8 jit_solution(9531959450921879713)
XLA Ops:
  0.0 4.8 %collective-permute-start.5 = (bf16[384,384]{1,0:T(8,128)(2,1)}, bf16[384,384]{1,0:T(8,128)(2,1)S(1)}, u32[]{:S(2)}, u32[]{:S(2)}) collective-permute-start(bf16[384,384]{1,0:T(8,128)(2,1)} %param.7), channel_id=1, source_target_pairs={{0,6},{1,7},{2,0},{3,1},{4,2},{5,3},{6,4},{7,5},{8,14},{9,15},{10,... | collective-permute-start | bytes 884744 | tf_op jit(solution)/shard_map/ppermute | solution.py:17
  4.8 1.3 collective-permute-start.4
  6.0 2.3 %collective-permute-start.3 = (bf16[384,384]{1,0:T(8,128)(2,1)}, bf16[384,384]{1,0:T(8,128)(2,1)S(1)}, u32[]{:S(2)}, u32[]{:S(2)}) collective-permute-start(bf16[384,384]{1,0:T(8,128)(2,1)} %param.7), channel_id=1, source_target_pairs={{0,4},{1,5},{2,6},{3,7},{4,0},{5,1},{6,2},{7,3},{8,12},{9,13},{10,... | collective-permute-start | bytes 884744 | tf_op jit(solution)/shard_map/ppermute | solution.py:17
  8.3 0.9 collective-permute-start.2
  9.2 1.8 %collective-permute-start = (bf16[384,384]{1,0:T(8,128)(2,1)}, bf16[384,384]{1,0:T(8,128)(2,1)S(1)}, u32[]{:S(2)}, u32[]{:S(2)}) collective-permute-start(bf16[384,384]{1,0:T(8,128)(2,1)} %param.7), channel_id=1, source_target_pairs={{0,1},{1,2},{2,3},{3,4},{4,5},{5,6},{6,7},{7,0},{8,9},{9,10},{10,1... | collective-permute-start | bytes 884744 | tf_op jit(solution)/shard_map/ppermute | solution.py:17
  11.0 1.9 %fusion.21 = f32[3,384,384]{1,2,0:T(8,128)S(1)} fusion(bf16[3072,3,384]{2,0,1:T(8,128)(2,1)} %param.8, s32[]{:T(128)S(6)} %select_n.101, bf16[384,384]{1,0:T(8,128)(2,1)} %param.7), kind=kOutput, calls=%fused_computation.19 | convolution fusion | flops 339738624 | bytes 2949124 | tf_op jit(solution)/shard_map/tf,fjc->jtc/dot_general | solution.py:98
  13.1 6.4 %collective-permute-start.1 = (bf16[384,384]{1,0:T(8,128)(2,1)S(1)}, bf16[384,384]{1,0:T(8,128)(2,1)S(1)}, u32[]{:S(2)}, u32[]{:S(2)}) collective-permute-start(bf16[384,384]{1,0:T(8,128)(2,1)S(1)} %copy-done.8), channel_id=1, source_target_pairs={{0,2},{1,3},{2,4},{3,5},{4,6},{5,7},{6,0},{7,1},{8,10},{9,11},{10,... | collective-permute-start | bytes 884744 | tf_op jit(solution)/shard_map/ppermute | solution.py:17
  19.5 2.0 %fusion.9 = f32[3,384,384]{1,2,0:T(8,128)S(1)} fusion(bf16[3072,3,384]{2,0,1:T(8,128)(2,1)} %param.8, s32[]{:T(128)S(6)} %select_n.113, bf16[384,384]{1,0:T(8,128)(2,1)S(1)} %collective-permute-done.5), kind=kOutput, calls=%fused_computation.7 | convolution fusion | flops 339738624 | bytes 2949124 | tf_op jit(solution)/shard_map/tf,fjc->jtc/dot_general | solution.py:103
  21.5 7.7 %collective-permute-done = bf16[384,384]{1,0:T(8,128)(2,1)S(1)} collective-permute-done((bf16[384,384]{1,0:T(8,128)(2,1)}, bf16[384,384]{1,0:T(8,128)(2,1)S(1)}, u32[]{:S(2)}, u32[]{:S(2)}) %collective-permute-start) | collective-permute-done | bytes 294944 | tf_op jit(solution)/shard_map/ppermute | solution.py:17
  29.4 1.8 %fusion.19 = f32[3,384,384]{1,2,0:T(8,128)S(1)} fusion(bf16[3072,3,384]{2,0,1:T(8,128)(2,1)} %param.8, s32[]{:T(128)S(6)} %select_n.103, bf16[384,384]{1,0:T(8,128)(2,1)S(1)} %collective-permute-done), kind=kOutput, calls=%fused_computation.17 | convolution fusion | flops 339738624 | bytes 2949124 | tf_op jit(solution)/shard_map/tf,fjc->jtc/dot_general | solution.py:103
  31.3 3.1 %collective-permute-done.1 = bf16[384,384]{1,0:T(8,128)(2,1)S(1)} collective-permute-done((bf16[384,384]{1,0:T(8,128)(2,1)S(1)}, bf16[384,384]{1,0:T(8,128)(2,1)S(1)}, u32[]{:S(2)}, u32[]{:S(2)}) %collective-permute-start.1) | collective-permute-done | bytes 294944 | tf_op jit(solution)/shard_map/ppermute | solution.py:17
  34.3 1.8 %fusion.17 = f32[3,384,384]{1,2,0:T(8,128)S(1)} fusion(bf16[3072,3,384]{2,0,1:T(8,128)(2,1)} %param.8, s32[]{:T(128)S(6)} %select_n.105, bf16[384,384]{1,0:T(8,128)(2,1)S(1)} %collective-permute-done.1), kind=kOutput, calls=%fused_computation.15 | convolution fusion | flops 339738624 | bytes 2949124 | tf_op jit(solution)/shard_map/tf,fjc->jtc/dot_general | solution.py:103
  39.0 0.9 fusion.42
  41.2 1.0 collective-permute-start.9
  42.3 2.0 %collective-permute-start.8 = (bf16[2,3,384,128]{3,2,1,0:T(8,128)(2,1)S(1)}, bf16[2,3,384,128]{3,2,1,0:T(8,128)(2,1)S(1)}, u32[]{:S(2)}, u32[]{:S(2)}) collective-permute-start(bf16[2,3,384,128]{3,2,1,0:T(8,128)(2,1)S(1)} %pad_maximum_fusion.rest_0_), channel_id=1, source_target_pairs={{0,16},{8,24},{16,32},{24,40},{32,48},{40,56},{48,64},{56,72},{64,... | collective-permute-start | bytes 1769480 | tf_op jit(solution)/shard_map/ppermute | solution.py:17
  44.2 7.1 %collective-permute-start.10 = (bf16[2,3,384,128]{3,2,1,0:T(8,128)(2,1)S(1)}, bf16[2,3,384,128]{3,2,1,0:T(8,128)(2,1)S(1)}, u32[]{:S(2)}, u32[]{:S(2)}) collective-permute-start(bf16[2,3,384,128]{3,2,1,0:T(8,128)(2,1)S(1)} %pad_maximum_fusion.rest_0_), channel_id=1, source_target_pairs={{0,224},{8,232},{16,240},{24,248},{32,0},{40,8},{48,16},{56,24},{6... | collective-permute-start | bytes 1769480 | tf_op jit(solution)/shard_map/ppermute | solution.py:17
  51.3 15.4 %collective-permute-done.9.rest_3_ = bf16[2,3,384,128]{3,2,1,0:T(8,128)(2,1)S(1)} collective-permute-done((bf16[2,3,384,128]{3,2,1,0:T(8,128)(2,1)S(1)}, bf16[2,3,384,128]{3,2,1,0:T(8,128)(2,1)S(1)}, u32[]{:S(2)}, u32[]{:S(2)}) %collective-permute-start.9) | collective-permute-done | bytes 589856 | tf_op jit(solution)/shard_map/ppermute | solution.py:17
  66.7 2.4 %collective-permute-done.8.rest_2_ = bf16[2,3,384,128]{3,2,1,0:T(8,128)(2,1)S(1)} collective-permute-done((bf16[2,3,384,128]{3,2,1,0:T(8,128)(2,1)S(1)}, bf16[2,3,384,128]{3,2,1,0:T(8,128)(2,1)S(1)}, u32[]{:S(2)}, u32[]{:S(2)}) %collective-permute-start.8) | collective-permute-done | bytes 589856 | tf_op jit(solution)/shard_map/ppermute | solution.py:17
  69.1 6.8 %collective-permute-done.7.rest_1_ = bf16[2,3,384,128]{3,2,1,0:T(8,128)(2,1)S(1)} collective-permute-done((bf16[2,3,384,128]{3,2,1,0:T(8,128)(2,1)S(1)}, bf16[2,3,384,128]{3,2,1,0:T(8,128)(2,1)S(1)}, u32[]{:S(2)}, u32[]{:S(2)}) %collective-permute-start.7) | collective-permute-done | bytes 589856 | tf_op jit(solution)/shard_map/ppermute | solution.py:17
  76.0 0.9 broadcast_select_fusion
  79.9 11.3 %shard_map.73 = bf16[384,384]{1,0:T(8,128)(2,1)} custom-call(s32[9]{0:T(128)} %convert_element_type.19.mask_ref, f32[384,384]{1,0:T(8,128)} %get-tuple-element.6.q_ref, f32[1,128]{1,0:T(1,128)} %bitcast.58, bf16[2,3,384,128]{3,2,1,0:T(8,128)(2,1)} %copy-done.2, bf16[2,3,384,128]{3,2,1,0:T(8,128)(2,1)} %copy-done.4, bf16[2,3,384,128]{3,2,1,0:T(8,128)(2,1)} %copy-done.6, ...), custom_call_target="tpu_custom_call" | custom-call | tf_op jit(solution)/shard_map/pallas_call | solution.py:63
  91.2 3.2 %convert_bitcast_fusion = bf16[8,384,384]{2,1,0:T(8,128)(2,1)S(1)} fusion(bf16[48,8,8,384]{3,2,1,0:T(8,128)(2,1)} %bitcast.59, bf16[384,384]{1,0:T(8,128)(2,1)} %shard_map.73), kind=kOutput, calls=%fused_computation.3 | convolution fusion | flops 907149312 | bytes 5013504 | tf_op jit(solution)/shard_map/tk,kjc->jtc/dot_general | solution.py:148
  94.4 37.3 %all_to_all.5 = bf16[8,384,384]{2,1,0:T(8,128)(2,1)S(1)} all-to-all(bf16[8,384,384]{2,1,0:T(8,128)(2,1)S(1)} %convert_bitcast_fusion), channel_id=1, replica_groups=mesh['seq'=32,'mp'=8] {'mp'}, dimensions={0} | all-to-all | bytes 4718592 | tf_op jit(solution)/shard_map/all_to_all | solution.py:154
  131.7 1.1 reduce_sum.22
  (58 shorter events, 7.3 us)
Async XLA Ops:
  0.0 77.5 %copy-start = (s32[32,6]{0,1:T(8,128)S(1)}, s32[32,6]{0,1:T(8,128)}, u32[]{:S(2)}) copy-start(s32[32,6]{0,1:T(8,128)} %param.12) | copy-start | bytes 2308
  0.0 13.1 %copy-start.8 = (bf16[384,384]{1,0:T(8,128)(2,1)S(1)}, bf16[384,384]{1,0:T(8,128)(2,1)}, u32[]{:S(2)}) copy-start(bf16[384,384]{1,0:T(8,128)(2,1)} %param.7) | copy-start | bytes 884740
  0.0 13.1 %collective-permute-start.5 = (bf16[384,384]{1,0:T(8,128)(2,1)}, bf16[384,384]{1,0:T(8,128)(2,1)S(1)}, u32[]{:S(2)}, u32[]{:S(2)}) collective-permute-start(bf16[384,384]{1,0:T(8,128)(2,1)} %param.7), channel_id=1, source_target_pairs={{0,6},{1,7},{2,0},{3,1},{4,2},{5,3},{6,4},{7,5},{8,14},{9,15},{10,... | collective-permute-start | bytes 884744 | tf_op jit(solution)/shard_map/ppermute | solution.py:17
  4.8 32.7 %collective-permute-start.4 = (bf16[384,384]{1,0:T(8,128)(2,1)}, bf16[384,384]{1,0:T(8,128)(2,1)S(1)}, u32[]{:S(2)}, u32[]{:S(2)}) collective-permute-start(bf16[384,384]{1,0:T(8,128)(2,1)} %param.7), channel_id=1, source_target_pairs={{0,5},{1,6},{2,7},{3,0},{4,1},{5,2},{6,3},{7,4},{8,13},{9,14},{10,... | collective-permute-start | bytes 884744 | tf_op jit(solution)/shard_map/ppermute | solution.py:17
  6.0 30.8 %collective-permute-start.3 = (bf16[384,384]{1,0:T(8,128)(2,1)}, bf16[384,384]{1,0:T(8,128)(2,1)S(1)}, u32[]{:S(2)}, u32[]{:S(2)}) collective-permute-start(bf16[384,384]{1,0:T(8,128)(2,1)} %param.7), channel_id=1, source_target_pairs={{0,4},{1,5},{2,6},{3,7},{4,0},{5,1},{6,2},{7,3},{8,12},{9,13},{10,... | collective-permute-start | bytes 884744 | tf_op jit(solution)/shard_map/ppermute | solution.py:17
  8.3 27.8 %collective-permute-start.2 = (bf16[384,384]{1,0:T(8,128)(2,1)}, bf16[384,384]{1,0:T(8,128)(2,1)S(1)}, u32[]{:S(2)}, u32[]{:S(2)}) collective-permute-start(bf16[384,384]{1,0:T(8,128)(2,1)} %param.7), channel_id=1, source_target_pairs={{0,3},{1,4},{2,5},{3,6},{4,7},{5,0},{6,1},{7,2},{8,11},{9,12},{10,... | collective-permute-start | bytes 884744 | tf_op jit(solution)/shard_map/ppermute | solution.py:17
  9.2 20.0 %collective-permute-start = (bf16[384,384]{1,0:T(8,128)(2,1)}, bf16[384,384]{1,0:T(8,128)(2,1)S(1)}, u32[]{:S(2)}, u32[]{:S(2)}) collective-permute-start(bf16[384,384]{1,0:T(8,128)(2,1)} %param.7), channel_id=1, source_target_pairs={{0,1},{1,2},{2,3},{3,4},{4,5},{5,6},{6,7},{7,0},{8,9},{9,10},{10,1... | collective-permute-start | bytes 884744 | tf_op jit(solution)/shard_map/ppermute | solution.py:17
  13.1 21.2 %collective-permute-start.1 = (bf16[384,384]{1,0:T(8,128)(2,1)S(1)}, bf16[384,384]{1,0:T(8,128)(2,1)S(1)}, u32[]{:S(2)}, u32[]{:S(2)}) collective-permute-start(bf16[384,384]{1,0:T(8,128)(2,1)S(1)} %copy-done.8), channel_id=1, source_target_pairs={{0,2},{1,3},{2,4},{3,5},{4,6},{5,7},{6,0},{7,1},{8,10},{9,11},{10,... | collective-permute-start | bytes 884744 | tf_op jit(solution)/shard_map/ppermute | solution.py:17
  19.5 16.6 %copy-start.1 = (bf16[3072,3,384]{2,0,1:T(8,128)(2,1)S(1)}, bf16[3072,3,384]{2,0,1:T(8,128)(2,1)}, u32[]{:S(2)}) copy-start(bf16[3072,3,384]{2,0,1:T(8,128)(2,1)} %param.8) | copy-start | bytes 21233668
  29.2 8.9 %collective-permute-start.6 = (bf16[384,384]{1,0:T(8,128)(2,1)S(1)}, bf16[384,384]{1,0:T(8,128)(2,1)S(1)}, u32[]{:S(2)}, u32[]{:S(2)}) collective-permute-start(bf16[384,384]{1,0:T(8,128)(2,1)S(1)} %copy-done.8), channel_id=1, source_target_pairs={{0,7},{1,0},{2,1},{3,2},{4,3},{5,4},{6,5},{7,6},{8,15},{9,8},{10,9... | collective-permute-start | bytes 884744 | tf_op jit(solution)/shard_map/ppermute | solution.py:17
  40.9 36.0 %copy-start.10 = (s32[32]{0:T(128)S(1)}, s32[32]{0:T(128)}, u32[]{:S(2)}) copy-start(s32[32]{0:T(128)} %param.13) | copy-start | bytes 388
  41.2 38.0 %copy-start.2 = (bf16[2,3,384,128]{3,2,1,0:T(8,128)(2,1)}, bf16[2,3,384,128]{3,2,1,0:T(8,128)(2,1)S(1)}, u32[]{:S(2)}) copy-start(bf16[2,3,384,128]{3,2,1,0:T(8,128)(2,1)S(1)} %pad_maximum_fusion.rest_0_) | copy-start | bytes 1769476
  41.2 25.4 %collective-permute-start.9 = (bf16[2,3,384,128]{3,2,1,0:T(8,128)(2,1)S(1)}, bf16[2,3,384,128]{3,2,1,0:T(8,128)(2,1)S(1)}, u32[]{:S(2)}, u32[]{:S(2)}) collective-permute-start(bf16[2,3,384,128]{3,2,1,0:T(8,128)(2,1)S(1)} %pad_maximum_fusion.rest_0_), channel_id=1, source_target_pairs={{0,240},{8,248},{16,0},{24,8},{32,16},{40,24},{48,32},{56,40},{64,... | collective-permute-start | bytes 1769480 | tf_op jit(solution)/shard_map/ppermute | solution.py:17
  42.3 26.9 %collective-permute-start.8 = (bf16[2,3,384,128]{3,2,1,0:T(8,128)(2,1)S(1)}, bf16[2,3,384,128]{3,2,1,0:T(8,128)(2,1)S(1)}, u32[]{:S(2)}, u32[]{:S(2)}) collective-permute-start(bf16[2,3,384,128]{3,2,1,0:T(8,128)(2,1)S(1)} %pad_maximum_fusion.rest_0_), channel_id=1, source_target_pairs={{0,16},{8,24},{16,32},{24,40},{32,48},{40,56},{48,64},{56,72},{64,... | collective-permute-start | bytes 1769480 | tf_op jit(solution)/shard_map/ppermute | solution.py:17
  44.2 24.9 %collective-permute-start.10 = (bf16[2,3,384,128]{3,2,1,0:T(8,128)(2,1)S(1)}, bf16[2,3,384,128]{3,2,1,0:T(8,128)(2,1)S(1)}, u32[]{:S(2)}, u32[]{:S(2)}) collective-permute-start(bf16[2,3,384,128]{3,2,1,0:T(8,128)(2,1)S(1)} %pad_maximum_fusion.rest_0_), channel_id=1, source_target_pairs={{0,224},{8,232},{16,240},{24,248},{32,0},{40,8},{48,16},{56,24},{6... | collective-permute-start | bytes 1769480 | tf_op jit(solution)/shard_map/ppermute | solution.py:17
  51.3 24.6 %collective-permute-start.7 = (bf16[2,3,384,128]{3,2,1,0:T(8,128)(2,1)S(1)}, bf16[2,3,384,128]{3,2,1,0:T(8,128)(2,1)S(1)}, u32[]{:S(2)}, u32[]{:S(2)}) collective-permute-start(bf16[2,3,384,128]{3,2,1,0:T(8,128)(2,1)S(1)} %pad_maximum_fusion.rest_0_), channel_id=1, source_target_pairs={{0,32},{8,40},{16,48},{24,56},{32,64},{40,72},{48,80},{56,88},{64,... | collective-permute-start | bytes 1769480 | tf_op jit(solution)/shard_map/ppermute | solution.py:17
  51.3 27.7 %collective-permute-start.11 = (bf16[2,3,384,128]{3,2,1,0:T(8,128)(2,1)S(1)}, bf16[2,3,384,128]{3,2,1,0:T(8,128)(2,1)S(1)}, u32[]{:S(2)}, u32[]{:S(2)}) collective-permute-start(bf16[2,3,384,128]{3,2,1,0:T(8,128)(2,1)S(1)} %pad_maximum_fusion.rest_0_), channel_id=1, source_target_pairs={{0,8},{8,0},{16,24},{24,16},{32,40},{40,32},{48,56},{56,48},{64,72... | collective-permute-start | bytes 1769480 | tf_op jit(solution)/shard_map/ppermute | solution.py:120
  66.7 12.6 %copy-start.5 = (bf16[2,3,384,128]{3,2,1,0:T(8,128)(2,1)}, bf16[2,3,384,128]{3,2,1,0:T(8,128)(2,1)S(1)}, u32[]{:S(2)}) copy-start(bf16[2,3,384,128]{3,2,1,0:T(8,128)(2,1)S(1)} %collective-permute-done.9.rest_3_) | copy-start | bytes 1769476
  66.7 12.4 %collective-permute-start.13 = (bf16[2,3,384,128]{3,2,1,0:T(8,128)(2,1)S(1)}, bf16[2,3,384,128]{3,2,1,0:T(8,128)(2,1)}, u32[]{:S(2)}, u32[]{:S(2)}) collective-permute-start(bf16[2,3,384,128]{3,2,1,0:T(8,128)(2,1)S(1)} %collective-permute-done.9.rest_3_), channel_id=1, source_target_pairs={{0,8},{8,0},{16,24},{24,16},{32,40},{40,32},{48,56},{56,48},{64,72... | collective-permute-start | bytes 1769480 | tf_op jit(solution)/shard_map/ppermute | solution.py:122
  69.1 10.1 %copy-start.6 = (bf16[2,3,384,128]{3,2,1,0:T(8,128)(2,1)}, bf16[2,3,384,128]{3,2,1,0:T(8,128)(2,1)S(1)}, u32[]{:S(2)}) copy-start(bf16[2,3,384,128]{3,2,1,0:T(8,128)(2,1)S(1)} %collective-permute-done.8.rest_2_) | copy-start | bytes 1769476
  69.1 9.9 %collective-permute-start.12 = (bf16[2,3,384,128]{3,2,1,0:T(8,128)(2,1)S(1)}, bf16[2,3,384,128]{3,2,1,0:T(8,128)(2,1)}, u32[]{:S(2)}, u32[]{:S(2)}) collective-permute-start(bf16[2,3,384,128]{3,2,1,0:T(8,128)(2,1)S(1)} %collective-permute-done.8.rest_2_), channel_id=1, source_target_pairs={{0,8},{8,0},{16,24},{24,16},{32,40},{40,32},{48,56},{56,48},{64,72... | collective-permute-start | bytes 1769480 | tf_op jit(solution)/shard_map/ppermute | solution.py:121
  69.1 10.1 %copy-start.3 = (bf16[2,3,384,128]{3,2,1,0:T(8,128)(2,1)}, bf16[2,3,384,128]{3,2,1,0:T(8,128)(2,1)S(1)}, u32[]{:S(2)}) copy-start(bf16[2,3,384,128]{3,2,1,0:T(8,128)(2,1)S(1)} %collective-permute-done.10.rest_4_) | copy-start | bytes 1769476
  76.0 3.3 %copy-start.4 = (bf16[2,3,384,128]{3,2,1,0:T(8,128)(2,1)}, bf16[2,3,384,128]{3,2,1,0:T(8,128)(2,1)S(1)}, u32[]{:S(2)}) copy-start(bf16[2,3,384,128]{3,2,1,0:T(8,128)(2,1)S(1)} %collective-permute-done.7.rest_1_) | copy-start | bytes 1769476
  76.9 2.3 %collective-permute-start.14 = (bf16[2,3,384,128]{3,2,1,0:T(8,128)(2,1)}, bf16[2,3,384,128]{3,2,1,0:T(8,128)(2,1)}, u32[]{:S(2)}, u32[]{:S(2)}) collective-permute-start(bf16[2,3,384,128]{3,2,1,0:T(8,128)(2,1)} %broadcast_select_fusion), channel_id=1, source_target_pairs={{0,8},{8,0},{16,24},{24,16},{32,40},{40,32},{48,56},{56,48},{64,72... | collective-permute-start | bytes 1769480 | tf_op jit(solution)/shard_map/ppermute | solution.py:123
  (2 other events, 1.6 us)

commit v7 on v5

--- a/solution.py
+++ b/solution.py
@@ -95,30 +95,53 @@
     mp_count = lax.axis_size("mp")
     mp_here = lax.axis_index("mp")
 
-    spread = jnp.broadcast_to(tokens[None], (mp_count,) + tokens.shape)
-    gathered = lax.all_to_all(spread, "mp", 0, 0, tiled=True)
-    projected = jnp.einsum(
-        "itf,ifjc->jtc",
-        gathered,
-        w_qkv.reshape(mp_count, feats, 3, columns),
-        preferred_element_type=jnp.float32,
-    )
-    key_part = head_norm(projected[1], k_gain).transpose(1, 0, 2)
-    value_part = projected[2].astype(jnp.bfloat16).reshape(tok_rows, heads_here, HD).transpose(1, 0, 2)
-    paired = jnp.stack([key_part, value_part])
+    def rows_of(block):
+        return lax.dynamic_slice_in_dim(w_qkv, block * feats, feats, 0)
+
     position = lax.axis_index("seq")
     seq_count = lax.axis_size("seq")
     core = position % 2
     partner = [(source, source ^ 1) for source in range(seq_count)]
-    from_m4 = passed_along(paired, "seq", 4)
-    from_m2 = passed_along(paired, "seq", 2)
-    from_p2 = passed_along(paired, "seq", -2)
-    from_p4 = passed_along(paired, "seq", -4)
-    fwd_own = lax.ppermute(paired, "seq", partner)
-    fwd_a = lax.ppermute(from_m2, "seq", partner)
-    fwd_b = lax.ppermute(from_p2, "seq", partner)
-    fwd_c = lax.ppermute(jnp.where(core == 0, from_p4, from_m4), "seq", partner)
-    kv_tiles = [paired, from_m4, from_m2, from_p2, from_p4, fwd_own, fwd_a, fwd_b, fwd_c]
+
+    def gathered_projection(part):
+        projected = jnp.einsum(
+            "tf,fjc->jtc", part, rows_of(mp_here), preferred_element_type=jnp.float32
+        )
+        for step in range(1, mp_count):
+            source = (mp_here - step) % mp_count
+            projected = projected + jnp.einsum(
+                "tf,fjc->jtc",
+                passed_along(part, "mp", step),
+                rows_of(source),
+                preferred_element_type=jnp.float32,
+            )
+        return projected
+
+    def exchanged(paired):
+        from_m4 = passed_along(paired, "seq", 4)
+        from_m2 = passed_along(paired, "seq", 2)
+        from_p2 = passed_along(paired, "seq", -2)
+        from_p4 = passed_along(paired, "seq", -4)
+        fwd_own = lax.ppermute(paired, "seq", partner)
+        fwd_a = lax.ppermute(from_m2, "seq", partner)
+        fwd_b = lax.ppermute(from_p2, "seq", partner)
+        fwd_c = lax.ppermute(jnp.where(core == 0, from_p4, from_m4), "seq", partner)
+        return [paired, from_m4, from_m2, from_p2, from_p4, fwd_own, fwd_a, fwd_b, fwd_c]
+
+    half = tok_rows // 2
+    kv_tiles = []
+    query_parts = []
+    later_rows = tokens[half:]
+    for lower in (0, half):
+        part = tokens[:half] if lower == 0 else later_rows
+        projected = gathered_projection(part)
+        key_part = head_norm(projected[1], k_gain).transpose(1, 0, 2)
+        value_part = projected[2].astype(jnp.bfloat16).reshape(half, heads_here, HD).transpose(1, 0, 2)
+        paired = jnp.stack([key_part, value_part])
+        if lower == 0:
+            paired, later_rows = lax.optimization_barrier((paired, later_rows))
+        kv_tiles = kv_tiles + exchanged(paired)
+        query_parts.append(projected[0])
     odd = core == 1
     slot_offsets = jnp.stack(
         [
@@ -139,7 +162,8 @@
     slot_used = jnp.arange(NB, dtype=jnp.int32)[None, :] < used_counts[:, None]
     hits = (listed[:, :, None] == slot_tile[None, None, :]) & slot_used[:, :, None]
     tile_mask = jnp.any(hits, axis=1)[0].astype(jnp.int32)
-    q_raw = projected[0]
+    tile_mask = jnp.concatenate([tile_mask, tile_mask])
+    q_raw = jnp.concatenate(query_parts, axis=0)
     attended = attend(tile_mask, q_raw, q_gain, kv_tiles)
     out_cols = w_out.shape[1] // mp_count
     terms = jnp.einsum(

time: 131 us -> 148 us (1.13)
  the two profiles are of different devices: /device:TPU:64 before, /device:TPU:2 now
where the time goes in v7:
time: 148 us; the launch traced here: 147 us
  starting transfers between devices  45.3 us (31%)
  blocking collectives  27 us (18%)
  Pallas kernels  26.9 us (18%)
  matrix products  24 us (16%)
  waiting for transfers between devices  14.8 us (10%)
  other arithmetic  4.32 us (3%)
  local copies, waits for them, and re-layouts  4.26 us (3%)
    ppermute x22, starting transfers between devices, passed_along(): return lax.ppermute(value, axis, pairs)  43.9 us
    all_to_all x1, blocking collectives, on_device(): received = lax.all_to_all(terms, 'mp', 0, 0, tiled=True).astype(jnp.float32)  27 us
    pallas_call x1, Pallas kernels, attend(): pl.pallas_call(attend_kernel, grid_spec=pltpu.PrefetchScalarGridSpec(num_...  26.9 us
    dot_general x14, matrix products, gathered_projection(): jnp.einsum('tf,fjc->jtc', passed_along(part, 'mp', step), rows_of(source)...  17.5 us
    ppermute x22, waiting for transfers between devices, passed_along(): return lax.ppermute(value, axis, pairs)  14.7 us
    dot_general x2, matrix products, gathered_projection(): jnp.einsum('tf,fjc->jtc', part, rows_of(mp_here), preferred_element_type=...  3.35 us
    dot_general x1, matrix products, on_device(): jnp.einsum('tk,kjc->jtc', attended, w_out.reshape(w_out.shape[0], mp_coun...  3.16 us
  transfers between devices with their start and end apart: 30, of which 4 were waited for; matrix products, arithmetic and copies ran while one was open for 17% of the time, Pallas kernels for 0%

profile of v7, /device:TPU:2, one launch (start us, length us, event | category | flops | bytes accessed | tf_op | source)
XLA Modules:
  0.0 147.4 jit_solution(2139007341351670547)
XLA Ops:
  2.6 5.2 %collective-permute-start.5 = (bf16[192,384]{1,0:T(8,128)(2,1)S(1)}, bf16[192,384]{1,0:T(8,128)(2,1)S(1)}, u32[]{:S(2)}, u32[]{:S(2)}) collective-permute-start(bf16[192,384]{1,0:T(8,128)(2,1)S(1)} %get-tuple-element.14), channel_id=1, source_target_pairs={{0,6},{1,7},{2,0},{3,1},{4,2},{5,3},{6,4},{7,5},{8,14},{9,15},{10,... | collective-permute-start | bytes 442376 | tf_op jit(solution)/shard_map/ppermute | solution.py:17
  9.3 4.4 %collective-permute-start.2 = (bf16[192,384]{1,0:T(8,128)(2,1)S(1)}, bf16[192,384]{1,0:T(8,128)(2,1)S(1)}, u32[]{:S(2)}, u32[]{:S(2)}) collective-permute-start(bf16[192,384]{1,0:T(8,128)(2,1)S(1)} %get-tuple-element.14), channel_id=1, source_target_pairs={{0,3},{1,4},{2,5},{3,6},{4,7},{5,0},{6,1},{7,2},{8,11},{9,12},{10,... | collective-permute-start | bytes 442376 | tf_op jit(solution)/shard_map/ppermute | solution.py:17
  13.8 1.8 %fusion.41 = f32[3,384,192]{1,2,0:T(8,128)S(1)} fusion(bf16[3072,3,384]{2,0,1:T(8,128)(2,1)} %param.8, s32[]{:T(128)S(6)} %select_n.127, bf16[384,384]{1,0:T(8,128)(2,1)} %param.7), kind=kOutput, calls=%fused_computation.44 | convolution fusion | flops 169869312 | bytes 1916932 | tf_op jit(solution)/shard_map/tf,fjc->jtc/dot_general | solution.py:107
  18.1 1.6 %fusion.21 = f32[3,384,192]{1,2,0:T(8,128)S(1)} fusion(bf16[3072,3,384]{2,0,1:T(8,128)(2,1)} %param.8, s32[]{:T(128)S(6)} %select_n.139, bf16[192,384]{1,0:T(8,128)(2,1)S(1)} %collective-permute-done.5), kind=kOutput, calls=%fused_computation.24 | convolution fusion | flops 169869312 | bytes 1916932 | tf_op jit(solution)/shard_map/tf,fjc->jtc/dot_general | solution.py:112
  19.7 1.6 %fusion.25 = f32[3,384,192]{1,2,0:T(8,128)S(1)} fusion(bf16[3072,3,384]{2,0,1:T(8,128)(2,1)} %param.8, s32[]{:T(128)S(6)} %select_n.137, bf16[192,384]{1,0:T(8,128)(2,1)S(1)} %collective-permute-done.4), kind=kOutput, calls=%fused_computation.28 | convolution fusion | flops 169869312 | bytes 1916932 | tf_op jit(solution)/shard_map/tf,fjc->jtc/dot_general | solution.py:112
  22.6 4.6 %collective-permute-done.1 = bf16[192,384]{1,0:T(8,128)(2,1)S(1)} collective-permute-done((bf16[192,384]{1,0:T(8,128)(2,1)S(1)}, bf16[192,384]{1,0:T(8,128)(2,1)S(1)}, u32[]{:S(2)}, u32[]{:S(2)}) %collective-permute-start.1) | collective-permute-done | bytes 147488 | tf_op jit(solution)/shard_map/ppermute | solution.py:17
  28.6 4.9 %collective-permute-start.12 = (bf16[192,384]{1,0:T(8,128)(2,1)S(1)}, bf16[192,384]{1,0:T(8,128)(2,1)S(1)}, u32[]{:S(2)}, u32[]{:S(2)}) collective-permute-start(bf16[192,384]{1,0:T(8,128)(2,1)S(1)} %get-tuple-element.7), channel_id=1, source_target_pairs={{0,6},{1,7},{2,0},{3,1},{4,2},{5,3},{6,4},{7,5},{8,14},{9,15},{10,... | collective-permute-start | bytes 442376 | tf_op jit(solution)/shard_map/ppermute | solution.py:17
  33.5 3.0 %collective-permute-start.10 = (bf16[192,384]{1,0:T(8,128)(2,1)S(1)}, bf16[192,384]{1,0:T(8,128)(2,1)S(1)}, u32[]{:S(2)}, u32[]{:S(2)}) collective-permute-start(bf16[192,384]{1,0:T(8,128)(2,1)S(1)} %get-tuple-element.7), channel_id=1, source_target_pairs={{0,4},{1,5},{2,6},{3,7},{4,0},{5,1},{6,2},{7,3},{8,12},{9,13},{10,... | collective-permute-start | bytes 442376 | tf_op jit(solution)/shard_map/ppermute | solution.py:17
  36.5 4.4 %collective-permute-start.9 = (bf16[192,384]{1,0:T(8,128)(2,1)S(1)}, bf16[192,384]{1,0:T(8,128)(2,1)S(1)}, u32[]{:S(2)}, u32[]{:S(2)}) collective-permute-start(bf16[192,384]{1,0:T(8,128)(2,1)S(1)} %get-tuple-element.7), channel_id=1, source_target_pairs={{0,3},{1,4},{2,5},{3,6},{4,7},{5,0},{6,1},{7,2},{8,11},{9,12},{10,... | collective-permute-start | bytes 442376 | tf_op jit(solution)/shard_map/ppermute | solution.py:17
  40.9 1.6 %fusion.43 = f32[3,384,192]{1,2,0:T(8,128)S(1)} fusion(bf16[3072,3,384]{2,0,1:T(8,128)(2,1)} %param.8, s32[]{:T(128)S(6)} %select_n.127, bf16[192,384]{1,0:T(8,128)(2,1)S(1)} %get-tuple-element.7), kind=kOutput, calls=%fused_computation.46 | convolution fusion | flops 169869312 | bytes 1916932 | tf_op jit(solution)/shard_map/tf,fjc->jtc/dot_general | solution.py:107
  42.6 1.6 %convolution_add_fusion.1 = f32[3,384,192]{1,2,0:T(8,128)S(1)} fusion(f32[3,384,192]{1,2,0:T(8,128)S(1)} %fusion.43, bf16[3072,3,384]{2,0,1:T(8,128)(2,1)} %param.8, s32[]{:T(128)S(6)} %select_n.129, bf16[192,384]{1,0:T(8,128)(2,1)S(1)} %collective-permute-done.7), kind=kOutput, calls=%fused_computation.11 | convolution fusion | flops 170090496 | bytes 2801668 | tf_op jit(solution)/shard_map/tf,fjc->jtc/dot_general | solution.py:112
  44.3 1.6 %fusion.23 = f32[3,384,192]{1,2,0:T(8,128)S(1)} fusion(bf16[3072,3,384]{2,0,1:T(8,128)(2,1)} %param.8, s32[]{:T(128)S(6)} %select_n.139, bf16[192,384]{1,0:T(8,128)(2,1)S(1)} %collective-permute-done.12), kind=kOutput, calls=%fused_computation.26 | convolution fusion | flops 169869312 | bytes 1916932 | tf_op jit(solution)/shard_map/tf,fjc->jtc/dot_general | solution.py:112
  45.9 2.0 %collective-permute-start.14 = (bf16[2,3,192,128]{3,2,1,0:T(8,128)(2,1)S(1)}, bf16[2,3,192,128]{3,2,1,0:T(8,128)(2,1)S(1)}, u32[]{:S(2)}, u32[]{:S(2)}) collective-permute-start(bf16[2,3,192,128]{3,2,1,0:T(8,128)(2,1)S(1)} %pad_maximum_fusion.1.rest_0_), channel_id=1, source_target_pairs={{0,32},{8,40},{16,48},{24,56},{32,64},{40,72},{48,80},{56,88},{64,... | collective-permute-start | bytes 884744 | tf_op jit(solution)/shard_map/ppermute | solution.py:17
  49.5 4.0 %collective-permute-start.17 = (bf16[2,3,192,128]{3,2,1,0:T(8,128)(2,1)S(1)}, bf16[2,3,192,128]{3,2,1,0:T(8,128)(2,1)S(1)}, u32[]{:S(2)}, u32[]{:S(2)}) collective-permute-start(bf16[2,3,192,128]{3,2,1,0:T(8,128)(2,1)S(1)} %pad_maximum_fusion.1.rest_0_), channel_id=1, source_target_pairs={{0,224},{8,232},{16,240},{24,248},{32,0},{40,8},{48,16},{56,24},{6... | collective-permute-start | bytes 884744 | tf_op jit(solution)/shard_map/ppermute | solution.py:17
  57.5 3.5 %collective-permute-start.16 = (bf16[2,3,192,128]{3,2,1,0:T(8,128)(2,1)S(1)}, bf16[2,3,192,128]{3,2,1,0:T(8,128)(2,1)S(1)}, u32[]{:S(2)}, u32[]{:S(2)}) collective-permute-start(bf16[2,3,192,128]{3,2,1,0:T(8,128)(2,1)S(1)} %pad_maximum_fusion.1.rest_0_), channel_id=1, source_target_pairs={{0,240},{8,248},{16,0},{24,8},{32,16},{40,24},{48,32},{56,40},{64,... | collective-permute-start | bytes 884744 | tf_op jit(solution)/shard_map/ppermute | solution.py:17
  61.0 1.6 %fusion.19 = f32[3,384,192]{1,2,0:T(8,128)S(1)} fusion(bf16[3072,3,384]{2,0,1:T(8,128)(2,1)} %param.8, s32[]{:T(128)S(6)} %select_n.141, bf16[192,384]{1,0:T(8,128)(2,1)S(1)} %collective-permute-done.13), kind=kOutput, calls=%fused_computation.22 | convolution fusion | flops 169869312 | bytes 1916932 | tf_op jit(solution)/shard_map/tf,fjc->jtc/dot_general | solution.py:112
  62.6 1.6 %fusion.10 = f32[3,192,384]{2,1,0:T(8,128)S(1)} fusion(f32[3,384,192]{1,2,0:T(8,128)S(1)} %fusion.19, f32[3,384,192]{1,2,0:T(8,128)S(1)} %fusion.23, f32[3,384,192]{1,2,0:T(8,128)S(1)} %fusion.27, f32[3,384,192]{1,2,0:T(8,128)S(1)} %fusion.31, f32[3,384,192]{1,2,0:T(8,128)S(1)} %fusion.35, f32[3,384,192]{1,2,0:T(8,128)S(1)} %convolution_add_fusion.1, ...), kind=kOutput, calls=%fused_computation.10 | convolution fusion | flops 171196416 | bytes 7225348 | tf_op jit(solution)/shard_map/tf,fjc->jtc/dot_general | solution.py:112
  65.2 3.2 %collective-permute-start.25 = (bf16[2,3,192,128]{3,2,1,0:T(8,128)(2,1)S(1)}, bf16[2,3,192,128]{3,2,1,0:T(8,128)(2,1)S(1)}, u32[]{:S(2)}, u32[]{:S(2)}) collective-permute-start(bf16[2,3,192,128]{3,2,1,0:T(8,128)(2,1)S(1)} %pad_maximum_fusion.2.rest_9_), channel_id=1, source_target_pairs={{0,224},{8,232},{16,240},{24,248},{32,0},{40,8},{48,16},{56,24},{6... | collective-permute-start | bytes 884744 | tf_op jit(solution)/shard_map/ppermute | solution.py:17
  69.4 4.1 %collective-permute-start.24 = (bf16[2,3,192,128]{3,2,1,0:T(8,128)(2,1)S(1)}, bf16[2,3,192,128]{3,2,1,0:T(8,128)(2,1)S(1)}, u32[]{:S(2)}, u32[]{:S(2)}) collective-permute-start(bf16[2,3,192,128]{3,2,1,0:T(8,128)(2,1)S(1)} %pad_maximum_fusion.2.rest_9_), channel_id=1, source_target_pairs={{0,240},{8,248},{16,0},{24,8},{32,16},{40,24},{48,32},{56,40},{64,... | collective-permute-start | bytes 884744 | tf_op jit(solution)/shard_map/ppermute | solution.py:17
  75.1 7.8 %collective-permute-done.23.rest_11_ = bf16[2,3,192,128]{3,2,1,0:T(8,128)(2,1)S(1)} collective-permute-done((bf16[2,3,192,128]{3,2,1,0:T(8,128)(2,1)S(1)}, bf16[2,3,192,128]{3,2,1,0:T(8,128)(2,1)S(1)}, u32[]{:S(2)}, u32[]{:S(2)}) %collective-permute-start.23) | collective-permute-done | bytes 294944 | tf_op jit(solution)/shard_map/ppermute | solution.py:17
  82.9 2.3 %collective-permute-done.24.rest_12_ = bf16[2,3,192,128]{3,2,1,0:T(8,128)(2,1)S(1)} collective-permute-done((bf16[2,3,192,128]{3,2,1,0:T(8,128)(2,1)S(1)}, bf16[2,3,192,128]{3,2,1,0:T(8,128)(2,1)S(1)}, u32[]{:S(2)}, u32[]{:S(2)}) %collective-permute-start.24) | collective-permute-done | bytes 294944 | tf_op jit(solution)/shard_map/ppermute | solution.py:17
  89.2 26.9 %shard_map.73 = bf16[384,384]{1,0:T(8,128)(2,1)} custom-call(s32[18]{0:T(128)} %add_convert_fusion.mask_ref, f32[384,384]{1,0:T(8,128)} %pad_maximum_fusion.q_ref, f32[1,128]{1,0:T(1,128)} %bitcast.93, bf16[2,3,192,128]{3,2,1,0:T(8,128)(2,1)} %copy-done.6, bf16[2,3,192,128]{3,2,1,0:T(8,128)(2,1)} %copy-done.2, bf16[2,3,192,128]{3,2,1,0:T(8,128)(2,1)} %copy-done.8, ...), custom_call_target="tpu_custom_call" | custom-call | tf_op jit(solution)/shard_map/pallas_call | solution.py:67
  116.2 3.2 %convert_bitcast_fusion = bf16[8,384,384]{2,1,0:T(8,128)(2,1)S(1)} fusion(bf16[48,8,8,384]{3,2,1,0:T(8,128)(2,1)} %bitcast.94, bf16[384,384]{1,0:T(8,128)(2,1)} %shard_map.73), kind=kOutput, calls=%fused_computation.3 | convolution fusion | flops 907149312 | bytes 5013504 | tf_op jit(solution)/shard_map/tk,kjc->jtc/dot_general | solution.py:169
  119.3 27.0 %all_to_all.5 = bf16[8,384,384]{2,1,0:T(8,128)(2,1)S(1)} all-to-all(bf16[8,384,384]{2,1,0:T(8,128)(2,1)S(1)} %convert_bitcast_fusion), channel_id=1, replica_groups=mesh['seq'=32,'mp'=8] {'mp'}, dimensions={0} | all-to-all | bytes 4718592 | tf_op jit(solution)/shard_map/all_to_all | solution.py:175
  (131 shorter events, 23.3 us)
Async XLA Ops:
  1.0 14.6 %collective-permute-start = (bf16[192,384]{1,0:T(8,128)(2,1)S(1)}, bf16[192,384]{1,0:T(8,128)(2,1)S(1)}, u32[]{:S(2)}, u32[]{:S(2)}) collective-permute-start(bf16[192,384]{1,0:T(8,128)(2,1)S(1)} %get-tuple-element.14), channel_id=1, source_target_pairs={{0,1},{1,2},{2,3},{3,4},{4,5},{5,6},{6,7},{7,0},{8,9},{9,10},{10,1... | collective-permute-start | bytes 442376 | tf_op jit(solution)/shard_map/ppermute | solution.py:17
  2.6 15.4 %collective-permute-start.5 = (bf16[192,384]{1,0:T(8,128)(2,1)S(1)}, bf16[192,384]{1,0:T(8,128)(2,1)S(1)}, u32[]{:S(2)}, u32[]{:S(2)}) collective-permute-start(bf16[192,384]{1,0:T(8,128)(2,1)S(1)} %get-tuple-element.14), channel_id=1, source_target_pairs={{0,6},{1,7},{2,0},{3,1},{4,2},{5,3},{6,4},{7,5},{8,14},{9,15},{10,... | collective-permute-start | bytes 442376 | tf_op jit(solution)/shard_map/ppermute | solution.py:17
  7.8 11.9 %collective-permute-start.4 = (bf16[192,384]{1,0:T(8,128)(2,1)S(1)}, bf16[192,384]{1,0:T(8,128)(2,1)S(1)}, u32[]{:S(2)}, u32[]{:S(2)}) collective-permute-start(bf16[192,384]{1,0:T(8,128)(2,1)S(1)} %get-tuple-element.14), channel_id=1, source_target_pairs={{0,5},{1,6},{2,7},{3,0},{4,1},{5,2},{6,3},{7,4},{8,13},{9,14},{10,... | collective-permute-start | bytes 442376 | tf_op jit(solution)/shard_map/ppermute | solution.py:17
  7.8 13.5 %collective-permute-start.3 = (bf16[192,384]{1,0:T(8,128)(2,1)S(1)}, bf16[192,384]{1,0:T(8,128)(2,1)S(1)}, u32[]{:S(2)}, u32[]{:S(2)}) collective-permute-start(bf16[192,384]{1,0:T(8,128)(2,1)S(1)} %get-tuple-element.14), channel_id=1, source_target_pairs={{0,4},{1,5},{2,6},{3,7},{4,0},{5,1},{6,2},{7,3},{8,12},{9,13},{10,... | collective-permute-start | bytes 442376 | tf_op jit(solution)/shard_map/ppermute | solution.py:17
  9.3 12.4 %collective-permute-start.2 = (bf16[192,384]{1,0:T(8,128)(2,1)S(1)}, bf16[192,384]{1,0:T(8,128)(2,1)S(1)}, u32[]{:S(2)}, u32[]{:S(2)}) collective-permute-start(bf16[192,384]{1,0:T(8,128)(2,1)S(1)} %get-tuple-element.14), channel_id=1, source_target_pairs={{0,3},{1,4},{2,5},{3,6},{4,7},{5,0},{6,1},{7,2},{8,11},{9,12},{10,... | collective-permute-start | bytes 442376 | tf_op jit(solution)/shard_map/ppermute | solution.py:17
  18.0 9.1 %collective-permute-start.1 = (bf16[192,384]{1,0:T(8,128)(2,1)S(1)}, bf16[192,384]{1,0:T(8,128)(2,1)S(1)}, u32[]{:S(2)}, u32[]{:S(2)}) collective-permute-start(bf16[192,384]{1,0:T(8,128)(2,1)S(1)} %get-tuple-element.14), channel_id=1, source_target_pairs={{0,2},{1,3},{2,4},{3,5},{4,6},{5,7},{6,0},{7,1},{8,10},{9,11},{10,... | collective-permute-start | bytes 442376 | tf_op jit(solution)/shard_map/ppermute | solution.py:17
  28.6 14.0 %collective-permute-start.7 = (bf16[192,384]{1,0:T(8,128)(2,1)S(1)}, bf16[192,384]{1,0:T(8,128)(2,1)S(1)}, u32[]{:S(2)}, u32[]{:S(2)}) collective-permute-start(bf16[192,384]{1,0:T(8,128)(2,1)S(1)} %get-tuple-element.7), channel_id=1, source_target_pairs={{0,1},{1,2},{2,3},{3,4},{4,5},{5,6},{6,7},{7,0},{8,9},{9,10},{10,1... | collective-permute-start | bytes 442376 | tf_op jit(solution)/shard_map/ppermute | solution.py:17
  28.6 15.6 %collective-permute-start.12 = (bf16[192,384]{1,0:T(8,128)(2,1)S(1)}, bf16[192,384]{1,0:T(8,128)(2,1)S(1)}, u32[]{:S(2)}, u32[]{:S(2)}) collective-permute-start(bf16[192,384]{1,0:T(8,128)(2,1)S(1)} %get-tuple-element.7), channel_id=1, source_target_pairs={{0,6},{1,7},{2,0},{3,1},{4,2},{5,3},{6,4},{7,5},{8,14},{9,15},{10,... | collective-permute-start | bytes 442376 | tf_op jit(solution)/shard_map/ppermute | solution.py:17
  33.5 12.4 %collective-permute-start.11 = (bf16[192,384]{1,0:T(8,128)(2,1)S(1)}, bf16[192,384]{1,0:T(8,128)(2,1)S(1)}, u32[]{:S(2)}, u32[]{:S(2)}) collective-permute-start(bf16[192,384]{1,0:T(8,128)(2,1)S(1)} %get-tuple-element.7), channel_id=1, source_target_pairs={{0,5},{1,6},{2,7},{3,0},{4,1},{5,2},{6,3},{7,4},{8,13},{9,14},{10,... | collective-permute-start | bytes 442376 | tf_op jit(solution)/shard_map/ppermute | solution.py:17
  33.5 16.0 %collective-permute-start.10 = (bf16[192,384]{1,0:T(8,128)(2,1)S(1)}, bf16[192,384]{1,0:T(8,128)(2,1)S(1)}, u32[]{:S(2)}, u32[]{:S(2)}) collective-permute-start(bf16[192,384]{1,0:T(8,128)(2,1)S(1)} %get-tuple-element.7), channel_id=1, source_target_pairs={{0,4},{1,5},{2,6},{3,7},{4,0},{5,1},{6,2},{7,3},{8,12},{9,13},{10,... | collective-permute-start | bytes 442376 | tf_op jit(solution)/shard_map/ppermute | solution.py:17
  36.5 18.6 %collective-permute-start.9 = (bf16[192,384]{1,0:T(8,128)(2,1)S(1)}, bf16[192,384]{1,0:T(8,128)(2,1)S(1)}, u32[]{:S(2)}, u32[]{:S(2)}) collective-permute-start(bf16[192,384]{1,0:T(8,128)(2,1)S(1)} %get-tuple-element.7), channel_id=1, source_target_pairs={{0,3},{1,4},{2,5},{3,6},{4,7},{5,0},{6,1},{7,2},{8,11},{9,12},{10,... | collective-permute-start | bytes 442376 | tf_op jit(solution)/shard_map/ppermute | solution.py:17
  42.5 14.9 %collective-permute-start.13 = (bf16[192,384]{1,0:T(8,128)(2,1)S(1)}, bf16[192,384]{1,0:T(8,128)(2,1)S(1)}, u32[]{:S(2)}, u32[]{:S(2)}) collective-permute-start(bf16[192,384]{1,0:T(8,128)(2,1)S(1)} %get-tuple-element.7), channel_id=1, source_target_pairs={{0,7},{1,0},{2,1},{3,2},{4,3},{5,4},{6,5},{7,6},{8,15},{9,8},{10,9... | collective-permute-start | bytes 442376 | tf_op jit(solution)/shard_map/ppermute | solution.py:17
  44.2 18.4 %collective-permute-start.8 = (bf16[192,384]{1,0:T(8,128)(2,1)S(1)}, bf16[192,384]{1,0:T(8,128)(2,1)S(1)}, u32[]{:S(2)}, u32[]{:S(2)}) collective-permute-start(bf16[192,384]{1,0:T(8,128)(2,1)S(1)} %get-tuple-element.7), channel_id=1, source_target_pairs={{0,2},{1,3},{2,4},{3,5},{4,6},{5,7},{6,0},{7,1},{8,10},{9,11},{10,... | collective-permute-start | bytes 442376 | tf_op jit(solution)/shard_map/ppermute | solution.py:17
  45.9 19.3 %collective-permute-start.14 = (bf16[2,3,192,128]{3,2,1,0:T(8,128)(2,1)S(1)}, bf16[2,3,192,128]{3,2,1,0:T(8,128)(2,1)S(1)}, u32[]{:S(2)}, u32[]{:S(2)}) collective-permute-start(bf16[2,3,192,128]{3,2,1,0:T(8,128)(2,1)S(1)} %pad_maximum_fusion.1.rest_0_), channel_id=1, source_target_pairs={{0,32},{8,40},{16,48},{24,56},{32,64},{40,72},{48,80},{56,88},{64,... | collective-permute-start | bytes 884744 | tf_op jit(solution)/shard_map/ppermute | solution.py:17
  49.5 19.6 %collective-permute-start.17 = (bf16[2,3,192,128]{3,2,1,0:T(8,128)(2,1)S(1)}, bf16[2,3,192,128]{3,2,1,0:T(8,128)(2,1)S(1)}, u32[]{:S(2)}, u32[]{:S(2)}) collective-permute-start(bf16[2,3,192,128]{3,2,1,0:T(8,128)(2,1)S(1)} %pad_maximum_fusion.1.rest_0_), channel_id=1, source_target_pairs={{0,224},{8,232},{16,240},{24,248},{32,0},{40,8},{48,16},{56,24},{6... | collective-permute-start | bytes 884744 | tf_op jit(solution)/shard_map/ppermute | solution.py:17
  55.1 14.1 %collective-permute-start.15 = (bf16[2,3,192,128]{3,2,1,0:T(8,128)(2,1)S(1)}, bf16[2,3,192,128]{3,2,1,0:T(8,128)(2,1)S(1)}, u32[]{:S(2)}, u32[]{:S(2)}) collective-permute-start(bf16[2,3,192,128]{3,2,1,0:T(8,128)(2,1)S(1)} %pad_maximum_fusion.1.rest_0_), channel_id=1, source_target_pairs={{0,16},{8,24},{16,32},{24,40},{32,48},{40,56},{48,64},{56,72},{64,... | collective-permute-start | bytes 884744 | tf_op jit(solution)/shard_map/ppermute | solution.py:17
  57.5 11.8 %collective-permute-start.16 = (bf16[2,3,192,128]{3,2,1,0:T(8,128)(2,1)S(1)}, bf16[2,3,192,128]{3,2,1,0:T(8,128)(2,1)S(1)}, u32[]{:S(2)}, u32[]{:S(2)}) collective-permute-start(bf16[2,3,192,128]{3,2,1,0:T(8,128)(2,1)S(1)} %pad_maximum_fusion.1.rest_0_), channel_id=1, source_target_pairs={{0,240},{8,248},{16,0},{24,8},{32,16},{40,24},{48,32},{56,40},{64,... | collective-permute-start | bytes 884744 | tf_op jit(solution)/shard_map/ppermute | solution.py:17
  65.1 8.4 %collective-permute-start.22 = (bf16[2,3,192,128]{3,2,1,0:T(8,128)(2,1)S(1)}, bf16[2,3,192,128]{3,2,1,0:T(8,128)(2,1)S(1)}, u32[]{:S(2)}, u32[]{:S(2)}) collective-permute-start(bf16[2,3,192,128]{3,2,1,0:T(8,128)(2,1)S(1)} %pad_maximum_fusion.2.rest_9_), channel_id=1, source_target_pairs={{0,32},{8,40},{16,48},{24,56},{32,64},{40,72},{48,80},{56,88},{64,... | collective-permute-start | bytes 884744 | tf_op jit(solution)/shard_map/ppermute | solution.py:17
  65.2 8.3 %collective-permute-start.25 = (bf16[2,3,192,128]{3,2,1,0:T(8,128)(2,1)S(1)}, bf16[2,3,192,128]{3,2,1,0:T(8,128)(2,1)S(1)}, u32[]{:S(2)}, u32[]{:S(2)}) collective-permute-start(bf16[2,3,192,128]{3,2,1,0:T(8,128)(2,1)S(1)} %pad_maximum_fusion.2.rest_9_), channel_id=1, source_target_pairs={{0,224},{8,232},{16,240},{24,248},{32,0},{40,8},{48,16},{56,24},{6... | collective-permute-start | bytes 884744 | tf_op jit(solution)/shard_map/ppermute | solution.py:17
  69.2 13.6 %collective-permute-start.23 = (bf16[2,3,192,128]{3,2,1,0:T(8,128)(2,1)S(1)}, bf16[2,3,192,128]{3,2,1,0:T(8,128)(2,1)S(1)}, u32[]{:S(2)}, u32[]{:S(2)}) collective-permute-start(bf16[2,3,192,128]{3,2,1,0:T(8,128)(2,1)S(1)} %pad_maximum_fusion.2.rest_9_), channel_id=1, source_target_pairs={{0,16},{8,24},{16,32},{24,40},{32,48},{40,56},{48,64},{56,72},{64,... | collective-permute-start | bytes 884744 | tf_op jit(solution)/shard_map/ppermute | solution.py:17
  69.4 15.8 %collective-permute-start.24 = (bf16[2,3,192,128]{3,2,1,0:T(8,128)(2,1)S(1)}, bf16[2,3,192,128]{3,2,1,0:T(8,128)(2,1)S(1)}, u32[]{:S(2)}, u32[]{:S(2)}) collective-permute-start(bf16[2,3,192,128]{3,2,1,0:T(8,128)(2,1)S(1)} %pad_maximum_fusion.2.rest_9_), channel_id=1, source_target_pairs={{0,240},{8,248},{16,0},{24,8},{32,16},{40,24},{48,32},{56,40},{64,... | collective-permute-start | bytes 884744 | tf_op jit(solution)/shard_map/ppermute | solution.py:17
  73.5 11.7 %collective-permute-start.26 = (bf16[2,3,192,128]{3,2,1,0:T(8,128)(2,1)S(1)}, bf16[2,3,192,128]{3,2,1,0:T(8,128)(2,1)S(1)}, u32[]{:S(2)}, u32[]{:S(2)}) collective-permute-start(bf16[2,3,192,128]{3,2,1,0:T(8,128)(2,1)S(1)} %pad_maximum_fusion.2.rest_9_), channel_id=1, source_target_pairs={{0,8},{8,0},{16,24},{24,16},{32,40},{40,32},{48,56},{56,48},{64,72... | collective-permute-start | bytes 884744 | tf_op jit(solution)/shard_map/ppermute | solution.py:125
  73.5 12.2 %collective-permute-start.21 = (bf16[2,3,192,128]{3,2,1,0:T(8,128)(2,1)S(1)}, bf16[2,3,192,128]{3,2,1,0:T(8,128)(2,1)S(1)}, u32[]{:S(2)}, u32[]{:S(2)}) collective-permute-start(bf16[2,3,192,128]{3,2,1,0:T(8,128)(2,1)S(1)} %broadcast_select_fusion.1), channel_id=1, source_target_pairs={{0,8},{8,0},{16,24},{24,16},{32,40},{40,32},{48,56},{56,48},{64,72... | collective-permute-start | bytes 884744 | tf_op jit(solution)/shard_map/ppermute | solution.py:128
  74.9 12.5 %collective-permute-start.19 = (bf16[2,3,192,128]{3,2,1,0:T(8,128)(2,1)S(1)}, bf16[2,3,192,128]{3,2,1,0:T(8,128)(2,1)S(1)}, u32[]{:S(2)}, u32[]{:S(2)}) collective-permute-start(bf16[2,3,192,128]{3,2,1,0:T(8,128)(2,1)S(1)} %collective-permute-done.15.rest_2_), channel_id=1, source_target_pairs={{0,8},{8,0},{16,24},{24,16},{32,40},{40,32},{48,56},{56,48},{64,72... | collective-permute-start | bytes 884744 | tf_op jit(solution)/shard_map/ppermute | solution.py:126
  (28 other events, 333.4 us)

commit v8 on v4

--- a/solution.py
+++ b/solution.py
@@ -31,7 +31,7 @@
     factor = HD ** (-0.5)
     q_raw = q_ref[...]
     norm = lax.rsqrt(jnp.mean(q_raw * q_raw, axis=-1, keepdims=True) + 1e-06)
-    q = (q_raw * norm * gain_ref[...]).astype(jnp.bfloat16)
+    q = (q_raw * norm * gain_ref[...] * factor).astype(jnp.bfloat16)
     m_ref[...] = jnp.full(m_ref.shape, -jnp.inf, jnp.float32)
     l_ref[...] = jnp.zeros(l_ref.shape, jnp.float32)
     acc_ref[...] = jnp.zeros(acc_ref.shape, jnp.float32)
@@ -49,7 +49,7 @@
     for i in range(slots):
         @pl.when(mask_ref[i] > 0)
         def _():
-            p = jnp.exp((scores_of(i) - highest) * factor)
+            p = jnp.exp(scores_of(i) - highest)
             l_ref[...] = l_ref[...] + p
             acc_ref[...] = acc_ref[...] + jnp.dot(
                 p.astype(jnp.bfloat16), kv_refs[i][1], preferred_element_type=jnp.float32

time: 130 us -> 131 us (level)
  Pallas kernels: 8.65 us -> 12.6 us
  blocking collectives: 35.6 us -> 33.4 us
    pallas_call x1, Pallas kernels: 8.65 us -> 12.6 us  [attend(): pl.pallas_call(attend_kernel, grid_spec=pltpu.PrefetchScalarGridSpec(num_...]
    all_to_all x1, blocking collectives: 35.6 us -> 33.4 us  [on_device(): received = lax.all_to_all(terms, 'mp', 0, 0, tiled=True).astype(jnp.float32)]
where the time goes in v8:
time: 131 us; the launch traced here: 130 us
  waiting for transfers between devices  35.6 us (27%)
  blocking collectives  33.4 us (25%)
  starting transfers between devices  27.8 us (21%)
  matrix products  13.4 us (10%)
  Pallas kernels  12.6 us (10%)
  other arithmetic  3.64 us (3%)
  local copies, waits for them, and re-layouts  3.32 us (3%)
    ppermute x11, waiting for transfers between devices, passed_along(): return lax.ppermute(value, axis, pairs)  35.4 us
    all_to_all x1, blocking collectives, on_device(): received = lax.all_to_all(terms, 'mp', 0, 0, tiled=True).astype(jnp.float32)  33.4 us
    ppermute x11, starting transfers between devices, passed_along(): return lax.ppermute(value, axis, pairs)  27.7 us
    pallas_call x1, Pallas kernels, attend(): pl.pallas_call(attend_kernel, grid_spec=pltpu.PrefetchScalarGridSpec(num_...  12.6 us
    dot_general x7, matrix products, on_device(): jnp.einsum('tf,fjc->jtc', passed_along(tokens, 'mp', step), rows_of(sourc...  8.34 us
    dot_general x1, matrix products, on_device(): jnp.einsum('tk,kjc->jtc', attended, w_out.reshape(w_out.shape[0], mp_coun...  3.16 us
  transfers between devices with their start and end apart: 15, of which 6 were waited for; matrix products, arithmetic and copies ran while one was open for 10% of the time, Pallas kernels for 0%

profile of v8, /device:TPU:8, one launch (start us, length us, event | category | flops | bytes accessed | tf_op | source)
XLA Modules:
  0.0 130.1 jit_solution(1586341942895785871)
XLA Ops:
  0.0 4.8 %collective-permute-start.5 = (bf16[384,384]{1,0:T(8,128)(2,1)}, bf16[384,384]{1,0:T(8,128)(2,1)S(1)}, u32[]{:S(2)}, u32[]{:S(2)}) collective-permute-start(bf16[384,384]{1,0:T(8,128)(2,1)} %param.7), channel_id=1, source_target_pairs={{0,6},{1,7},{2,0},{3,1},{4,2},{5,3},{6,4},{7,5},{8,14},{9,15},{10,... | collective-permute-start | bytes 884744 | tf_op jit(solution)/shard_map/ppermute | solution.py:17
  4.8 1.3 collective-permute-start.4
  6.0 2.3 %collective-permute-start.3 = (bf16[384,384]{1,0:T(8,128)(2,1)}, bf16[384,384]{1,0:T(8,128)(2,1)S(1)}, u32[]{:S(2)}, u32[]{:S(2)}) collective-permute-start(bf16[384,384]{1,0:T(8,128)(2,1)} %param.7), channel_id=1, source_target_pairs={{0,4},{1,5},{2,6},{3,7},{4,0},{5,1},{6,2},{7,3},{8,12},{9,13},{10,... | collective-permute-start | bytes 884744 | tf_op jit(solution)/shard_map/ppermute | solution.py:17
  8.3 0.9 collective-permute-start.2
  9.2 1.8 %collective-permute-start = (bf16[384,384]{1,0:T(8,128)(2,1)}, bf16[384,384]{1,0:T(8,128)(2,1)S(1)}, u32[]{:S(2)}, u32[]{:S(2)}) collective-permute-start(bf16[384,384]{1,0:T(8,128)(2,1)} %param.7), channel_id=1, source_target_pairs={{0,1},{1,2},{2,3},{3,4},{4,5},{5,6},{6,7},{7,0},{8,9},{9,10},{10,1... | collective-permute-start | bytes 884744 | tf_op jit(solution)/shard_map/ppermute | solution.py:17
  11.0 1.9 %fusion.21 = f32[3,384,384]{1,2,0:T(8,128)S(1)} fusion(bf16[3072,3,384]{2,0,1:T(8,128)(2,1)} %param.8, s32[]{:T(128)S(6)} %select_n.101, bf16[384,384]{1,0:T(8,128)(2,1)} %param.7), kind=kOutput, calls=%fused_computation.19 | convolution fusion | flops 339738624 | bytes 2949124 | tf_op jit(solution)/shard_map/tf,fjc->jtc/dot_general | solution.py:101
  13.1 6.4 %collective-permute-start.1 = (bf16[384,384]{1,0:T(8,128)(2,1)S(1)}, bf16[384,384]{1,0:T(8,128)(2,1)S(1)}, u32[]{:S(2)}, u32[]{:S(2)}) collective-permute-start(bf16[384,384]{1,0:T(8,128)(2,1)S(1)} %copy-done.8), channel_id=1, source_target_pairs={{0,2},{1,3},{2,4},{3,5},{4,6},{5,7},{6,0},{7,1},{8,10},{9,11},{10,... | collective-permute-start | bytes 884744 | tf_op jit(solution)/shard_map/ppermute | solution.py:17
  19.5 2.0 %fusion.9 = f32[3,384,384]{1,2,0:T(8,128)S(1)} fusion(bf16[3072,3,384]{2,0,1:T(8,128)(2,1)} %param.8, s32[]{:T(128)S(6)} %select_n.113, bf16[384,384]{1,0:T(8,128)(2,1)S(1)} %collective-permute-done.5), kind=kOutput, calls=%fused_computation.7 | convolution fusion | flops 339738624 | bytes 2949124 | tf_op jit(solution)/shard_map/tf,fjc->jtc/dot_general | solution.py:106
  21.5 7.7 %collective-permute-done = bf16[384,384]{1,0:T(8,128)(2,1)S(1)} collective-permute-done((bf16[384,384]{1,0:T(8,128)(2,1)}, bf16[384,384]{1,0:T(8,128)(2,1)S(1)}, u32[]{:S(2)}, u32[]{:S(2)}) %collective-permute-start) | collective-permute-done | bytes 294944 | tf_op jit(solution)/shard_map/ppermute | solution.py:17
  29.4 1.8 %fusion.19 = f32[3,384,384]{1,2,0:T(8,128)S(1)} fusion(bf16[3072,3,384]{2,0,1:T(8,128)(2,1)} %param.8, s32[]{:T(128)S(6)} %select_n.103, bf16[384,384]{1,0:T(8,128)(2,1)S(1)} %collective-permute-done), kind=kOutput, calls=%fused_computation.17 | convolution fusion | flops 339738624 | bytes 2949124 | tf_op jit(solution)/shard_map/tf,fjc->jtc/dot_general | solution.py:106
  31.3 3.1 %collective-permute-done.1 = bf16[384,384]{1,0:T(8,128)(2,1)S(1)} collective-permute-done((bf16[384,384]{1,0:T(8,128)(2,1)S(1)}, bf16[384,384]{1,0:T(8,128)(2,1)S(1)}, u32[]{:S(2)}, u32[]{:S(2)}) %collective-permute-start.1) | collective-permute-done | bytes 294944 | tf_op jit(solution)/shard_map/ppermute | solution.py:17
  34.3 1.8 %fusion.17 = f32[3,384,384]{1,2,0:T(8,128)S(1)} fusion(bf16[3072,3,384]{2,0,1:T(8,128)(2,1)} %param.8, s32[]{:T(128)S(6)} %select_n.105, bf16[384,384]{1,0:T(8,128)(2,1)S(1)} %collective-permute-done.1), kind=kOutput, calls=%fused_computation.15 | convolution fusion | flops 339738624 | bytes 2949124 | tf_op jit(solution)/shard_map/tf,fjc->jtc/dot_general | solution.py:106
  39.0 0.9 fusion.42
  41.2 1.0 collective-permute-start.9
  42.3 2.0 %collective-permute-start.8 = (bf16[2,3,384,128]{3,2,1,0:T(8,128)(2,1)S(1)}, bf16[2,3,384,128]{3,2,1,0:T(8,128)(2,1)S(1)}, u32[]{:S(2)}, u32[]{:S(2)}) collective-permute-start(bf16[2,3,384,128]{3,2,1,0:T(8,128)(2,1)S(1)} %pad_maximum_fusion.rest_0_), channel_id=1, source_target_pairs={{0,16},{8,24},{16,32},{24,40},{32,48},{40,56},{48,64},{56,72},{64,... | collective-permute-start | bytes 1769480 | tf_op jit(solution)/shard_map/ppermute | solution.py:17
  44.2 7.1 %collective-permute-start.10 = (bf16[2,3,384,128]{3,2,1,0:T(8,128)(2,1)S(1)}, bf16[2,3,384,128]{3,2,1,0:T(8,128)(2,1)S(1)}, u32[]{:S(2)}, u32[]{:S(2)}) collective-permute-start(bf16[2,3,384,128]{3,2,1,0:T(8,128)(2,1)S(1)} %pad_maximum_fusion.rest_0_), channel_id=1, source_target_pairs={{0,224},{8,232},{16,240},{24,248},{32,0},{40,8},{48,16},{56,24},{6... | collective-permute-start | bytes 1769480 | tf_op jit(solution)/shard_map/ppermute | solution.py:17
  51.3 15.4 %collective-permute-done.9.rest_3_ = bf16[2,3,384,128]{3,2,1,0:T(8,128)(2,1)S(1)} collective-permute-done((bf16[2,3,384,128]{3,2,1,0:T(8,128)(2,1)S(1)}, bf16[2,3,384,128]{3,2,1,0:T(8,128)(2,1)S(1)}, u32[]{:S(2)}, u32[]{:S(2)}) %collective-permute-start.9) | collective-permute-done | bytes 589856 | tf_op jit(solution)/shard_map/ppermute | solution.py:17
  66.7 2.4 %collective-permute-done.8.rest_2_ = bf16[2,3,384,128]{3,2,1,0:T(8,128)(2,1)S(1)} collective-permute-done((bf16[2,3,384,128]{3,2,1,0:T(8,128)(2,1)S(1)}, bf16[2,3,384,128]{3,2,1,0:T(8,128)(2,1)S(1)}, u32[]{:S(2)}, u32[]{:S(2)}) %collective-permute-start.8) | collective-permute-done | bytes 589856 | tf_op jit(solution)/shard_map/ppermute | solution.py:17
  69.1 6.8 %collective-permute-done.7.rest_1_ = bf16[2,3,384,128]{3,2,1,0:T(8,128)(2,1)S(1)} collective-permute-done((bf16[2,3,384,128]{3,2,1,0:T(8,128)(2,1)S(1)}, bf16[2,3,384,128]{3,2,1,0:T(8,128)(2,1)S(1)}, u32[]{:S(2)}, u32[]{:S(2)}) %collective-permute-start.7) | collective-permute-done | bytes 589856 | tf_op jit(solution)/shard_map/ppermute | solution.py:17
  76.0 0.9 broadcast_select_fusion
  79.9 12.6 %shard_map.73 = bf16[384,384]{1,0:T(8,128)(2,1)} custom-call(s32[9]{0:T(128)} %convert_element_type.19.mask_ref, f32[384,384]{1,0:T(8,128)} %get-tuple-element.6.q_ref, f32[1,128]{1,0:T(1,128)} %bitcast.58, bf16[2,3,384,128]{3,2,1,0:T(8,128)(2,1)} %copy-done.2, bf16[2,3,384,128]{3,2,1,0:T(8,128)(2,1)} %copy-done.4, bf16[2,3,384,128]{3,2,1,0:T(8,128)(2,1)} %copy-done.6, ...), custom_call_target="tpu_custom_call" | custom-call | tf_op jit(solution)/shard_map/pallas_call | solution.py:67
  92.5 3.2 %convert_bitcast_fusion = bf16[8,384,384]{2,1,0:T(8,128)(2,1)S(1)} fusion(bf16[48,8,8,384]{3,2,1,0:T(8,128)(2,1)} %bitcast.59, bf16[384,384]{1,0:T(8,128)(2,1)} %shard_map.73), kind=kOutput, calls=%fused_computation.3 | convolution fusion | flops 907149312 | bytes 5013504 | tf_op jit(solution)/shard_map/tk,kjc->jtc/dot_general | solution.py:151
  95.6 33.4 %all_to_all.5 = bf16[8,384,384]{2,1,0:T(8,128)(2,1)S(1)} all-to-all(bf16[8,384,384]{2,1,0:T(8,128)(2,1)S(1)} %convert_bitcast_fusion), channel_id=1, replica_groups=mesh['seq'=32,'mp'=8] {'mp'}, dimensions={0} | all-to-all | bytes 4718592 | tf_op jit(solution)/shard_map/all_to_all | solution.py:157
  129.0 1.1 reduce_sum.22
  (58 shorter events, 7.3 us)
Async XLA Ops:
  0.0 77.5 %copy-start = (s32[32,6]{0,1:T(8,128)S(1)}, s32[32,6]{0,1:T(8,128)}, u32[]{:S(2)}) copy-start(s32[32,6]{0,1:T(8,128)} %param.12) | copy-start | bytes 2308
  0.0 13.1 %copy-start.8 = (bf16[384,384]{1,0:T(8,128)(2,1)S(1)}, bf16[384,384]{1,0:T(8,128)(2,1)}, u32[]{:S(2)}) copy-start(bf16[384,384]{1,0:T(8,128)(2,1)} %param.7) | copy-start | bytes 884740
  0.0 13.1 %collective-permute-start.5 = (bf16[384,384]{1,0:T(8,128)(2,1)}, bf16[384,384]{1,0:T(8,128)(2,1)S(1)}, u32[]{:S(2)}, u32[]{:S(2)}) collective-permute-start(bf16[384,384]{1,0:T(8,128)(2,1)} %param.7), channel_id=1, source_target_pairs={{0,6},{1,7},{2,0},{3,1},{4,2},{5,3},{6,4},{7,5},{8,14},{9,15},{10,... | collective-permute-start | bytes 884744 | tf_op jit(solution)/shard_map/ppermute | solution.py:17
  4.8 32.7 %collective-permute-start.4 = (bf16[384,384]{1,0:T(8,128)(2,1)}, bf16[384,384]{1,0:T(8,128)(2,1)S(1)}, u32[]{:S(2)}, u32[]{:S(2)}) collective-permute-start(bf16[384,384]{1,0:T(8,128)(2,1)} %param.7), channel_id=1, source_target_pairs={{0,5},{1,6},{2,7},{3,0},{4,1},{5,2},{6,3},{7,4},{8,13},{9,14},{10,... | collective-permute-start | bytes 884744 | tf_op jit(solution)/shard_map/ppermute | solution.py:17
  6.0 30.8 %collective-permute-start.3 = (bf16[384,384]{1,0:T(8,128)(2,1)}, bf16[384,384]{1,0:T(8,128)(2,1)S(1)}, u32[]{:S(2)}, u32[]{:S(2)}) collective-permute-start(bf16[384,384]{1,0:T(8,128)(2,1)} %param.7), channel_id=1, source_target_pairs={{0,4},{1,5},{2,6},{3,7},{4,0},{5,1},{6,2},{7,3},{8,12},{9,13},{10,... | collective-permute-start | bytes 884744 | tf_op jit(solution)/shard_map/ppermute | solution.py:17
  8.3 27.8 %collective-permute-start.2 = (bf16[384,384]{1,0:T(8,128)(2,1)}, bf16[384,384]{1,0:T(8,128)(2,1)S(1)}, u32[]{:S(2)}, u32[]{:S(2)}) collective-permute-start(bf16[384,384]{1,0:T(8,128)(2,1)} %param.7), channel_id=1, source_target_pairs={{0,3},{1,4},{2,5},{3,6},{4,7},{5,0},{6,1},{7,2},{8,11},{9,12},{10,... | collective-permute-start | bytes 884744 | tf_op jit(solution)/shard_map/ppermute | solution.py:17
  9.2 20.0 %collective-permute-start = (bf16[384,384]{1,0:T(8,128)(2,1)}, bf16[384,384]{1,0:T(8,128)(2,1)S(1)}, u32[]{:S(2)}, u32[]{:S(2)}) collective-permute-start(bf16[384,384]{1,0:T(8,128)(2,1)} %param.7), channel_id=1, source_target_pairs={{0,1},{1,2},{2,3},{3,4},{4,5},{5,6},{6,7},{7,0},{8,9},{9,10},{10,1... | collective-permute-start | bytes 884744 | tf_op jit(solution)/shard_map/ppermute | solution.py:17
  13.1 21.2 %collective-permute-start.1 = (bf16[384,384]{1,0:T(8,128)(2,1)S(1)}, bf16[384,384]{1,0:T(8,128)(2,1)S(1)}, u32[]{:S(2)}, u32[]{:S(2)}) collective-permute-start(bf16[384,384]{1,0:T(8,128)(2,1)S(1)} %copy-done.8), channel_id=1, source_target_pairs={{0,2},{1,3},{2,4},{3,5},{4,6},{5,7},{6,0},{7,1},{8,10},{9,11},{10,... | collective-permute-start | bytes 884744 | tf_op jit(solution)/shard_map/ppermute | solution.py:17
  19.5 16.6 %copy-start.1 = (bf16[3072,3,384]{2,0,1:T(8,128)(2,1)S(1)}, bf16[3072,3,384]{2,0,1:T(8,128)(2,1)}, u32[]{:S(2)}) copy-start(bf16[3072,3,384]{2,0,1:T(8,128)(2,1)} %param.8) | copy-start | bytes 21233668
  29.2 8.9 %collective-permute-start.6 = (bf16[384,384]{1,0:T(8,128)(2,1)S(1)}, bf16[384,384]{1,0:T(8,128)(2,1)S(1)}, u32[]{:S(2)}, u32[]{:S(2)}) collective-permute-start(bf16[384,384]{1,0:T(8,128)(2,1)S(1)} %copy-done.8), channel_id=1, source_target_pairs={{0,7},{1,0},{2,1},{3,2},{4,3},{5,4},{6,5},{7,6},{8,15},{9,8},{10,9... | collective-permute-start | bytes 884744 | tf_op jit(solution)/shard_map/ppermute | solution.py:17
  40.9 36.0 %copy-start.10 = (s32[32]{0:T(128)S(1)}, s32[32]{0:T(128)}, u32[]{:S(2)}) copy-start(s32[32]{0:T(128)} %param.13) | copy-start | bytes 388
  41.2 38.0 %copy-start.2 = (bf16[2,3,384,128]{3,2,1,0:T(8,128)(2,1)}, bf16[2,3,384,128]{3,2,1,0:T(8,128)(2,1)S(1)}, u32[]{:S(2)}) copy-start(bf16[2,3,384,128]{3,2,1,0:T(8,128)(2,1)S(1)} %pad_maximum_fusion.rest_0_) | copy-start | bytes 1769476
  41.2 25.4 %collective-permute-start.9 = (bf16[2,3,384,128]{3,2,1,0:T(8,128)(2,1)S(1)}, bf16[2,3,384,128]{3,2,1,0:T(8,128)(2,1)S(1)}, u32[]{:S(2)}, u32[]{:S(2)}) collective-permute-start(bf16[2,3,384,128]{3,2,1,0:T(8,128)(2,1)S(1)} %pad_maximum_fusion.rest_0_), channel_id=1, source_target_pairs={{0,240},{8,248},{16,0},{24,8},{32,16},{40,24},{48,32},{56,40},{64,... | collective-permute-start | bytes 1769480 | tf_op jit(solution)/shard_map/ppermute | solution.py:17
  42.3 26.9 %collective-permute-start.8 = (bf16[2,3,384,128]{3,2,1,0:T(8,128)(2,1)S(1)}, bf16[2,3,384,128]{3,2,1,0:T(8,128)(2,1)S(1)}, u32[]{:S(2)}, u32[]{:S(2)}) collective-permute-start(bf16[2,3,384,128]{3,2,1,0:T(8,128)(2,1)S(1)} %pad_maximum_fusion.rest_0_), channel_id=1, source_target_pairs={{0,16},{8,24},{16,32},{24,40},{32,48},{40,56},{48,64},{56,72},{64,... | collective-permute-start | bytes 1769480 | tf_op jit(solution)/shard_map/ppermute | solution.py:17
  44.2 24.9 %collective-permute-start.10 = (bf16[2,3,384,128]{3,2,1,0:T(8,128)(2,1)S(1)}, bf16[2,3,384,128]{3,2,1,0:T(8,128)(2,1)S(1)}, u32[]{:S(2)}, u32[]{:S(2)}) collective-permute-start(bf16[2,3,384,128]{3,2,1,0:T(8,128)(2,1)S(1)} %pad_maximum_fusion.rest_0_), channel_id=1, source_target_pairs={{0,224},{8,232},{16,240},{24,248},{32,0},{40,8},{48,16},{56,24},{6... | collective-permute-start | bytes 1769480 | tf_op jit(solution)/shard_map/ppermute | solution.py:17
  51.3 24.6 %collective-permute-start.7 = (bf16[2,3,384,128]{3,2,1,0:T(8,128)(2,1)S(1)}, bf16[2,3,384,128]{3,2,1,0:T(8,128)(2,1)S(1)}, u32[]{:S(2)}, u32[]{:S(2)}) collective-permute-start(bf16[2,3,384,128]{3,2,1,0:T(8,128)(2,1)S(1)} %pad_maximum_fusion.rest_0_), channel_id=1, source_target_pairs={{0,32},{8,40},{16,48},{24,56},{32,64},{40,72},{48,80},{56,88},{64,... | collective-permute-start | bytes 1769480 | tf_op jit(solution)/shard_map/ppermute | solution.py:17
  51.3 27.7 %collective-permute-start.11 = (bf16[2,3,384,128]{3,2,1,0:T(8,128)(2,1)S(1)}, bf16[2,3,384,128]{3,2,1,0:T(8,128)(2,1)S(1)}, u32[]{:S(2)}, u32[]{:S(2)}) collective-permute-start(bf16[2,3,384,128]{3,2,1,0:T(8,128)(2,1)S(1)} %pad_maximum_fusion.rest_0_), channel_id=1, source_target_pairs={{0,8},{8,0},{16,24},{24,16},{32,40},{40,32},{48,56},{56,48},{64,72... | collective-permute-start | bytes 1769480 | tf_op jit(solution)/shard_map/ppermute | solution.py:123
  66.7 12.6 %copy-start.5 = (bf16[2,3,384,128]{3,2,1,0:T(8,128)(2,1)}, bf16[2,3,384,128]{3,2,1,0:T(8,128)(2,1)S(1)}, u32[]{:S(2)}) copy-start(bf16[2,3,384,128]{3,2,1,0:T(8,128)(2,1)S(1)} %collective-permute-done.9.rest_3_) | copy-start | bytes 1769476
  66.7 12.4 %collective-permute-start.13 = (bf16[2,3,384,128]{3,2,1,0:T(8,128)(2,1)S(1)}, bf16[2,3,384,128]{3,2,1,0:T(8,128)(2,1)}, u32[]{:S(2)}, u32[]{:S(2)}) collective-permute-start(bf16[2,3,384,128]{3,2,1,0:T(8,128)(2,1)S(1)} %collective-permute-done.9.rest_3_), channel_id=1, source_target_pairs={{0,8},{8,0},{16,24},{24,16},{32,40},{40,32},{48,56},{56,48},{64,72... | collective-permute-start | bytes 1769480 | tf_op jit(solution)/shard_map/ppermute | solution.py:125
  69.1 10.1 %copy-start.6 = (bf16[2,3,384,128]{3,2,1,0:T(8,128)(2,1)}, bf16[2,3,384,128]{3,2,1,0:T(8,128)(2,1)S(1)}, u32[]{:S(2)}) copy-start(bf16[2,3,384,128]{3,2,1,0:T(8,128)(2,1)S(1)} %collective-permute-done.8.rest_2_) | copy-start | bytes 1769476
  69.1 9.9 %collective-permute-start.12 = (bf16[2,3,384,128]{3,2,1,0:T(8,128)(2,1)S(1)}, bf16[2,3,384,128]{3,2,1,0:T(8,128)(2,1)}, u32[]{:S(2)}, u32[]{:S(2)}) collective-permute-start(bf16[2,3,384,128]{3,2,1,0:T(8,128)(2,1)S(1)} %collective-permute-done.8.rest_2_), channel_id=1, source_target_pairs={{0,8},{8,0},{16,24},{24,16},{32,40},{40,32},{48,56},{56,48},{64,72... | collective-permute-start | bytes 1769480 | tf_op jit(solution)/shard_map/ppermute | solution.py:124
  69.1 10.1 %copy-start.3 = (bf16[2,3,384,128]{3,2,1,0:T(8,128)(2,1)}, bf16[2,3,384,128]{3,2,1,0:T(8,128)(2,1)S(1)}, u32[]{:S(2)}) copy-start(bf16[2,3,384,128]{3,2,1,0:T(8,128)(2,1)S(1)} %collective-permute-done.10.rest_4_) | copy-start | bytes 1769476
  76.0 3.3 %copy-start.4 = (bf16[2,3,384,128]{3,2,1,0:T(8,128)(2,1)}, bf16[2,3,384,128]{3,2,1,0:T(8,128)(2,1)S(1)}, u32[]{:S(2)}) copy-start(bf16[2,3,384,128]{3,2,1,0:T(8,128)(2,1)S(1)} %collective-permute-done.7.rest_1_) | copy-start | bytes 1769476
  76.9 2.3 %collective-permute-start.14 = (bf16[2,3,384,128]{3,2,1,0:T(8,128)(2,1)}, bf16[2,3,384,128]{3,2,1,0:T(8,128)(2,1)}, u32[]{:S(2)}, u32[]{:S(2)}) collective-permute-start(bf16[2,3,384,128]{3,2,1,0:T(8,128)(2,1)} %broadcast_select_fusion), channel_id=1, source_target_pairs={{0,8},{8,0},{16,24},{24,16},{32,40},{40,32},{48,56},{56,48},{64,72... | collective-permute-start | bytes 1769480 | tf_op jit(solution)/shard_map/ppermute | solution.py:126
  (2 other events, 1.6 us)

commit v9 on v4

--- a/solution.py
+++ b/solution.py
@@ -123,8 +123,9 @@
     fwd_own = lax.ppermute(paired, "seq", partner)
     fwd_a = lax.ppermute(from_m2, "seq", partner)
     fwd_b = lax.ppermute(from_p2, "seq", partner)
-    fwd_c = lax.ppermute(jnp.where(core == 0, from_p4, from_m4), "seq", partner)
-    kv_tiles = [paired, from_m4, from_m2, from_p2, from_p4, fwd_own, fwd_a, fwd_b, fwd_c]
+    fwd_even = lax.ppermute(from_m4, "seq", [(s, s ^ 1) for s in range(1, seq_count, 2)])
+    fwd_odd = lax.ppermute(from_p4, "seq", [(s, s ^ 1) for s in range(0, seq_count, 2)])
+    kv_tiles = [paired, from_m4, from_m2, from_p2, from_p4, fwd_own, fwd_a, fwd_b, fwd_even, fwd_odd]
     odd = core == 1
     slot_offsets = jnp.stack(
         [
@@ -136,10 +137,13 @@
             jnp.where(odd, -1, 1).astype(jnp.int32),
             jnp.where(odd, -3, -1).astype(jnp.int32),
             jnp.where(odd, 1, 3).astype(jnp.int32),
-            jnp.where(odd, 3, -3).astype(jnp.int32),
+            jnp.int32(-3),
+            jnp.int32(3),
         ]
     )
     slot_tile = jnp.mod(position + slot_offsets, total_tiles)
+    slot_tile = slot_tile.at[8].set(jnp.where(odd, -1, slot_tile[8]))
+    slot_tile = slot_tile.at[9].set(jnp.where(odd, slot_tile[9], -1))
     listed = lax.dynamic_slice_in_dim(neighbours, position, 1, 0)
     used_counts = lax.dynamic_slice_in_dim(counts, position, 1, 0)
     slot_used = jnp.arange(NB, dtype=jnp.int32)[None, :] < used_counts[:, None]

time: 130 us -> 136 us (1.046)
  starting transfers between devices: 27.8 us -> 29.9 us
  Pallas kernels: 8.65 us -> 10.7 us
  between operations: 0.42 us -> 1.79 us
    ppermute x1 -> x2, starting transfers between devices: 0.01 us -> 3.4 us  [the longest x1 2.12 us: on_device(): lax.ppermute(from_p4, 'seq', [(s, s ^ 1) for s in range(0, seq_count, 2)])]
    pallas_call x1, Pallas kernels: 8.65 us -> 10.7 us  [attend(): pl.pallas_call(attend_kernel, grid_spec=pltpu.PrefetchScalarGridSpec(num_...]
  transfers between devices with their start and end apart: 15 -> 16, of which waited for: 6 -> 6; matrix products, arithmetic and copies ran while one was open for 10% -> 9% of each run, Pallas kernels for 0% -> 0%
where the time goes in v9:
time: 136 us; the launch traced here: 135 us
  blocking collectives  36.8 us (27%)
  waiting for transfers between devices  35.2 us (26%)
  starting transfers between devices  29.9 us (22%)
  matrix products  13.4 us (10%)
  Pallas kernels  10.7 us (8%)
  local copies, waits for them, and re-layouts  4.67 us (3%)
  other arithmetic  2.78 us (2%)
  between operations  1.79 us (1%)
    all_to_all x1, blocking collectives, on_device(): received = lax.all_to_all(terms, 'mp', 0, 0, tiled=True).astype(jnp.float32)  36.8 us
    ppermute x11, waiting for transfers between devices, passed_along(): return lax.ppermute(value, axis, pairs)  35.2 us
    ppermute x11, starting transfers between devices, passed_along(): return lax.ppermute(value, axis, pairs)  26.5 us
    pallas_call x1, Pallas kernels, attend(): pl.pallas_call(attend_kernel, grid_spec=pltpu.PrefetchScalarGridSpec(num_...  10.7 us
    dot_general x7, matrix products, on_device(): jnp.einsum('tf,fjc->jtc', passed_along(tokens, 'mp', step), rows_of(sourc...  8.34 us
    dot_general x1, matrix products, on_device(): jnp.einsum('tk,kjc->jtc', attended, w_out.reshape(w_out.shape[0], mp_coun...  3.16 us
  transfers between devices with their start and end apart: 16, of which 6 were waited for; matrix products, arithmetic and copies ran while one was open for 9% of the time, Pallas kernels for 0%

profile of v9, /device:TPU:8, one launch (start us, length us, event | category | flops | bytes accessed | tf_op | source)
XLA Modules:
  0.0 135.3 jit_solution(9584615355418065238)
XLA Ops:
  0.0 4.8 %collective-permute-start.5 = (bf16[384,384]{1,0:T(8,128)(2,1)}, bf16[384,384]{1,0:T(8,128)(2,1)S(1)}, u32[]{:S(2)}, u32[]{:S(2)}) collective-permute-start(bf16[384,384]{1,0:T(8,128)(2,1)} %param.11), channel_id=1, source_target_pairs={{0,6},{1,7},{2,0},{3,1},{4,2},{5,3},{6,4},{7,5},{8,14},{9,15},{10,... | collective-permute-start | bytes 884744 | tf_op jit(solution)/shard_map/ppermute | solution.py:17
  4.8 1.3 collective-permute-start.4
  6.0 2.3 %collective-permute-start.3 = (bf16[384,384]{1,0:T(8,128)(2,1)}, bf16[384,384]{1,0:T(8,128)(2,1)S(1)}, u32[]{:S(2)}, u32[]{:S(2)}) collective-permute-start(bf16[384,384]{1,0:T(8,128)(2,1)} %param.11), channel_id=1, source_target_pairs={{0,4},{1,5},{2,6},{3,7},{4,0},{5,1},{6,2},{7,3},{8,12},{9,13},{10,... | collective-permute-start | bytes 884744 | tf_op jit(solution)/shard_map/ppermute | solution.py:17
  9.2 1.8 %collective-permute-start = (bf16[384,384]{1,0:T(8,128)(2,1)}, bf16[384,384]{1,0:T(8,128)(2,1)S(1)}, u32[]{:S(2)}, u32[]{:S(2)}) collective-permute-start(bf16[384,384]{1,0:T(8,128)(2,1)} %param.11), channel_id=1, source_target_pairs={{0,1},{1,2},{2,3},{3,4},{4,5},{5,6},{6,7},{7,0},{8,9},{9,10},{10,1... | collective-permute-start | bytes 884744 | tf_op jit(solution)/shard_map/ppermute | solution.py:17
  11.0 1.9 %fusion.21 = f32[3,384,384]{1,2,0:T(8,128)S(1)} fusion(bf16[3072,3,384]{2,0,1:T(8,128)(2,1)} %param.12, s32[]{:T(128)S(6)} %select_n.95, bf16[384,384]{1,0:T(8,128)(2,1)} %param.11), kind=kOutput, calls=%fused_computation.19 | convolution fusion | flops 339738624 | bytes 2949124 | tf_op jit(solution)/shard_map/tf,fjc->jtc/dot_general | solution.py:101
  13.1 6.4 %collective-permute-start.1 = (bf16[384,384]{1,0:T(8,128)(2,1)S(1)}, bf16[384,384]{1,0:T(8,128)(2,1)S(1)}, u32[]{:S(2)}, u32[]{:S(2)}) collective-permute-start(bf16[384,384]{1,0:T(8,128)(2,1)S(1)} %copy-done.8), channel_id=1, source_target_pairs={{0,2},{1,3},{2,4},{3,5},{4,6},{5,7},{6,0},{7,1},{8,10},{9,11},{10,... | collective-permute-start | bytes 884744 | tf_op jit(solution)/shard_map/ppermute | solution.py:17
  19.5 2.0 %fusion.9 = f32[3,384,384]{1,2,0:T(8,128)S(1)} fusion(bf16[3072,3,384]{2,0,1:T(8,128)(2,1)} %param.12, s32[]{:T(128)S(6)} %select_n.107, bf16[384,384]{1,0:T(8,128)(2,1)S(1)} %collective-permute-done.5), kind=kOutput, calls=%fused_computation.7 | convolution fusion | flops 339738624 | bytes 2949124 | tf_op jit(solution)/shard_map/tf,fjc->jtc/dot_general | solution.py:106
  21.5 7.7 %collective-permute-done = bf16[384,384]{1,0:T(8,128)(2,1)S(1)} collective-permute-done((bf16[384,384]{1,0:T(8,128)(2,1)}, bf16[384,384]{1,0:T(8,128)(2,1)S(1)}, u32[]{:S(2)}, u32[]{:S(2)}) %collective-permute-start) | collective-permute-done | bytes 294944 | tf_op jit(solution)/shard_map/ppermute | solution.py:17
  29.4 1.8 %fusion.19 = f32[3,384,384]{1,2,0:T(8,128)S(1)} fusion(bf16[3072,3,384]{2,0,1:T(8,128)(2,1)} %param.12, s32[]{:T(128)S(6)} %select_n.97, bf16[384,384]{1,0:T(8,128)(2,1)S(1)} %collective-permute-done), kind=kOutput, calls=%fused_computation.17 | convolution fusion | flops 339738624 | bytes 2949124 | tf_op jit(solution)/shard_map/tf,fjc->jtc/dot_general | solution.py:106
  31.3 3.1 %collective-permute-done.1 = bf16[384,384]{1,0:T(8,128)(2,1)S(1)} collective-permute-done((bf16[384,384]{1,0:T(8,128)(2,1)S(1)}, bf16[384,384]{1,0:T(8,128)(2,1)S(1)}, u32[]{:S(2)}, u32[]{:S(2)}) %collective-permute-start.1) | collective-permute-done | bytes 294944 | tf_op jit(solution)/shard_map/ppermute | solution.py:17
  34.3 1.8 %fusion.17 = f32[3,384,384]{1,2,0:T(8,128)S(1)} fusion(bf16[3072,3,384]{2,0,1:T(8,128)(2,1)} %param.12, s32[]{:T(128)S(6)} %select_n.99, bf16[384,384]{1,0:T(8,128)(2,1)S(1)} %collective-permute-done.1), kind=kOutput, calls=%fused_computation.15 | convolution fusion | flops 339738624 | bytes 2949124 | tf_op jit(solution)/shard_map/tf,fjc->jtc/dot_general | solution.py:106
  41.2 5.9 %collective-permute-start.10 = (bf16[2,3,384,128]{3,2,1,0:T(8,128)(2,1)S(1)}, bf16[2,3,384,128]{3,2,1,0:T(8,128)(2,1)S(1)}, u32[]{:S(2)}, u32[]{:S(2)}) collective-permute-start(bf16[2,3,384,128]{3,2,1,0:T(8,128)(2,1)S(1)} %pad_maximum_fusion.rest_0_), channel_id=1, source_target_pairs={{0,224},{8,232},{16,240},{24,248},{32,0},{40,8},{48,16},{56,24},{6... | collective-permute-start | bytes 1769480 | tf_op jit(solution)/shard_map/ppermute | solution.py:17
  47.2 0.9 collective-permute-start.9
  48.1 2.0 %collective-permute-start.8 = (bf16[2,3,384,128]{3,2,1,0:T(8,128)(2,1)S(1)}, bf16[2,3,384,128]{3,2,1,0:T(8,128)(2,1)S(1)}, u32[]{:S(2)}, u32[]{:S(2)}) collective-permute-start(bf16[2,3,384,128]{3,2,1,0:T(8,128)(2,1)S(1)} %pad_maximum_fusion.rest_0_), channel_id=1, source_target_pairs={{0,16},{8,24},{16,32},{24,40},{32,48},{40,56},{48,64},{56,72},{64,... | collective-permute-start | bytes 1769480 | tf_op jit(solution)/shard_map/ppermute | solution.py:17
  50.1 8.8 %collective-permute-done.10.rest_4_ = bf16[2,3,384,128]{3,2,1,0:T(8,128)(2,1)S(1)} collective-permute-done((bf16[2,3,384,128]{3,2,1,0:T(8,128)(2,1)S(1)}, bf16[2,3,384,128]{3,2,1,0:T(8,128)(2,1)S(1)}, u32[]{:S(2)}, u32[]{:S(2)}) %collective-permute-start.10) | collective-permute-done | bytes 589856 | tf_op jit(solution)/shard_map/ppermute | solution.py:17
  58.9 2.1 %collective-permute-start.15 = (bf16[2,3,384,128]{3,2,1,0:T(8,128)(2,1)S(1)}, bf16[2,3,384,128]{3,2,1,0:T(8,128)(2,1)}, u32[]{:S(2)}, u32[]{:S(2)}) collective-permute-start(bf16[2,3,384,128]{3,2,1,0:T(8,128)(2,1)S(1)} %collective-permute-done.10.rest_4_), channel_id=1, source_target_pairs={{0,8},{16,24},{32,40},{48,56},{64,72},{80,88},{96,104},{112,120},{... | collective-permute-start | bytes 1769480 | tf_op jit(solution)/shard_map/ppermute | solution.py:127
  61.1 11.2 %collective-permute-done.9.rest_3_ = bf16[2,3,384,128]{3,2,1,0:T(8,128)(2,1)S(1)} collective-permute-done((bf16[2,3,384,128]{3,2,1,0:T(8,128)(2,1)S(1)}, bf16[2,3,384,128]{3,2,1,0:T(8,128)(2,1)S(1)}, u32[]{:S(2)}, u32[]{:S(2)}) %collective-permute-start.9) | collective-permute-done | bytes 589856 | tf_op jit(solution)/shard_map/ppermute | solution.py:17
  72.2 2.2 %collective-permute-done.8.rest_2_ = bf16[2,3,384,128]{3,2,1,0:T(8,128)(2,1)S(1)} collective-permute-done((bf16[2,3,384,128]{3,2,1,0:T(8,128)(2,1)S(1)}, bf16[2,3,384,128]{3,2,1,0:T(8,128)(2,1)S(1)}, u32[]{:S(2)}, u32[]{:S(2)}) %collective-permute-start.8) | collective-permute-done | bytes 589856 | tf_op jit(solution)/shard_map/ppermute | solution.py:17
  74.4 2.2 %collective-permute-done.7.rest_1_ = bf16[2,3,384,128]{3,2,1,0:T(8,128)(2,1)S(1)} collective-permute-done((bf16[2,3,384,128]{3,2,1,0:T(8,128)(2,1)S(1)}, bf16[2,3,384,128]{3,2,1,0:T(8,128)(2,1)S(1)}, u32[]{:S(2)}, u32[]{:S(2)}) %collective-permute-start.7) | collective-permute-done | bytes 589856 | tf_op jit(solution)/shard_map/ppermute | solution.py:17
  76.7 1.3 collective-permute-start.14
  83.5 10.7 %shard_map.73 = bf16[384,384]{1,0:T(8,128)(2,1)} custom-call(s32[10]{0:T(128)} %convert_element_type.19.mask_ref, f32[384,384]{1,0:T(8,128)} %get-tuple-element.30.q_ref, f32[1,128]{1,0:T(1,128)} %bitcast.61, bf16[2,3,384,128]{3,2,1,0:T(8,128)(2,1)} %copy-done.2, bf16[2,3,384,128]{3,2,1,0:T(8,128)(2,1)} %copy-done.6, bf16[2,3,384,128]{3,2,1,0:T(8,128)(2,1)} %copy-done.5, ...), custom_call_target="tpu_custom_call" | custom-call | tf_op jit(solution)/shard_map/pallas_call | solution.py:67
  94.2 3.2 %convert_bitcast_fusion = bf16[8,384,384]{2,1,0:T(8,128)(2,1)S(1)} fusion(bf16[48,8,8,384]{3,2,1,0:T(8,128)(2,1)} %bitcast.62, bf16[384,384]{1,0:T(8,128)(2,1)} %shard_map.73), kind=kOutput, calls=%fused_computation.3 | convolution fusion | flops 907149312 | bytes 5013504 | tf_op jit(solution)/shard_map/tk,kjc->jtc/dot_general | solution.py:155
  97.4 36.8 %all_to_all.5 = bf16[8,384,384]{2,1,0:T(8,128)(2,1)S(1)} all-to-all(bf16[8,384,384]{2,1,0:T(8,128)(2,1)S(1)} %convert_bitcast_fusion), channel_id=1, replica_groups=mesh['seq'=32,'mp'=8] {'mp'}, dimensions={0} | all-to-all | bytes 4718592 | tf_op jit(solution)/shard_map/all_to_all | solution.py:161
  134.2 1.1 reduce_sum.22
  (63 shorter events, 10.3 us)
Async XLA Ops:
  0.0 81.2 %copy-start = (s32[32,6]{0,1:T(8,128)S(1)}, s32[32,6]{0,1:T(8,128)}, u32[]{:S(2)}) copy-start(s32[32,6]{0,1:T(8,128)} %param.16) | copy-start | bytes 2308
  0.0 13.1 %copy-start.8 = (bf16[384,384]{1,0:T(8,128)(2,1)S(1)}, bf16[384,384]{1,0:T(8,128)(2,1)}, u32[]{:S(2)}) copy-start(bf16[384,384]{1,0:T(8,128)(2,1)} %param.11) | copy-start | bytes 884740
  0.0 13.1 %collective-permute-start.5 = (bf16[384,384]{1,0:T(8,128)(2,1)}, bf16[384,384]{1,0:T(8,128)(2,1)S(1)}, u32[]{:S(2)}, u32[]{:S(2)}) collective-permute-start(bf16[384,384]{1,0:T(8,128)(2,1)} %param.11), channel_id=1, source_target_pairs={{0,6},{1,7},{2,0},{3,1},{4,2},{5,3},{6,4},{7,5},{8,14},{9,15},{10,... | collective-permute-start | bytes 884744 | tf_op jit(solution)/shard_map/ppermute | solution.py:17
  4.8 32.7 %collective-permute-start.4 = (bf16[384,384]{1,0:T(8,128)(2,1)}, bf16[384,384]{1,0:T(8,128)(2,1)S(1)}, u32[]{:S(2)}, u32[]{:S(2)}) collective-permute-start(bf16[384,384]{1,0:T(8,128)(2,1)} %param.11), channel_id=1, source_target_pairs={{0,5},{1,6},{2,7},{3,0},{4,1},{5,2},{6,3},{7,4},{8,13},{9,14},{10,... | collective-permute-start | bytes 884744 | tf_op jit(solution)/shard_map/ppermute | solution.py:17
  6.0 30.8 %collective-permute-start.3 = (bf16[384,384]{1,0:T(8,128)(2,1)}, bf16[384,384]{1,0:T(8,128)(2,1)S(1)}, u32[]{:S(2)}, u32[]{:S(2)}) collective-permute-start(bf16[384,384]{1,0:T(8,128)(2,1)} %param.11), channel_id=1, source_target_pairs={{0,4},{1,5},{2,6},{3,7},{4,0},{5,1},{6,2},{7,3},{8,12},{9,13},{10,... | collective-permute-start | bytes 884744 | tf_op jit(solution)/shard_map/ppermute | solution.py:17
  8.3 27.8 %collective-permute-start.2 = (bf16[384,384]{1,0:T(8,128)(2,1)}, bf16[384,384]{1,0:T(8,128)(2,1)S(1)}, u32[]{:S(2)}, u32[]{:S(2)}) collective-permute-start(bf16[384,384]{1,0:T(8,128)(2,1)} %param.11), channel_id=1, source_target_pairs={{0,3},{1,4},{2,5},{3,6},{4,7},{5,0},{6,1},{7,2},{8,11},{9,12},{10,... | collective-permute-start | bytes 884744 | tf_op jit(solution)/shard_map/ppermute | solution.py:17
  9.2 20.0 %collective-permute-start = (bf16[384,384]{1,0:T(8,128)(2,1)}, bf16[384,384]{1,0:T(8,128)(2,1)S(1)}, u32[]{:S(2)}, u32[]{:S(2)}) collective-permute-start(bf16[384,384]{1,0:T(8,128)(2,1)} %param.11), channel_id=1, source_target_pairs={{0,1},{1,2},{2,3},{3,4},{4,5},{5,6},{6,7},{7,0},{8,9},{9,10},{10,1... | collective-permute-start | bytes 884744 | tf_op jit(solution)/shard_map/ppermute | solution.py:17
  13.1 21.2 %collective-permute-start.1 = (bf16[384,384]{1,0:T(8,128)(2,1)S(1)}, bf16[384,384]{1,0:T(8,128)(2,1)S(1)}, u32[]{:S(2)}, u32[]{:S(2)}) collective-permute-start(bf16[384,384]{1,0:T(8,128)(2,1)S(1)} %copy-done.8), channel_id=1, source_target_pairs={{0,2},{1,3},{2,4},{3,5},{4,6},{5,7},{6,0},{7,1},{8,10},{9,11},{10,... | collective-permute-start | bytes 884744 | tf_op jit(solution)/shard_map/ppermute | solution.py:17
  19.5 16.6 %copy-start.1 = (bf16[3072,3,384]{2,0,1:T(8,128)(2,1)S(1)}, bf16[3072,3,384]{2,0,1:T(8,128)(2,1)}, u32[]{:S(2)}) copy-start(bf16[3072,3,384]{2,0,1:T(8,128)(2,1)} %param.12) | copy-start | bytes 21233668
  29.2 8.9 %collective-permute-start.6 = (bf16[384,384]{1,0:T(8,128)(2,1)S(1)}, bf16[384,384]{1,0:T(8,128)(2,1)S(1)}, u32[]{:S(2)}, u32[]{:S(2)}) collective-permute-start(bf16[384,384]{1,0:T(8,128)(2,1)S(1)} %copy-done.8), channel_id=1, source_target_pairs={{0,7},{1,0},{2,1},{3,2},{4,3},{5,4},{6,5},{7,6},{8,15},{9,8},{10,9... | collective-permute-start | bytes 884744 | tf_op jit(solution)/shard_map/ppermute | solution.py:17
  40.5 40.1 %copy-start.10 = (s32[32]{0:T(128)S(1)}, s32[32]{0:T(128)}, u32[]{:S(2)}) copy-start(s32[32]{0:T(128)} %param.17) | copy-start | bytes 388
  41.2 41.5 %copy-start.2 = (bf16[2,3,384,128]{3,2,1,0:T(8,128)(2,1)}, bf16[2,3,384,128]{3,2,1,0:T(8,128)(2,1)S(1)}, u32[]{:S(2)}) copy-start(bf16[2,3,384,128]{3,2,1,0:T(8,128)(2,1)S(1)} %pad_maximum_fusion.rest_0_) | copy-start | bytes 1769476
  41.2 17.7 %collective-permute-start.10 = (bf16[2,3,384,128]{3,2,1,0:T(8,128)(2,1)S(1)}, bf16[2,3,384,128]{3,2,1,0:T(8,128)(2,1)S(1)}, u32[]{:S(2)}, u32[]{:S(2)}) collective-permute-start(bf16[2,3,384,128]{3,2,1,0:T(8,128)(2,1)S(1)} %pad_maximum_fusion.rest_0_), channel_id=1, source_target_pairs={{0,224},{8,232},{16,240},{24,248},{32,0},{40,8},{48,16},{56,24},{6... | collective-permute-start | bytes 1769480 | tf_op jit(solution)/shard_map/ppermute | solution.py:17
  47.2 25.1 %collective-permute-start.9 = (bf16[2,3,384,128]{3,2,1,0:T(8,128)(2,1)S(1)}, bf16[2,3,384,128]{3,2,1,0:T(8,128)(2,1)S(1)}, u32[]{:S(2)}, u32[]{:S(2)}) collective-permute-start(bf16[2,3,384,128]{3,2,1,0:T(8,128)(2,1)S(1)} %pad_maximum_fusion.rest_0_), channel_id=1, source_target_pairs={{0,240},{8,248},{16,0},{24,8},{32,16},{40,24},{48,32},{56,40},{64,... | collective-permute-start | bytes 1769480 | tf_op jit(solution)/shard_map/ppermute | solution.py:17
  48.1 26.3 %collective-permute-start.8 = (bf16[2,3,384,128]{3,2,1,0:T(8,128)(2,1)S(1)}, bf16[2,3,384,128]{3,2,1,0:T(8,128)(2,1)S(1)}, u32[]{:S(2)}, u32[]{:S(2)}) collective-permute-start(bf16[2,3,384,128]{3,2,1,0:T(8,128)(2,1)S(1)} %pad_maximum_fusion.rest_0_), channel_id=1, source_target_pairs={{0,16},{8,24},{16,32},{24,40},{32,48},{40,56},{48,64},{56,72},{64,... | collective-permute-start | bytes 1769480 | tf_op jit(solution)/shard_map/ppermute | solution.py:17
  50.1 26.6 %collective-permute-start.7 = (bf16[2,3,384,128]{3,2,1,0:T(8,128)(2,1)S(1)}, bf16[2,3,384,128]{3,2,1,0:T(8,128)(2,1)S(1)}, u32[]{:S(2)}, u32[]{:S(2)}) collective-permute-start(bf16[2,3,384,128]{3,2,1,0:T(8,128)(2,1)S(1)} %pad_maximum_fusion.rest_0_), channel_id=1, source_target_pairs={{0,32},{8,40},{16,48},{24,56},{32,64},{40,72},{48,80},{56,88},{64,... | collective-permute-start | bytes 1769480 | tf_op jit(solution)/shard_map/ppermute | solution.py:17
  50.1 32.6 %collective-permute-start.11 = (bf16[2,3,384,128]{3,2,1,0:T(8,128)(2,1)S(1)}, bf16[2,3,384,128]{3,2,1,0:T(8,128)(2,1)S(1)}, u32[]{:S(2)}, u32[]{:S(2)}) collective-permute-start(bf16[2,3,384,128]{3,2,1,0:T(8,128)(2,1)S(1)} %pad_maximum_fusion.rest_0_), channel_id=1, source_target_pairs={{0,8},{8,0},{16,24},{24,16},{32,40},{40,32},{48,56},{56,48},{64,72... | collective-permute-start | bytes 1769480 | tf_op jit(solution)/shard_map/ppermute | solution.py:123
  58.9 23.8 %copy-start.3 = (bf16[2,3,384,128]{3,2,1,0:T(8,128)(2,1)}, bf16[2,3,384,128]{3,2,1,0:T(8,128)(2,1)S(1)}, u32[]{:S(2)}) copy-start(bf16[2,3,384,128]{3,2,1,0:T(8,128)(2,1)S(1)} %collective-permute-done.10.rest_4_) | copy-start | bytes 1769476
  58.9 23.8 %collective-permute-start.15 = (bf16[2,3,384,128]{3,2,1,0:T(8,128)(2,1)S(1)}, bf16[2,3,384,128]{3,2,1,0:T(8,128)(2,1)}, u32[]{:S(2)}, u32[]{:S(2)}) collective-permute-start(bf16[2,3,384,128]{3,2,1,0:T(8,128)(2,1)S(1)} %collective-permute-done.10.rest_4_), channel_id=1, source_target_pairs={{0,8},{16,24},{32,40},{48,56},{64,72},{80,88},{96,104},{112,120},{... | collective-permute-start | bytes 1769480 | tf_op jit(solution)/shard_map/ppermute | solution.py:127
  72.2 10.5 %copy-start.4 = (bf16[2,3,384,128]{3,2,1,0:T(8,128)(2,1)}, bf16[2,3,384,128]{3,2,1,0:T(8,128)(2,1)S(1)}, u32[]{:S(2)}) copy-start(bf16[2,3,384,128]{3,2,1,0:T(8,128)(2,1)S(1)} %collective-permute-done.9.rest_3_) | copy-start | bytes 1769476
  72.2 10.5 %collective-permute-start.13 = (bf16[2,3,384,128]{3,2,1,0:T(8,128)(2,1)S(1)}, bf16[2,3,384,128]{3,2,1,0:T(8,128)(2,1)}, u32[]{:S(2)}, u32[]{:S(2)}) collective-permute-start(bf16[2,3,384,128]{3,2,1,0:T(8,128)(2,1)S(1)} %collective-permute-done.9.rest_3_), channel_id=1, source_target_pairs={{0,8},{8,0},{16,24},{24,16},{32,40},{40,32},{48,56},{56,48},{64,72... | collective-permute-start | bytes 1769480 | tf_op jit(solution)/shard_map/ppermute | solution.py:125
  74.4 8.3 %copy-start.5 = (bf16[2,3,384,128]{3,2,1,0:T(8,128)(2,1)}, bf16[2,3,384,128]{3,2,1,0:T(8,128)(2,1)S(1)}, u32[]{:S(2)}) copy-start(bf16[2,3,384,128]{3,2,1,0:T(8,128)(2,1)S(1)} %collective-permute-done.8.rest_2_) | copy-start | bytes 1769476
  74.4 8.3 %collective-permute-start.12 = (bf16[2,3,384,128]{3,2,1,0:T(8,128)(2,1)S(1)}, bf16[2,3,384,128]{3,2,1,0:T(8,128)(2,1)}, u32[]{:S(2)}, u32[]{:S(2)}) collective-permute-start(bf16[2,3,384,128]{3,2,1,0:T(8,128)(2,1)S(1)} %collective-permute-done.8.rest_2_), channel_id=1, source_target_pairs={{0,8},{8,0},{16,24},{24,16},{32,40},{40,32},{48,56},{56,48},{64,72... | collective-permute-start | bytes 1769480 | tf_op jit(solution)/shard_map/ppermute | solution.py:124
  76.7 6.1 %collective-permute-start.14 = (bf16[2,3,384,128]{3,2,1,0:T(8,128)(2,1)S(1)}, bf16[2,3,384,128]{3,2,1,0:T(8,128)(2,1)}, u32[]{:S(2)}, u32[]{:S(2)}) collective-permute-start(bf16[2,3,384,128]{3,2,1,0:T(8,128)(2,1)S(1)} %collective-permute-done.7.rest_1_), channel_id=1, source_target_pairs={{8,0},{24,16},{40,32},{56,48},{72,64},{88,80},{104,96},{120,112},{... | collective-permute-start | bytes 1769480 | tf_op jit(solution)/shard_map/ppermute | solution.py:126
  (3 other events, 7.7 us)
